TPU v7x, 512 devices: a whole 4x8x8 slice. The times are simulated.
512 devices in a mesh: page: 32 (over y_lo, z), req: 16 (over y_hi, x, core).
Axes of the slice: x: 4, y: 8 (y_hi: 2, y_lo: 4; y = y_hi * 4 + y_lo), z: 8, core: 2. Of those that a mesh axis runs over, the one named last changes fastest.
Arguments:
- queries: bfloat16 [256, 8192], P('req'), may hold values from -250 to 250
- key_pool: bfloat16 [512, 128, 1024], P(('page', 'req')), may hold values from -6 to 6
- value_pool: bfloat16 [512, 128, 1024], P(('page', 'req')), may hold values from -6 to 6
- page_table: int32 [256, 32], P('req'), may hold values from 0 to 511, as said below
- page_count: int32 [256], P('req'), may hold values from 1 to 32, as said below
Outputs:
- attended: bfloat16 [256, 8192], P('req', 'page')
Inputs may be any that keep to these rules, and one draw needn't show every extreme that they name: `page_table`: rows of a request's table up to page_count are distinct pages; slots beyond it hold 0 and are not part of the context. `page_count`: some request has 32 live slots and some has one.
All inputs are finite; a program needn't handle non-finite values.
Results may differ from a plain program's by a relative error of at most 0.013.
Values may be sent and summed in bfloat16 or wider, within the bound.
No kernel may reach another device: no remote copies, remote signals or barrier semaphores. Data moves between devices by JAX's collectives and lax.ppermute only.
A program may use at most 64 MiB of HBM per device.

v0:
```python
import math

import jax
import jax.numpy as jnp
from jax import lax
from jax.sharding import PartitionSpec as P

H = 64
KVH = 8
HD = 128


def from_behind(value, axis, steps):
    count = lax.axis_size(axis)
    pairs = [(source, (source + steps) % count) for source in range(count)]
    return lax.ppermute(value, axis, pairs)


def joined(part, axis, combine):
    gathered = jax.tree.map(lambda a: lax.all_gather(a, axis), part)

    def take(source):
        return jax.tree.map(lambda a: lax.dynamic_index_in_dim(a, source, 0, False), gathered)

    return lax.fori_loop(
        1, lax.axis_size(axis), lambda source, state: combine(state, take(source)), take(0)
    )


def body(queries, key_pool, value_pool, page_table, page_count):
    req_rows = queries.shape[0]
    pages_held = key_pool.shape[0]
    page_len = key_pool.shape[1]
    per_kv = H // KVH
    req_size = lax.axis_size("req")
    page_size = lax.axis_size("page")
    req_index = lax.axis_index("req")
    page_index = lax.axis_index("page")
    grouped = queries.reshape(req_rows, KVH, per_kv, HD)
    slot_live = jnp.arange(page_table.shape[1], dtype=jnp.int32)[None, :] < page_count[:, None]
    score_scale = 1.0 / math.sqrt(HD)

    def absorb(partial_value, resident, source):
        key_rows, value_rows = resident
        first_page = (page_index * req_size + source) * pages_held
        held_ids = first_page + jnp.arange(pages_held, dtype=jnp.int32)
        page_hit = jnp.any(
            (page_table[:, :, None] == held_ids[None, None, :]) & slot_live[:, :, None], axis=1
        )
        run_max, run_sum, run_out = partial_value
        token_keys = key_rows.reshape(pages_held * page_len, KVH, HD)
        token_values = value_rows.reshape(pages_held * page_len, KVH, HD)
        scores = (
            jnp.einsum("rkgd,tkd->rkgt", grouped, token_keys, preferred_element_type=jnp.float32)
            * score_scale
        )
        token_hit = jnp.repeat(page_hit, page_len, axis=1)[:, None, None, :]
        scores = jnp.where(token_hit, scores, jnp.float32(-1e30))
        new_max = jnp.maximum(run_max, jnp.max(scores, axis=3))
        exp_terms = jnp.where(token_hit, jnp.exp(scores - new_max[..., None]), jnp.float32(0.0))
        factor = jnp.exp(run_max - new_max)
        new_sum = run_sum * factor + jnp.sum(exp_terms, axis=3)
        weights = exp_terms.astype(jnp.bfloat16)
        new_out = run_out * factor[..., None] + jnp.einsum(
            "rkgt,tkd->rkgd", weights, token_values, preferred_element_type=jnp.float32
        )
        return (new_max, new_sum, new_out)

    start_state = (
        jnp.full((req_rows, KVH, per_kv), -1e30, jnp.float32),
        jnp.zeros((req_rows, KVH, per_kv), jnp.float32),
        jnp.zeros((req_rows, KVH, per_kv, HD), jnp.float32),
    )
    own_block = (key_pool, value_pool)

    def rotate_once(offset, carry):
        resident, partial_in = carry
        arrived = from_behind((resident[0], resident[1]), "req", 1)
        partial_out = absorb(partial_in, resident, (req_index - offset) % req_size)
        return (arrived, partial_out)

    last_block, partial_value = lax.fori_loop(
        0, req_size - 1, rotate_once, (own_block, start_state)
    )
    partial_value = absorb(partial_value, last_block, (req_index - (req_size - 1)) % req_size)
    run_max, run_sum, run_out = partial_value
    own_heads = H // page_size

    def combine(first_part, second_part):
        first_max, first_sum, first_out = first_part
        second_max, second_sum, second_out = second_part
        joint_max = jnp.maximum(first_max, second_max)
        first_factor = jnp.exp(first_max - joint_max)
        second_factor = jnp.exp(second_max - joint_max)
        joint_sum = first_sum * first_factor + second_sum * second_factor
        joint_out = first_out * first_factor[..., None] + second_out * second_factor[..., None]
        return (joint_max, joint_sum, joint_out)

    merged_max, merged_sum, merged_out = joined((run_max, run_sum, run_out), "page", combine)
    flat_out = merged_out.reshape(req_rows, H, HD)
    flat_sum = merged_sum.reshape(req_rows, H)
    head_out = lax.dynamic_slice_in_dim(flat_out, page_index * own_heads, own_heads, 1)
    head_sum = lax.dynamic_slice_in_dim(flat_sum, page_index * own_heads, own_heads, 1)
    result = head_out / head_sum[..., None]
    return result.reshape(req_rows, own_heads * HD).astype(jnp.bfloat16)


def solution(mesh):
    return jax.shard_map(
        body,
        mesh=mesh,
        in_specs=(
            P("req", None),
            P(("page", "req"), None, None),
            P(("page", "req"), None, None),
            P("req", None),
            P("req"),
        ),
        out_specs=P("req", "page"),
        check_vma=False,
    )
```

profile of v0, /device:TPU:6, one launch (start us, length us, event | category | flops | bytes accessed | tf_op | source)
XLA Modules:
  0.0 610.9 jit_solution(12180921930636312561)
XLA Ops:
  10.5 249.1 %while.44 = (s32[]{:T(128)}, bf16[1,128,1024]{2,1,0:T(8,128)(2,1)S(1)}, bf16[1,128,1024]{2,1,0:T(8,128)(2,1)S(1)}, f32[16,8,8]{0,2,1:T(8,128)S(1)}, f32[16,8,8]{...) while((s32[]{:T(128)}, ...), condition=%wide.region_4.5_spmd.clone, body=%wide.region_0.4_spmd.clone.sunk | while | flops 68426752 | bytes 7674338 | solution.py:82
  12.5 7.8 %collective-permute-start.1 = (bf16[1,128,1024]{2,1,0:T(8,128)(2,1)S(1)}, bf16[1,128,1024]{2,1,0:T(8,128)(2,1)S(1)}, u32[]{:S(2)}, u32[]{:S(2)}) collective-permute-start(bf16[1,128,1024]{2,1,0:T(8,128)(2,1)S(1)} %copy.160), channel_id=1, source_target_pairs={{0,1},{1,2},{2,3},{3,4},{4,5},{5,6},{6,7},{7,8},{8,9},{9,10},{10,1... | collective-permute-start | bytes 786440 | tf_op jit(solution)/shard_map/while/body/eval_jaxpr/ppermute | solution.py:16
  22.7 9.1 %collective-permute-start = (bf16[1,128,1024]{2,1,0:T(8,128)(2,1)S(1)}, bf16[1,128,1024]{2,1,0:T(8,128)(2,1)S(1)}, u32[]{:S(2)}, u32[]{:S(2)}) collective-permute-start(bf16[1,128,1024]{2,1,0:T(8,128)(2,1)S(1)} %copy.159), channel_id=1, source_target_pairs={{0,1},{1,2},{2,3},{3,4},{4,5},{5,6},{6,7},{7,8},{8,9},{9,10},{10,1... | collective-permute-start | bytes 786440 | tf_op jit(solution)/shard_map/while/body/eval_jaxpr/ppermute | solution.py:16
  31.8 10.4 %collective-permute-start.1 = (bf16[1,128,1024]{2,1,0:T(8,128)(2,1)S(1)}, bf16[1,128,1024]{2,1,0:T(8,128)(2,1)S(1)}, u32[]{:S(2)}, u32[]{:S(2)}) collective-permute-start(bf16[1,128,1024]{2,1,0:T(8,128)(2,1)S(1)} %copy.160), channel_id=1, source_target_pairs={{0,1},{1,2},{2,3},{3,4},{4,5},{5,6},{6,7},{7,8},{8,9},{9,10},{10,1... | collective-permute-start | bytes 786440 | tf_op jit(solution)/shard_map/while/body/eval_jaxpr/ppermute | solution.py:16
  44.6 3.8 collective-permute-start
  48.4 10.4 %collective-permute-start.1 = (bf16[1,128,1024]{2,1,0:T(8,128)(2,1)S(1)}, bf16[1,128,1024]{2,1,0:T(8,128)(2,1)S(1)}, u32[]{:S(2)}, u32[]{:S(2)}) collective-permute-start(bf16[1,128,1024]{2,1,0:T(8,128)(2,1)S(1)} %copy.160), channel_id=1, source_target_pairs={{0,1},{1,2},{2,3},{3,4},{4,5},{5,6},{6,7},{7,8},{8,9},{9,10},{10,1... | collective-permute-start | bytes 786440 | tf_op jit(solution)/shard_map/while/body/eval_jaxpr/ppermute | solution.py:16
  61.2 3.7 collective-permute-start
  65.0 10.4 %collective-permute-start.1 = (bf16[1,128,1024]{2,1,0:T(8,128)(2,1)S(1)}, bf16[1,128,1024]{2,1,0:T(8,128)(2,1)S(1)}, u32[]{:S(2)}, u32[]{:S(2)}) collective-permute-start(bf16[1,128,1024]{2,1,0:T(8,128)(2,1)S(1)} %copy.160), channel_id=1, source_target_pairs={{0,1},{1,2},{2,3},{3,4},{4,5},{5,6},{6,7},{7,8},{8,9},{9,10},{10,1... | collective-permute-start | bytes 786440 | tf_op jit(solution)/shard_map/while/body/eval_jaxpr/ppermute | solution.py:16
  77.8 3.7 collective-permute-start
  81.5 10.4 %collective-permute-start.1 = (bf16[1,128,1024]{2,1,0:T(8,128)(2,1)S(1)}, bf16[1,128,1024]{2,1,0:T(8,128)(2,1)S(1)}, u32[]{:S(2)}, u32[]{:S(2)}) collective-permute-start(bf16[1,128,1024]{2,1,0:T(8,128)(2,1)S(1)} %copy.160), channel_id=1, source_target_pairs={{0,1},{1,2},{2,3},{3,4},{4,5},{5,6},{6,7},{7,8},{8,9},{9,10},{10,1... | collective-permute-start | bytes 786440 | tf_op jit(solution)/shard_map/while/body/eval_jaxpr/ppermute | solution.py:16
  94.3 3.7 collective-permute-start
  98.0 10.4 %collective-permute-start.1 = (bf16[1,128,1024]{2,1,0:T(8,128)(2,1)S(1)}, bf16[1,128,1024]{2,1,0:T(8,128)(2,1)S(1)}, u32[]{:S(2)}, u32[]{:S(2)}) collective-permute-start(bf16[1,128,1024]{2,1,0:T(8,128)(2,1)S(1)} %copy.160), channel_id=1, source_target_pairs={{0,1},{1,2},{2,3},{3,4},{4,5},{5,6},{6,7},{7,8},{8,9},{9,10},{10,1... | collective-permute-start | bytes 786440 | tf_op jit(solution)/shard_map/while/body/eval_jaxpr/ppermute | solution.py:16
  110.9 3.7 collective-permute-start
  114.6 10.4 %collective-permute-start.1 = (bf16[1,128,1024]{2,1,0:T(8,128)(2,1)S(1)}, bf16[1,128,1024]{2,1,0:T(8,128)(2,1)S(1)}, u32[]{:S(2)}, u32[]{:S(2)}) collective-permute-start(bf16[1,128,1024]{2,1,0:T(8,128)(2,1)S(1)} %copy.160), channel_id=1, source_target_pairs={{0,1},{1,2},{2,3},{3,4},{4,5},{5,6},{6,7},{7,8},{8,9},{9,10},{10,1... | collective-permute-start | bytes 786440 | tf_op jit(solution)/shard_map/while/body/eval_jaxpr/ppermute | solution.py:16
  127.4 3.7 collective-permute-start
  131.1 10.4 %collective-permute-start.1 = (bf16[1,128,1024]{2,1,0:T(8,128)(2,1)S(1)}, bf16[1,128,1024]{2,1,0:T(8,128)(2,1)S(1)}, u32[]{:S(2)}, u32[]{:S(2)}) collective-permute-start(bf16[1,128,1024]{2,1,0:T(8,128)(2,1)S(1)} %copy.160), channel_id=1, source_target_pairs={{0,1},{1,2},{2,3},{3,4},{4,5},{5,6},{6,7},{7,8},{8,9},{9,10},{10,1... | collective-permute-start | bytes 786440 | tf_op jit(solution)/shard_map/while/body/eval_jaxpr/ppermute | solution.py:16
  147.7 10.4 %collective-permute-start.1 = (bf16[1,128,1024]{2,1,0:T(8,128)(2,1)S(1)}, bf16[1,128,1024]{2,1,0:T(8,128)(2,1)S(1)}, u32[]{:S(2)}, u32[]{:S(2)}) collective-permute-start(bf16[1,128,1024]{2,1,0:T(8,128)(2,1)S(1)} %copy.160), channel_id=1, source_target_pairs={{0,1},{1,2},{2,3},{3,4},{4,5},{5,6},{6,7},{7,8},{8,9},{9,10},{10,1... | collective-permute-start | bytes 786440 | tf_op jit(solution)/shard_map/while/body/eval_jaxpr/ppermute | solution.py:16
  160.5 3.7 collective-permute-start
  164.2 10.4 %collective-permute-start.1 = (bf16[1,128,1024]{2,1,0:T(8,128)(2,1)S(1)}, bf16[1,128,1024]{2,1,0:T(8,128)(2,1)S(1)}, u32[]{:S(2)}, u32[]{:S(2)}) collective-permute-start(bf16[1,128,1024]{2,1,0:T(8,128)(2,1)S(1)} %copy.160), channel_id=1, source_target_pairs={{0,1},{1,2},{2,3},{3,4},{4,5},{5,6},{6,7},{7,8},{8,9},{9,10},{10,1... | collective-permute-start | bytes 786440 | tf_op jit(solution)/shard_map/while/body/eval_jaxpr/ppermute | solution.py:16
  177.0 3.7 collective-permute-start
  180.7 10.4 %collective-permute-start.1 = (bf16[1,128,1024]{2,1,0:T(8,128)(2,1)S(1)}, bf16[1,128,1024]{2,1,0:T(8,128)(2,1)S(1)}, u32[]{:S(2)}, u32[]{:S(2)}) collective-permute-start(bf16[1,128,1024]{2,1,0:T(8,128)(2,1)S(1)} %copy.160), channel_id=1, source_target_pairs={{0,1},{1,2},{2,3},{3,4},{4,5},{5,6},{6,7},{7,8},{8,9},{9,10},{10,1... | collective-permute-start | bytes 786440 | tf_op jit(solution)/shard_map/while/body/eval_jaxpr/ppermute | solution.py:16
  193.5 3.7 collective-permute-start
  197.3 10.4 %collective-permute-start.1 = (bf16[1,128,1024]{2,1,0:T(8,128)(2,1)S(1)}, bf16[1,128,1024]{2,1,0:T(8,128)(2,1)S(1)}, u32[]{:S(2)}, u32[]{:S(2)}) collective-permute-start(bf16[1,128,1024]{2,1,0:T(8,128)(2,1)S(1)} %copy.160), channel_id=1, source_target_pairs={{0,1},{1,2},{2,3},{3,4},{4,5},{5,6},{6,7},{7,8},{8,9},{9,10},{10,1... | collective-permute-start | bytes 786440 | tf_op jit(solution)/shard_map/while/body/eval_jaxpr/ppermute | solution.py:16
  210.1 3.7 collective-permute-start
  213.8 10.4 %collective-permute-start.1 = (bf16[1,128,1024]{2,1,0:T(8,128)(2,1)S(1)}, bf16[1,128,1024]{2,1,0:T(8,128)(2,1)S(1)}, u32[]{:S(2)}, u32[]{:S(2)}) collective-permute-start(bf16[1,128,1024]{2,1,0:T(8,128)(2,1)S(1)} %copy.160), channel_id=1, source_target_pairs={{0,1},{1,2},{2,3},{3,4},{4,5},{5,6},{6,7},{7,8},{8,9},{9,10},{10,1... | collective-permute-start | bytes 786440 | tf_op jit(solution)/shard_map/while/body/eval_jaxpr/ppermute | solution.py:16
  226.6 3.7 collective-permute-start
  230.4 10.4 %collective-permute-start.1 = (bf16[1,128,1024]{2,1,0:T(8,128)(2,1)S(1)}, bf16[1,128,1024]{2,1,0:T(8,128)(2,1)S(1)}, u32[]{:S(2)}, u32[]{:S(2)}) collective-permute-start(bf16[1,128,1024]{2,1,0:T(8,128)(2,1)S(1)} %copy.160), channel_id=1, source_target_pairs={{0,1},{1,2},{2,3},{3,4},{4,5},{5,6},{6,7},{7,8},{8,9},{9,10},{10,1... | collective-permute-start | bytes 786440 | tf_op jit(solution)/shard_map/while/body/eval_jaxpr/ppermute | solution.py:16
  246.9 10.4 %collective-permute-start.1 = (bf16[1,128,1024]{2,1,0:T(8,128)(2,1)S(1)}, bf16[1,128,1024]{2,1,0:T(8,128)(2,1)S(1)}, u32[]{:S(2)}, u32[]{:S(2)}) collective-permute-start(bf16[1,128,1024]{2,1,0:T(8,128)(2,1)S(1)} %copy.160), channel_id=1, source_target_pairs={{0,1},{1,2},{2,3},{3,4},{4,5},{5,6},{6,7},{7,8},{8,9},{9,10},{10,1... | collective-permute-start | bytes 786440 | tf_op jit(solution)/shard_map/while/body/eval_jaxpr/ppermute | solution.py:16
  262.0 129.4 %all-gather = f32[512,8,8]{2,1,0:T(8,128)S(1)} all-gather(f32[16,8,8]{2,1,0:T(8,128)S(1)} %copy.70), channel_id=2, replica_groups=mesh['page'=32,'req'=16] {'page'}, dimensions={0}, use_global_device_ids=true | all-gather | bytes 135168 | tf_op jit(solution)/shard_map/all_gather | solution.py:20
  392.1 109.5 %all-gather.1 = f32[512,8,8]{2,1,0:T(8,128)S(1)} all-gather(f32[16,8,8]{2,1,0:T(8,128)S(1)} %copy.71), channel_id=3, replica_groups=mesh['page'=32,'req'=16] {'page'}, dimensions={0}, use_global_device_ids=true | all-gather | bytes 135168 | tf_op jit(solution)/shard_map/all_gather | solution.py:20
  503.3 16.9 %all-gather.5.cloned.1.call-done = f32[512,8,8,128]{3,0,2,1:T(8,128)} async-done(((f32[16,8,8,128]{3,0,2,1:T(8,128)}), f32[512,8,8,128]{3,0,2,1:T(8,128)}) %all-gather.5.cloned.1.call-update) | async-done | bytes 16777232 | tf_op jit(solution)/shard_map/all_gather | solution.py:20
  521.5 81.7 %while.43 = (s32[]{:T(128)}, f32[16,8,8]{0,2,1:T(8,128)S(1)}, f32[16,8,8]{0,2,1:T(8,128)S(1)}, f32[16,8,8,128]{3,2,1,0:T(8,128)S(1)}, f32[32,16,8,8]{1,3,2,0:T(8...) while((s32[]{:T(128)}, f32[16,8,8]{0,2,1:T(8,128)S(1)}, ...), condition=%wide.region_9.10_spmd, body=%wide.region_8.9_spmd.sunk | while | flops 399365 | bytes 2678927 | solution.py:25
  (399 shorter events, 134.7 us)
Async XLA Ops:
  6.5 513.7 %all-gather.5.cloned.1.call-start = ((), (), s32[]{:S(2)}) async-start(), calls=%async_computation | async-start | bytes 17301504 | tf_op jit(solution)/shard_map/all_gather | solution.py:20
  10.6 12.1 %collective-permute-start = (bf16[1,128,1024]{2,1,0:T(8,128)(2,1)S(1)}, bf16[1,128,1024]{2,1,0:T(8,128)(2,1)S(1)}, u32[]{:S(2)}, u32[]{:S(2)}) collective-permute-start(bf16[1,128,1024]{2,1,0:T(8,128)(2,1)S(1)} %copy.159), channel_id=1, source_target_pairs={{0,1},{1,2},{2,3},{3,4},{4,5},{5,6},{6,7},{7,8},{8,9},{9,10},{10,1... | collective-permute-start | bytes 786440 | tf_op jit(solution)/shard_map/while/body/eval_jaxpr/ppermute | solution.py:16
  12.5 10.1 %collective-permute-start.1 = (bf16[1,128,1024]{2,1,0:T(8,128)(2,1)S(1)}, bf16[1,128,1024]{2,1,0:T(8,128)(2,1)S(1)}, u32[]{:S(2)}, u32[]{:S(2)}) collective-permute-start(bf16[1,128,1024]{2,1,0:T(8,128)(2,1)S(1)} %copy.160), channel_id=1, source_target_pairs={{0,1},{1,2},{2,3},{3,4},{4,5},{5,6},{6,7},{7,8},{8,9},{9,10},{10,1... | collective-permute-start | bytes 786440 | tf_op jit(solution)/shard_map/while/body/eval_jaxpr/ppermute | solution.py:16
  22.7 21.9 %collective-permute-start = (bf16[1,128,1024]{2,1,0:T(8,128)(2,1)S(1)}, bf16[1,128,1024]{2,1,0:T(8,128)(2,1)S(1)}, u32[]{:S(2)}, u32[]{:S(2)}) collective-permute-start(bf16[1,128,1024]{2,1,0:T(8,128)(2,1)S(1)} %copy.159), channel_id=1, source_target_pairs={{0,1},{1,2},{2,3},{3,4},{4,5},{5,6},{6,7},{7,8},{8,9},{9,10},{10,1... | collective-permute-start | bytes 786440 | tf_op jit(solution)/shard_map/while/body/eval_jaxpr/ppermute | solution.py:16
  31.8 12.8 %collective-permute-start.1 = (bf16[1,128,1024]{2,1,0:T(8,128)(2,1)S(1)}, bf16[1,128,1024]{2,1,0:T(8,128)(2,1)S(1)}, u32[]{:S(2)}, u32[]{:S(2)}) collective-permute-start(bf16[1,128,1024]{2,1,0:T(8,128)(2,1)S(1)} %copy.160), channel_id=1, source_target_pairs={{0,1},{1,2},{2,3},{3,4},{4,5},{5,6},{6,7},{7,8},{8,9},{9,10},{10,1... | collective-permute-start | bytes 786440 | tf_op jit(solution)/shard_map/while/body/eval_jaxpr/ppermute | solution.py:16
  44.6 16.6 %collective-permute-start = (bf16[1,128,1024]{2,1,0:T(8,128)(2,1)S(1)}, bf16[1,128,1024]{2,1,0:T(8,128)(2,1)S(1)}, u32[]{:S(2)}, u32[]{:S(2)}) collective-permute-start(bf16[1,128,1024]{2,1,0:T(8,128)(2,1)S(1)} %copy.159), channel_id=1, source_target_pairs={{0,1},{1,2},{2,3},{3,4},{4,5},{5,6},{6,7},{7,8},{8,9},{9,10},{10,1... | collective-permute-start | bytes 786440 | tf_op jit(solution)/shard_map/while/body/eval_jaxpr/ppermute | solution.py:16
  48.4 12.8 %collective-permute-start.1 = (bf16[1,128,1024]{2,1,0:T(8,128)(2,1)S(1)}, bf16[1,128,1024]{2,1,0:T(8,128)(2,1)S(1)}, u32[]{:S(2)}, u32[]{:S(2)}) collective-permute-start(bf16[1,128,1024]{2,1,0:T(8,128)(2,1)S(1)} %copy.160), channel_id=1, source_target_pairs={{0,1},{1,2},{2,3},{3,4},{4,5},{5,6},{6,7},{7,8},{8,9},{9,10},{10,1... | collective-permute-start | bytes 786440 | tf_op jit(solution)/shard_map/while/body/eval_jaxpr/ppermute | solution.py:16
  61.2 16.5 %collective-permute-start = (bf16[1,128,1024]{2,1,0:T(8,128)(2,1)S(1)}, bf16[1,128,1024]{2,1,0:T(8,128)(2,1)S(1)}, u32[]{:S(2)}, u32[]{:S(2)}) collective-permute-start(bf16[1,128,1024]{2,1,0:T(8,128)(2,1)S(1)} %copy.159), channel_id=1, source_target_pairs={{0,1},{1,2},{2,3},{3,4},{4,5},{5,6},{6,7},{7,8},{8,9},{9,10},{10,1... | collective-permute-start | bytes 786440 | tf_op jit(solution)/shard_map/while/body/eval_jaxpr/ppermute | solution.py:16
  65.0 12.8 %collective-permute-start.1 = (bf16[1,128,1024]{2,1,0:T(8,128)(2,1)S(1)}, bf16[1,128,1024]{2,1,0:T(8,128)(2,1)S(1)}, u32[]{:S(2)}, u32[]{:S(2)}) collective-permute-start(bf16[1,128,1024]{2,1,0:T(8,128)(2,1)S(1)} %copy.160), channel_id=1, source_target_pairs={{0,1},{1,2},{2,3},{3,4},{4,5},{5,6},{6,7},{7,8},{8,9},{9,10},{10,1... | collective-permute-start | bytes 786440 | tf_op jit(solution)/shard_map/while/body/eval_jaxpr/ppermute | solution.py:16
  77.8 16.5 %collective-permute-start = (bf16[1,128,1024]{2,1,0:T(8,128)(2,1)S(1)}, bf16[1,128,1024]{2,1,0:T(8,128)(2,1)S(1)}, u32[]{:S(2)}, u32[]{:S(2)}) collective-permute-start(bf16[1,128,1024]{2,1,0:T(8,128)(2,1)S(1)} %copy.159), channel_id=1, source_target_pairs={{0,1},{1,2},{2,3},{3,4},{4,5},{5,6},{6,7},{7,8},{8,9},{9,10},{10,1... | collective-permute-start | bytes 786440 | tf_op jit(solution)/shard_map/while/body/eval_jaxpr/ppermute | solution.py:16
  81.5 12.8 %collective-permute-start.1 = (bf16[1,128,1024]{2,1,0:T(8,128)(2,1)S(1)}, bf16[1,128,1024]{2,1,0:T(8,128)(2,1)S(1)}, u32[]{:S(2)}, u32[]{:S(2)}) collective-permute-start(bf16[1,128,1024]{2,1,0:T(8,128)(2,1)S(1)} %copy.160), channel_id=1, source_target_pairs={{0,1},{1,2},{2,3},{3,4},{4,5},{5,6},{6,7},{7,8},{8,9},{9,10},{10,1... | collective-permute-start | bytes 786440 | tf_op jit(solution)/shard_map/while/body/eval_jaxpr/ppermute | solution.py:16
  94.3 16.5 %collective-permute-start = (bf16[1,128,1024]{2,1,0:T(8,128)(2,1)S(1)}, bf16[1,128,1024]{2,1,0:T(8,128)(2,1)S(1)}, u32[]{:S(2)}, u32[]{:S(2)}) collective-permute-start(bf16[1,128,1024]{2,1,0:T(8,128)(2,1)S(1)} %copy.159), channel_id=1, source_target_pairs={{0,1},{1,2},{2,3},{3,4},{4,5},{5,6},{6,7},{7,8},{8,9},{9,10},{10,1... | collective-permute-start | bytes 786440 | tf_op jit(solution)/shard_map/while/body/eval_jaxpr/ppermute | solution.py:16
  98.0 12.8 %collective-permute-start.1 = (bf16[1,128,1024]{2,1,0:T(8,128)(2,1)S(1)}, bf16[1,128,1024]{2,1,0:T(8,128)(2,1)S(1)}, u32[]{:S(2)}, u32[]{:S(2)}) collective-permute-start(bf16[1,128,1024]{2,1,0:T(8,128)(2,1)S(1)} %copy.160), channel_id=1, source_target_pairs={{0,1},{1,2},{2,3},{3,4},{4,5},{5,6},{6,7},{7,8},{8,9},{9,10},{10,1... | collective-permute-start | bytes 786440 | tf_op jit(solution)/shard_map/while/body/eval_jaxpr/ppermute | solution.py:16
  110.9 16.5 %collective-permute-start = (bf16[1,128,1024]{2,1,0:T(8,128)(2,1)S(1)}, bf16[1,128,1024]{2,1,0:T(8,128)(2,1)S(1)}, u32[]{:S(2)}, u32[]{:S(2)}) collective-permute-start(bf16[1,128,1024]{2,1,0:T(8,128)(2,1)S(1)} %copy.159), channel_id=1, source_target_pairs={{0,1},{1,2},{2,3},{3,4},{4,5},{5,6},{6,7},{7,8},{8,9},{9,10},{10,1... | collective-permute-start | bytes 786440 | tf_op jit(solution)/shard_map/while/body/eval_jaxpr/ppermute | solution.py:16
  114.6 12.8 %collective-permute-start.1 = (bf16[1,128,1024]{2,1,0:T(8,128)(2,1)S(1)}, bf16[1,128,1024]{2,1,0:T(8,128)(2,1)S(1)}, u32[]{:S(2)}, u32[]{:S(2)}) collective-permute-start(bf16[1,128,1024]{2,1,0:T(8,128)(2,1)S(1)} %copy.160), channel_id=1, source_target_pairs={{0,1},{1,2},{2,3},{3,4},{4,5},{5,6},{6,7},{7,8},{8,9},{9,10},{10,1... | collective-permute-start | bytes 786440 | tf_op jit(solution)/shard_map/while/body/eval_jaxpr/ppermute | solution.py:16
  127.4 16.5 %collective-permute-start = (bf16[1,128,1024]{2,1,0:T(8,128)(2,1)S(1)}, bf16[1,128,1024]{2,1,0:T(8,128)(2,1)S(1)}, u32[]{:S(2)}, u32[]{:S(2)}) collective-permute-start(bf16[1,128,1024]{2,1,0:T(8,128)(2,1)S(1)} %copy.159), channel_id=1, source_target_pairs={{0,1},{1,2},{2,3},{3,4},{4,5},{5,6},{6,7},{7,8},{8,9},{9,10},{10,1... | collective-permute-start | bytes 786440 | tf_op jit(solution)/shard_map/while/body/eval_jaxpr/ppermute | solution.py:16
  131.1 12.8 %collective-permute-start.1 = (bf16[1,128,1024]{2,1,0:T(8,128)(2,1)S(1)}, bf16[1,128,1024]{2,1,0:T(8,128)(2,1)S(1)}, u32[]{:S(2)}, u32[]{:S(2)}) collective-permute-start(bf16[1,128,1024]{2,1,0:T(8,128)(2,1)S(1)} %copy.160), channel_id=1, source_target_pairs={{0,1},{1,2},{2,3},{3,4},{4,5},{5,6},{6,7},{7,8},{8,9},{9,10},{10,1... | collective-permute-start | bytes 786440 | tf_op jit(solution)/shard_map/while/body/eval_jaxpr/ppermute | solution.py:16
  143.9 16.5 %collective-permute-start = (bf16[1,128,1024]{2,1,0:T(8,128)(2,1)S(1)}, bf16[1,128,1024]{2,1,0:T(8,128)(2,1)S(1)}, u32[]{:S(2)}, u32[]{:S(2)}) collective-permute-start(bf16[1,128,1024]{2,1,0:T(8,128)(2,1)S(1)} %copy.159), channel_id=1, source_target_pairs={{0,1},{1,2},{2,3},{3,4},{4,5},{5,6},{6,7},{7,8},{8,9},{9,10},{10,1... | collective-permute-start | bytes 786440 | tf_op jit(solution)/shard_map/while/body/eval_jaxpr/ppermute | solution.py:16
  147.7 12.8 %collective-permute-start.1 = (bf16[1,128,1024]{2,1,0:T(8,128)(2,1)S(1)}, bf16[1,128,1024]{2,1,0:T(8,128)(2,1)S(1)}, u32[]{:S(2)}, u32[]{:S(2)}) collective-permute-start(bf16[1,128,1024]{2,1,0:T(8,128)(2,1)S(1)} %copy.160), channel_id=1, source_target_pairs={{0,1},{1,2},{2,3},{3,4},{4,5},{5,6},{6,7},{7,8},{8,9},{9,10},{10,1... | collective-permute-start | bytes 786440 | tf_op jit(solution)/shard_map/while/body/eval_jaxpr/ppermute | solution.py:16
  160.5 16.5 %collective-permute-start = (bf16[1,128,1024]{2,1,0:T(8,128)(2,1)S(1)}, bf16[1,128,1024]{2,1,0:T(8,128)(2,1)S(1)}, u32[]{:S(2)}, u32[]{:S(2)}) collective-permute-start(bf16[1,128,1024]{2,1,0:T(8,128)(2,1)S(1)} %copy.159), channel_id=1, source_target_pairs={{0,1},{1,2},{2,3},{3,4},{4,5},{5,6},{6,7},{7,8},{8,9},{9,10},{10,1... | collective-permute-start | bytes 786440 | tf_op jit(solution)/shard_map/while/body/eval_jaxpr/ppermute | solution.py:16
  164.2 12.8 %collective-permute-start.1 = (bf16[1,128,1024]{2,1,0:T(8,128)(2,1)S(1)}, bf16[1,128,1024]{2,1,0:T(8,128)(2,1)S(1)}, u32[]{:S(2)}, u32[]{:S(2)}) collective-permute-start(bf16[1,128,1024]{2,1,0:T(8,128)(2,1)S(1)} %copy.160), channel_id=1, source_target_pairs={{0,1},{1,2},{2,3},{3,4},{4,5},{5,6},{6,7},{7,8},{8,9},{9,10},{10,1... | collective-permute-start | bytes 786440 | tf_op jit(solution)/shard_map/while/body/eval_jaxpr/ppermute | solution.py:16
  177.0 16.5 %collective-permute-start = (bf16[1,128,1024]{2,1,0:T(8,128)(2,1)S(1)}, bf16[1,128,1024]{2,1,0:T(8,128)(2,1)S(1)}, u32[]{:S(2)}, u32[]{:S(2)}) collective-permute-start(bf16[1,128,1024]{2,1,0:T(8,128)(2,1)S(1)} %copy.159), channel_id=1, source_target_pairs={{0,1},{1,2},{2,3},{3,4},{4,5},{5,6},{6,7},{7,8},{8,9},{9,10},{10,1... | collective-permute-start | bytes 786440 | tf_op jit(solution)/shard_map/while/body/eval_jaxpr/ppermute | solution.py:16
  180.7 12.8 %collective-permute-start.1 = (bf16[1,128,1024]{2,1,0:T(8,128)(2,1)S(1)}, bf16[1,128,1024]{2,1,0:T(8,128)(2,1)S(1)}, u32[]{:S(2)}, u32[]{:S(2)}) collective-permute-start(bf16[1,128,1024]{2,1,0:T(8,128)(2,1)S(1)} %copy.160), channel_id=1, source_target_pairs={{0,1},{1,2},{2,3},{3,4},{4,5},{5,6},{6,7},{7,8},{8,9},{9,10},{10,1... | collective-permute-start | bytes 786440 | tf_op jit(solution)/shard_map/while/body/eval_jaxpr/ppermute | solution.py:16
  193.5 16.5 %collective-permute-start = (bf16[1,128,1024]{2,1,0:T(8,128)(2,1)S(1)}, bf16[1,128,1024]{2,1,0:T(8,128)(2,1)S(1)}, u32[]{:S(2)}, u32[]{:S(2)}) collective-permute-start(bf16[1,128,1024]{2,1,0:T(8,128)(2,1)S(1)} %copy.159), channel_id=1, source_target_pairs={{0,1},{1,2},{2,3},{3,4},{4,5},{5,6},{6,7},{7,8},{8,9},{9,10},{10,1... | collective-permute-start | bytes 786440 | tf_op jit(solution)/shard_map/while/body/eval_jaxpr/ppermute | solution.py:16
  197.3 12.8 %collective-permute-start.1 = (bf16[1,128,1024]{2,1,0:T(8,128)(2,1)S(1)}, bf16[1,128,1024]{2,1,0:T(8,128)(2,1)S(1)}, u32[]{:S(2)}, u32[]{:S(2)}) collective-permute-start(bf16[1,128,1024]{2,1,0:T(8,128)(2,1)S(1)} %copy.160), channel_id=1, source_target_pairs={{0,1},{1,2},{2,3},{3,4},{4,5},{5,6},{6,7},{7,8},{8,9},{9,10},{10,1... | collective-permute-start | bytes 786440 | tf_op jit(solution)/shard_map/while/body/eval_jaxpr/ppermute | solution.py:16
  210.1 16.5 %collective-permute-start = (bf16[1,128,1024]{2,1,0:T(8,128)(2,1)S(1)}, bf16[1,128,1024]{2,1,0:T(8,128)(2,1)S(1)}, u32[]{:S(2)}, u32[]{:S(2)}) collective-permute-start(bf16[1,128,1024]{2,1,0:T(8,128)(2,1)S(1)} %copy.159), channel_id=1, source_target_pairs={{0,1},{1,2},{2,3},{3,4},{4,5},{5,6},{6,7},{7,8},{8,9},{9,10},{10,1... | collective-permute-start | bytes 786440 | tf_op jit(solution)/shard_map/while/body/eval_jaxpr/ppermute | solution.py:16
  213.8 12.8 %collective-permute-start.1 = (bf16[1,128,1024]{2,1,0:T(8,128)(2,1)S(1)}, bf16[1,128,1024]{2,1,0:T(8,128)(2,1)S(1)}, u32[]{:S(2)}, u32[]{:S(2)}) collective-permute-start(bf16[1,128,1024]{2,1,0:T(8,128)(2,1)S(1)} %copy.160), channel_id=1, source_target_pairs={{0,1},{1,2},{2,3},{3,4},{4,5},{5,6},{6,7},{7,8},{8,9},{9,10},{10,1... | collective-permute-start | bytes 786440 | tf_op jit(solution)/shard_map/while/body/eval_jaxpr/ppermute | solution.py:16
  226.6 16.5 %collective-permute-start = (bf16[1,128,1024]{2,1,0:T(8,128)(2,1)S(1)}, bf16[1,128,1024]{2,1,0:T(8,128)(2,1)S(1)}, u32[]{:S(2)}, u32[]{:S(2)}) collective-permute-start(bf16[1,128,1024]{2,1,0:T(8,128)(2,1)S(1)} %copy.159), channel_id=1, source_target_pairs={{0,1},{1,2},{2,3},{3,4},{4,5},{5,6},{6,7},{7,8},{8,9},{9,10},{10,1... | collective-permute-start | bytes 786440 | tf_op jit(solution)/shard_map/while/body/eval_jaxpr/ppermute | solution.py:16
  230.4 12.8 %collective-permute-start.1 = (bf16[1,128,1024]{2,1,0:T(8,128)(2,1)S(1)}, bf16[1,128,1024]{2,1,0:T(8,128)(2,1)S(1)}, u32[]{:S(2)}, u32[]{:S(2)}) collective-permute-start(bf16[1,128,1024]{2,1,0:T(8,128)(2,1)S(1)} %copy.160), channel_id=1, source_target_pairs={{0,1},{1,2},{2,3},{3,4},{4,5},{5,6},{6,7},{7,8},{8,9},{9,10},{10,1... | collective-permute-start | bytes 786440 | tf_op jit(solution)/shard_map/while/body/eval_jaxpr/ppermute | solution.py:16
  243.2 16.5 %collective-permute-start = (bf16[1,128,1024]{2,1,0:T(8,128)(2,1)S(1)}, bf16[1,128,1024]{2,1,0:T(8,128)(2,1)S(1)}, u32[]{:S(2)}, u32[]{:S(2)}) collective-permute-start(bf16[1,128,1024]{2,1,0:T(8,128)(2,1)S(1)} %copy.159), channel_id=1, source_target_pairs={{0,1},{1,2},{2,3},{3,4},{4,5},{5,6},{6,7},{7,8},{8,9},{9,10},{10,1... | collective-permute-start | bytes 786440 | tf_op jit(solution)/shard_map/while/body/eval_jaxpr/ppermute | solution.py:16
  246.9 12.8 %collective-permute-start.1 = (bf16[1,128,1024]{2,1,0:T(8,128)(2,1)S(1)}, bf16[1,128,1024]{2,1,0:T(8,128)(2,1)S(1)}, u32[]{:S(2)}, u32[]{:S(2)}) collective-permute-start(bf16[1,128,1024]{2,1,0:T(8,128)(2,1)S(1)} %copy.160), channel_id=1, source_target_pairs={{0,1},{1,2},{2,3},{3,4},{4,5},{5,6},{6,7},{7,8},{8,9},{9,10},{10,1... | collective-permute-start | bytes 786440 | tf_op jit(solution)/shard_map/while/body/eval_jaxpr/ppermute | solution.py:16
Sparse Core Ops, SparseCore 0:
  262.0 258.2 all-gather.4
where the time goes:
time: 616 us; the launch traced here: 611 us
  blocking collectives  239 us (39%)
  starting transfers between devices  213 us (35%)
  other arithmetic  62.3 us (10%)
  local copies, waits for them, and re-layouts  50 us (8%)
  waiting for transfers between devices  17 us (3%)
  between operations  13.5 us (2%)
  matrix products  13 us (2%)
    all_gather x2, blocking collectives, joined(): gathered = jax.tree.map(lambda a: lax.all_gather(a, axis), part)  239 us
    ppermute x30, starting transfers between devices, from_behind(): return lax.ppermute(value, axis, pairs)  213 us
    dynamic_slice x34, local copies, waits for them, and re-layouts, take(): lax.dynamic_index_in_dim(a, source, 0, False)  35 us
    add x31, other arithmetic, combine(): joint_sum = first_sum * first_factor + second_sum * second_factor  24.9 us
    all_gather x1, waiting for transfers between devices, joined(): gathered = jax.tree.map(lambda a: lax.all_gather(a, axis), part)  16.9 us
    add x31, other arithmetic, combine(): first_out * first_factor[..., None] + second_out * second_factor[..., None]  16.3 us
    reduce_or x16, other arithmetic, absorb(): jnp.any((page_table[:, :, None] == held_ids[None, None, :]) & slot_live[:...  14.1 us
  transfers between devices with their start and end apart: 31, of which 1 were waited for; matrix products, arithmetic and copies ran while one was open for 6% of the time, Pallas kernels for 0%

commit v1 on v0

v1 whole, which is shorter than its diff:
```python
import math

import jax
import jax.numpy as jnp
from jax import lax
from jax.sharding import Mesh
from jax.sharding import PartitionSpec as P

H = 64
KVH = 8
HD = 128


def body(queries, key_pool, value_pool, page_table, page_count):
    n_page = lax.axis_size("page")
    n_yh = lax.axis_size("yh")
    n_xc = lax.axis_size("xc")
    page_index = lax.axis_index("page")
    yh_index = lax.axis_index("yh")
    pages_held = key_pool.shape[0]
    page_len = key_pool.shape[1]
    per_kv = H // KVH
    own_heads = H // n_page
    rows = queries.shape[0]
    score_scale = 1.0 / math.sqrt(HD)

    all_q = lax.all_gather(queries, "yh", tiled=True)
    all_table = lax.all_gather(page_table, "yh", tiled=True)
    all_count = lax.all_gather(page_count, "yh", tiled=True)
    keys = lax.all_gather(key_pool, "xc", tiled=True)
    values = lax.all_gather(value_pool, "xc", tiled=True)

    req_rows = all_q.shape[0]
    first_page = (page_index * n_yh + yh_index) * n_xc * pages_held
    held_ids = first_page + jnp.arange(n_xc * pages_held, dtype=jnp.int32)
    slot_live = jnp.arange(all_table.shape[1], dtype=jnp.int32)[None, :] < all_count[:, None]
    page_hit = jnp.any(
        (all_table[:, :, None] == held_ids[None, None, :]) & slot_live[:, :, None], axis=1
    )
    token_hit = jnp.repeat(page_hit, page_len, axis=1)[:, None, None, :]

    grouped = all_q.reshape(req_rows, KVH, per_kv, HD)
    token_keys = keys.reshape(-1, KVH, HD)
    token_values = values.reshape(-1, KVH, HD)
    scores = (
        jnp.einsum("rkgd,tkd->rkgt", grouped, token_keys, preferred_element_type=jnp.float32)
        * score_scale
    )
    scores = jnp.where(token_hit, scores, jnp.float32(-1e30))
    local_max = jnp.max(scores, axis=3)
    global_max = lax.pmax(local_max, ("page", "yh"))
    exp_terms = jnp.where(token_hit, jnp.exp(scores - local_max[..., None]), jnp.float32(0.0))
    local_sum = jnp.sum(exp_terms, axis=3)
    weights = exp_terms.astype(jnp.bfloat16)
    local_out = jnp.einsum(
        "rkgt,tkd->rkgd", weights, token_values, preferred_element_type=jnp.float32
    )
    factor = jnp.exp(local_max - global_max)
    local_out = local_out * factor[..., None]
    local_sum = local_sum * factor

    out_blocks = local_out.reshape(n_yh, rows, n_page, own_heads, HD).transpose(2, 0, 1, 3, 4)
    out_blocks = out_blocks.reshape(n_page * n_yh, rows, own_heads, HD)
    sum_blocks = local_sum.reshape(n_yh, rows, n_page, own_heads).transpose(2, 0, 1, 3)
    sum_blocks = sum_blocks.reshape(n_page * n_yh, rows, own_heads)
    out_red = lax.psum_scatter(out_blocks, ("page", "yh"), scatter_dimension=0, tiled=True)
    sum_red = lax.psum_scatter(sum_blocks, ("page", "yh"), scatter_dimension=0, tiled=True)
    result = out_red[0] / sum_red[0][..., None]
    return result.reshape(rows, own_heads * HD).astype(jnp.bfloat16)


def solution(mesh):
    n_page, n_req = mesh.devices.shape
    n_yh = 2 if n_req % 2 == 0 else 1
    split = Mesh(mesh.devices.reshape(n_page, n_yh, n_req // n_yh), ("page", "yh", "xc"))
    req = ("yh", "xc")
    return jax.shard_map(
        body,
        mesh=split,
        in_specs=(
            P(req, None),
            P(("page",) + req, None, None),
            P(("page",) + req, None, None),
            P(req, None),
            P(req),
        ),
        out_specs=P(req, "page"),
        check_vma=False,
    )
```

time: 616 us -> 818 us (1.33)
  blocking collectives: 239 us -> 761 us
  starting transfers between devices: 213 us -> 0.08 us
  other arithmetic: 62.3 us -> 6.08 us
  local copies, waits for them, and re-layouts: 50 us -> 10.9 us
    unnamed x0 -> x2, blocking collectives: none -> 371 us
    pmax x0 -> x1, blocking collectives: none -> 366 us  [body(): global_max = lax.pmax(local_max, ('page', 'yh'))]
    all_gather x2, blocking collectives: 239 us -> 24.3 us  [the longest x1 15.9 us: body(): all_q = lax.all_gather(queries, 'yh', tiled=True)]
    ppermute x30 -> x0, starting transfers between devices: 213 us -> none  [from_behind(): return lax.ppermute(value, axis, pairs)]
    add x78 -> x1, other arithmetic: 41.5 us -> 0.01 us  [body(): held_ids = first_page + jnp.arange(n_xc * pages_held, dtype=jnp.int32)]
    dynamic_slice x36 -> x0, local copies, waits for them, and re-layouts: 35.1 us -> none  [the longest x34 35 us: take(): lax.dynamic_index_in_dim(a, source, 0, False)]
    all_gather x1 -> x2, waiting for transfers between devices: 16.9 us -> 0.04 us  [the longest x1 0.02 us: body(): keys = lax.all_gather(key_pool, 'xc', tiled=True)]
    reduce_or x16 -> x1, other arithmetic: 14.1 us -> 0.7 us  [body(): jnp.any((all_table[:, :, None] == held_ids[None, None, :]) & slot_live[:,...]
  transfers between devices with their start and end apart: 31 -> 3, of which waited for: 1 -> 1; matrix products, arithmetic and copies ran while one was open for 6% -> 2% of each run, Pallas kernels for 0% -> 0%
where the time goes in v1:
time: 818 us; the launch traced here: 816 us
  blocking collectives  761 us (93%)
  waiting for transfers between devices  13.9 us (2%)
  between operations  13.9 us (2%)
  local copies, waits for them, and re-layouts  10.9 us (1%)
  matrix products  10.1 us (1%)
    unnamed x2, blocking collectives  371 us
    pmax x1, blocking collectives, body(): global_max = lax.pmax(local_max, ('page', 'yh'))  366 us
  transfers between devices with their start and end apart: 3, of which 1 were waited for; matrix products, arithmetic and copies ran while one was open for 2% of the time, Pallas kernels for 0%

profile of v1, /device:TPU:6, one launch (start us, length us, event | category | flops | bytes accessed | tf_op | source)
XLA Modules:
  0.0 816.3 jit_solution(12329927334446514234)
XLA Ops:
  6.5 0.7 all-gather.3.cloned.1.call-update
  7.3 0.0 all-gather.5.cloned.1.call-start
  7.3 0.7 all-gather.5.cloned.1.call-update
  8.0 0.0 reduce-scatter.2.cloned.1.call-start
  8.1 1.3 dynamic-slice
  10.0 0.9 dynamic-update-slice
  10.8 8.2 all-reduce
  19.0 8.5 %all_gather.15 = s32[32,32]{1,0:T(8,128)S(1)} all-gather(s32[16,32]{1,0:T(8,128)} %param.8), channel_id=1, replica_groups=mesh['page'=32,'yh'=2,'xc'=8] {'yh'}, dimensions={0}, use_global_device_ids=true | all-gather | bytes 6144 | tf_op jit(solution)/shard_map/all_gather | solution.py:28
  27.5 0.1 iota_compare_fusion
  27.6 0.7 and_reduce_fusion
  28.2 0.1 broadcast_in_dim.30
  28.4 15.9 %all_gather.18 = bf16[32,8192]{1,0:T(8,128)(2,1)S(1)} all-gather(bf16[16,8192]{1,0:T(8,128)(2,1)} %param.5), channel_id=1, replica_groups=mesh['page'=32,'yh'=2,'xc'=8] {'yh'}, dimensions={0}, use_global_device_ids=true | all-gather | bytes 786432 | tf_op jit(solution)/shard_map/all_gather | solution.py:27
  44.3 0.1 copy.54
  44.4 0.0 all-gather.3.cloned.1.call-done
  44.4 2.2 copy.53
  46.6 5.3 fusion
  51.9 365.6 %pmax.7 = f32[32,8,8]{0,2,1:T(8,128)S(1)} all-reduce(f32[32,8,8]{0,2,1:T(8,128)S(1)} %get-tuple-element.7), channel_id=1, replica_groups=mesh['page'=32,'yh'=2,'xc'=8] {'page','yh'}, use_global_device_ids=true, to_apply=%region_2.3 | all-reduce | flops 2048 | bytes 16384 | tf_op jit(solution)/shard_map/pmax | solution.py:51
  417.5 4.7 fusion.1
  422.2 0.0 all-gather.5.cloned.1.call-done
  422.2 2.2 copy.55
  424.5 4.8 fusion.14
  429.3 1.1 copy.41
  430.5 1.3 dynamic-slice.1
  431.7 0.1 reshape.59
  431.9 0.1 copy.44
  431.9 363.2 %all-reduce.1 = f32[64,16,2]{1,2,0:T(2,128)S(1)} all-reduce(f32[64,16,2]{1,2,0:T(2,128)S(1)} %copy.44), channel_id=3, replica_groups=mesh['page'=32,'yh'=2,'xc'=8] {'page','yh'}, use_global_device_ids=true, to_apply=%region_5.6.clone | all-reduce | flops 2048 | bytes 16384
  795.1 0.6 dynamic-slice_bitcast_fusion
  795.8 0.1 copy.45
  795.9 12.5 %reduce-scatter.2.cloned.1.call-done = f32[1,16,2,128]{3,1,2,0:T(8,128)} async-done(((f32[64,16,2,128]{3,1,2,0:T(8,128)}), f32[1,16,2,128]{3,1,2,0:T(8,128)}) %reduce-scatter.2.cloned.1.call-update) | async-done | bytes 16400 | tf_op jit(solution)/shard_map/reduce_scatter | solution.py:66
  808.4 0.7 copy.42
  809.1 0.1 div.14
  809.2 0.6 fusion.20
  (7 shorter events, 0.1 us)
Async XLA Ops:
  6.5 37.9 %all-gather.3.cloned.1.call-start = ((), (), s32[]{:S(2)}) async-start(), calls=%async_computation.1 | async-start | bytes 2359296 | tf_op jit(solution)/shard_map/all_gather | solution.py:30
  7.3 415.0 %all-gather.5.cloned.1.call-start = ((), (), s32[]{:S(2)}) async-start(), calls=%async_computation.2 | async-start | bytes 2359296 | tf_op jit(solution)/shard_map/all_gather | solution.py:31
  8.0 800.4 %reduce-scatter.2.cloned.1.call-start = ((), (), s32[]{:S(2)}) async-start(), calls=%async_computation.3 | async-start | bytes 1064960 | tf_op jit(solution)/shard_map/reduce_scatter | solution.py:66
Sparse Core Ops, SparseCore 0:
  9.5 34.0 all-gather.2
  45.7 30.9 all-gather.4
  430.6 377.7 reduce-scatter.1

commit v2 on v1

v2 whole, which is shorter than its diff:
```python
import math

import jax
import jax.numpy as jnp
from jax import lax
from jax.sharding import Mesh
from jax.sharding import PartitionSpec as P

H = 64
KVH = 8
HD = 128
LANES = 128


def body(queries, key_pool, value_pool, page_table, page_count):
    n_page = lax.axis_size("page")
    n_yh = lax.axis_size("yh")
    n_xc = lax.axis_size("xc")
    page_index = lax.axis_index("page")
    yh_index = lax.axis_index("yh")
    pages_held = key_pool.shape[0]
    page_len = key_pool.shape[1]
    per_kv = H // KVH
    own_heads = H // n_page
    rows = queries.shape[0]
    score_scale = 1.0 / math.sqrt(HD)

    row_pages = n_yh * n_xc * pages_held
    row_ids = page_index * row_pages + jnp.arange(row_pages, dtype=jnp.int32)
    slot_live = jnp.arange(page_table.shape[1], dtype=jnp.int32)[None, :] < page_count[:, None]
    row_hit = jnp.any(
        (page_table[:, :, None] == row_ids[None, None, :]) & slot_live[:, :, None], axis=1
    )
    mask_cols = -(-row_pages // LANES) * LANES
    row_hit = jnp.pad(row_hit.astype(queries.dtype), ((0, 0), (0, mask_cols - row_pages)))
    packed = jnp.concatenate([queries, row_hit], axis=1)

    all_packed = lax.all_gather(packed, "yh", tiled=True)
    keys = lax.all_gather(key_pool, "xc", tiled=True)
    values = lax.all_gather(value_pool, "xc", tiled=True)

    req_rows = all_packed.shape[0]
    all_q = all_packed[:, : H * HD]
    held = n_xc * pages_held
    page_hit = lax.dynamic_slice_in_dim(all_packed, H * HD + yh_index * held, held, 1) > 0.5
    token_hit = jnp.repeat(page_hit, page_len, axis=1)[:, None, None, :]

    grouped = all_q.reshape(req_rows, KVH, per_kv, HD)
    token_keys = keys.reshape(-1, KVH, HD)
    token_values = values.reshape(-1, KVH, HD)
    scores = (
        jnp.einsum("rkgd,tkd->rkgt", grouped, token_keys, preferred_element_type=jnp.float32)
        * score_scale
    )
    scores = jnp.where(token_hit, scores, jnp.float32(-1e30))
    local_max = jnp.max(scores, axis=3)
    exp_terms = jnp.where(token_hit, jnp.exp(scores - local_max[..., None]), jnp.float32(0.0))
    local_sum = jnp.sum(exp_terms, axis=3)
    weights = exp_terms.astype(jnp.bfloat16)
    local_out = jnp.einsum(
        "rkgt,tkd->rkgd", weights, token_values, preferred_element_type=jnp.float32
    )

    n_blocks = n_page * n_yh
    block_rows = rows * own_heads
    out_blocks = local_out.reshape(n_yh, rows, n_page, own_heads, HD).transpose(2, 0, 1, 3, 4)
    out_blocks = out_blocks.reshape(n_blocks, block_rows, HD)
    max_blocks = local_max.reshape(n_yh, rows, n_page, own_heads).transpose(2, 0, 1, 3)
    sum_blocks = local_sum.reshape(n_yh, rows, n_page, own_heads).transpose(2, 0, 1, 3)
    stat_cols = -(-2 * block_rows // HD) * HD
    stats = jnp.concatenate(
        [
            max_blocks.reshape(n_blocks, block_rows),
            sum_blocks.reshape(n_blocks, block_rows),
            jnp.zeros((n_blocks, stat_cols - 2 * block_rows), jnp.float32),
        ],
        axis=1,
    )
    payload = jnp.concatenate([out_blocks, stats.reshape(n_blocks, -1, HD)], axis=1)
    arrived = lax.all_to_all(payload, ("page", "yh"), 0, 0, tiled=True)

    part_out = arrived[:, :block_rows, :]
    part_stats = arrived[:, block_rows:, :].reshape(n_blocks, stat_cols)
    part_max = part_stats[:, :block_rows]
    part_sum = part_stats[:, block_rows : 2 * block_rows]
    joint_max = jnp.max(part_max, axis=0)
    factor = jnp.exp(part_max - joint_max[None, :])
    joint_sum = jnp.sum(part_sum * factor, axis=0)
    joint_out = jnp.sum(part_out * factor[..., None], axis=0)
    result = joint_out / joint_sum[:, None]
    return result.reshape(rows, own_heads * HD).astype(jnp.bfloat16)


def solution(mesh):
    n_page, n_req = mesh.devices.shape
    n_yh = 2 if n_req % 2 == 0 else 1
    split = Mesh(mesh.devices.reshape(n_page, n_yh, n_req // n_yh), ("page", "yh", "xc"))
    req = ("yh", "xc")
    return jax.shard_map(
        body,
        mesh=split,
        in_specs=(
            P(req, None),
            P(("page",) + req, None, None),
            P(("page",) + req, None, None),
            P(req, None),
            P(req),
        ),
        out_specs=P(req, "page"),
        check_vma=False,
    )
```

time: 818 us -> 145 us (0.18)
  blocking collectives: 761 us -> 63.7 us
  waiting for transfers between devices: 13.9 us -> 37.9 us
    unnamed x2 -> x0, blocking collectives: 371 us -> none
    pmax x1 -> x0, blocking collectives: 366 us -> none  [body(): global_max = lax.pmax(local_max, ('page', 'yh'))]
    all_to_all x0 -> x1, blocking collectives: none -> 49.1 us  [body(): arrived = lax.all_to_all(payload, ('page', 'yh'), 0, 0, tiled=True)]
    all_gather x1, waiting for transfers between devices: 0.02 us -> 18.9 us  [body(): values = lax.all_gather(value_pool, 'xc', tiled=True)]
    all_gather x1, waiting for transfers between devices: 0.02 us -> 17.5 us  [body(): keys = lax.all_gather(key_pool, 'xc', tiled=True)]
    reduce_scatter x1 -> x0, waiting for transfers between devices: 12.5 us -> none  [body(): lax.psum_scatter(out_blocks, ('page', 'yh'), scatter_dimension=0, tiled=T...]
    all_gather x2 -> x1, blocking collectives: 24.3 us -> 14.7 us  [body(): all_packed = lax.all_gather(packed, 'yh', tiled=True)]
  transfers between devices with their start and end apart: 3 -> 2, of which waited for: 1 -> 2; matrix products, arithmetic and copies ran while one was open for 2% -> 12% of each run, Pallas kernels for 0% -> 0%
where the time goes in v2:
time: 145 us; the launch traced here: 143 us
  blocking collectives  63.7 us (44%)
  waiting for transfers between devices  37.9 us (26%)
  between operations  13.6 us (9%)
  matrix products  10.3 us (7%)
  other arithmetic  9.35 us (6%)
  local copies, waits for them, and re-layouts  7.74 us (5%)
    all_to_all x1, blocking collectives, body(): arrived = lax.all_to_all(payload, ('page', 'yh'), 0, 0, tiled=True)  49.1 us
    all_gather x1, waiting for transfers between devices, body(): values = lax.all_gather(value_pool, 'xc', tiled=True)  18.9 us
    all_gather x1, waiting for transfers between devices, body(): keys = lax.all_gather(key_pool, 'xc', tiled=True)  17.5 us
    all_gather x1, blocking collectives, body(): all_packed = lax.all_gather(packed, 'yh', tiled=True)  14.7 us
    reduce_sum x1, other arithmetic, body(): local_sum = jnp.sum(exp_terms, axis=3)  5.17 us
    dot_general x1, matrix products, body(): jnp.einsum('rkgt,tkd->rkgd', weights, token_values, preferred_element_typ...  5.14 us
    dot_general x1, matrix products, body(): jnp.einsum('rkgd,tkd->rkgt', grouped, token_keys, preferred_element_type=...  5.13 us
    unnamed x5, local copies, waits for them, and re-layouts  4.59 us
  transfers between devices with their start and end apart: 2, of which 2 were waited for; matrix products, arithmetic and copies ran while one was open for 12% of the time, Pallas kernels for 0%

profile of v2, /device:TPU:6, one launch (start us, length us, event | category | flops | bytes accessed | tf_op | source)
XLA Modules:
  0.0 142.6 jit_solution(15947121690895109157)
XLA Ops:
  6.5 0.7 all-gather.3.cloned.1.call-update
  7.3 0.7 all-gather.5.cloned.1.call-update
  8.0 0.7 iota_compare_fusion
  8.8 1.1 and_reduce_fusion
  9.9 1.0 pad_maximum_fusion.1
  10.9 14.7 %all_gather.9 = bf16[32,8320]{1,0:T(8,128)(2,1)S(1)} all-gather(bf16[16,8320]{1,0:T(8,128)(2,1)S(1)} %pad_maximum_fusion.1), channel_id=1, replica_groups=mesh['page'=32,'yh'=2,'xc'=8] {'yh'}, dimensions={0}, use_global_device_ids=true | all-gather | bytes 798720 | tf_op jit(solution)/shard_map/all_gather | solution.py:38
  25.6 0.1 broadcast_in_dim.37
  25.8 0.1 copy.49
  26.0 17.5 %all-gather.3.cloned.1.call-done = bf16[8,128,1024]{2,1,0:T(8,128)(2,1)} async-done(((bf16[1,128,1024]{2,1,0:T(8,128)(2,1)}), bf16[8,128,1024]{2,1,0:T(8,128)(2,1)}) %all-gather.3.cloned.1.call-update) | async-done | bytes 2097168 | tf_op jit(solution)/shard_map/all_gather | solution.py:39
  43.5 2.2 %copy.50 = bf16[128,8,8,128]{3,2,1,0:T(8,128)(2,1)S(1)} copy(bf16[128,8,8,128]{3,1,2,0:T(8,128)(2,1)} %bitcast.60) | data formatting | bytes 4194304
  45.8 5.1 %bitcast_reduce_fusion = (f32[32,8,8]{2,0,1:T(8,128)S(1)}, f32[8,32,8,1024]{3,2,1,0:T(8,128)}) fusion(pred[32,1024]{1,0:T(8,128)(4,1)S(1)} %bitcast.62, bf16[1024,8,128,1]{2,1,0,3:T(8,128)(2,1)S(1)} %bitcast.55, bf16[32,8,8,128]{3,2,1,0:T(8,128)(2,1)S(1)} %bitcast.58), kind=kOutput, calls=%fused_computation.1 | convolution fusion | flops 543160320 | bytes 11051008 | tf_op jit(solution)/shard_map/rkgd,tkd->rkgt/dot_general | solution.py:52
  50.9 0.1 copy.32
  51.0 5.2 %fusion.2 = f32[32,8,8]{2,0,1:T(8,128)S(1)} fusion(f32[8,32,8,1024]{3,2,1,0:T(8,128)} %get-tuple-element.8, f32[32,8,8]{2,0,1:T(8,128)S(1)} %get-tuple-element.7, pred[32,1024]{1,0:T(8,128)(4,1)S(1)} %bitcast.63), kind=kLoop, calls=%fused_computation.5 | loop fusion | flops 10483712 | bytes 8437760 | tf_op jit(solution)/shard_map/reduce_sum | solution.py:58
  56.1 0.1 copy.34
  56.2 0.1 reshape.76
  56.3 0.4 copy.45
  56.8 0.2 reshape.83
  57.0 0.1 reshape.74
  57.1 0.4 copy.44
  57.6 0.2 reshape.82
  57.8 18.9 %all-gather.5.cloned.1.call-done = bf16[8,128,1024]{2,1,0:T(8,128)(2,1)} async-done(((bf16[1,128,1024]{2,1,0:T(8,128)(2,1)}), bf16[8,128,1024]{2,1,0:T(8,128)(2,1)}) %all-gather.5.cloned.1.call-update) | async-done | bytes 2097168 | tf_op jit(solution)/shard_map/all_gather | solution.py:40
  76.8 2.2 %copy.51 = bf16[128,8,8,128]{3,2,1,0:T(8,128)(2,1)S(1)} copy(bf16[128,8,8,128]{3,1,2,0:T(8,128)(2,1)} %bitcast.59) | data formatting | bytes 4194304
  79.0 5.1 %fusion.11 = f32[32,8,8,128]{3,2,0,1:T(8,128)S(1)} fusion(bf16[1024,8,128,1]{2,1,0,3:T(8,128)(2,1)S(1)} %bitcast.61, f32[8,32,8,1024]{3,2,1,0:T(8,128)} %get-tuple-element.8, f32[32,8,8]{2,0,1:T(8,128)S(1)} %get-tuple-element.7, pred[32,1024]{1,0:T(8,128)(4,1)S(1)} %bitcast.64), kind=kOutput, calls=%fused_computation.13 | convolution fusion | flops 547356672 | bytes 11575296 | tf_op jit(solution)/shard_map/rkgt,tkd->rkgd/dot_general | solution.py:60
  84.1 0.2 copy.30
  84.3 0.8 copy.31
  85.2 0.1 maximum_maximum_fusion
  85.3 0.1 pad_maximum_fusion
  85.4 49.1 %all_to_all.5 = f32[64,33,128]{2,1,0:T(8,128)S(1)} all-to-all(f32[64,33,128]{2,1,0:T(8,128)S(1)} %pad_maximum_fusion), channel_id=1, replica_groups=mesh['page'=32,'yh'=2,'xc'=8] {'page','yh'}, dimensions={0} | all-to-all | bytes 2162688 | tf_op jit(solution)/shard_map/all_to_all | solution.py:80
  134.5 0.1 fusion.18
  134.6 0.3 fusion.16
  134.9 0.1 div.13
  135.1 0.6 fusion.19
  (13 shorter events, 0.4 us)
Async XLA Ops:
  6.5 37.0 %all-gather.3.cloned.1.call-start = ((), (), s32[]{:S(2)}) async-start(), calls=%async_computation.1 | async-start | bytes 2359296 | tf_op jit(solution)/shard_map/all_gather | solution.py:39
  7.3 69.5 %all-gather.5.cloned.1.call-start = ((), (), s32[]{:S(2)}) async-start(), calls=%async_computation.2 | async-start | bytes 2359296 | tf_op jit(solution)/shard_map/all_gather | solution.py:40
Sparse Core Ops, SparseCore 0:
  9.5 34.0 all-gather.2
  45.7 31.0 all-gather.4

commit v3 on v2

--- a/solution.py
+++ b/solution.py
@@ -10,6 +10,12 @@
 KVH = 8
 HD = 128
 LANES = 128
+
+
+def split_pair(value):
+    high = lax.reduce_precision(value, exponent_bits=8, mantissa_bits=7)
+    low = lax.reduce_precision(value - high, exponent_bits=8, mantissa_bits=7)
+    return high, low
 
 
 def body(queries, key_pool, value_pool, page_table, page_count):
@@ -53,7 +59,8 @@
         * score_scale
     )
     scores = jnp.where(token_hit, scores, jnp.float32(-1e30))
-    local_max = jnp.max(scores, axis=3)
+    max_hi, max_lo = split_pair(jnp.max(scores, axis=3))
+    local_max = max_hi + max_lo
     exp_terms = jnp.where(token_hit, jnp.exp(scores - local_max[..., None]), jnp.float32(0.0))
     local_sum = jnp.sum(exp_terms, axis=3)
     weights = exp_terms.astype(jnp.bfloat16)
@@ -63,26 +70,28 @@
 
     n_blocks = n_page * n_yh
     block_rows = rows * own_heads
-    out_blocks = local_out.reshape(n_yh, rows, n_page, own_heads, HD).transpose(2, 0, 1, 3, 4)
+    out_blocks = local_out.astype(jnp.bfloat16)
+    out_blocks = out_blocks.reshape(n_yh, rows, n_page, own_heads, HD).transpose(2, 0, 1, 3, 4)
     out_blocks = out_blocks.reshape(n_blocks, block_rows, HD)
-    max_blocks = local_max.reshape(n_yh, rows, n_page, own_heads).transpose(2, 0, 1, 3)
-    sum_blocks = local_sum.reshape(n_yh, rows, n_page, own_heads).transpose(2, 0, 1, 3)
-    stat_cols = -(-2 * block_rows // HD) * HD
+    sum_hi, sum_lo = split_pair(local_sum)
+
+    def to_blocks(stat):
+        stat = stat.astype(jnp.bfloat16).reshape(n_yh, rows, n_page, own_heads).transpose(2, 0, 1, 3)
+        return stat.reshape(n_blocks, block_rows)
+
+    stat_cols = -(-4 * block_rows // HD) * HD
     stats = jnp.concatenate(
-        [
-            max_blocks.reshape(n_blocks, block_rows),
-            sum_blocks.reshape(n_blocks, block_rows),
-            jnp.zeros((n_blocks, stat_cols - 2 * block_rows), jnp.float32),
-        ],
+        [to_blocks(max_hi), to_blocks(max_lo), to_blocks(sum_hi), to_blocks(sum_lo)]
+        + [jnp.zeros((n_blocks, stat_cols - 4 * block_rows), jnp.bfloat16)],
         axis=1,
     )
     payload = jnp.concatenate([out_blocks, stats.reshape(n_blocks, -1, HD)], axis=1)
     arrived = lax.all_to_all(payload, ("page", "yh"), 0, 0, tiled=True)
 
-    part_out = arrived[:, :block_rows, :]
-    part_stats = arrived[:, block_rows:, :].reshape(n_blocks, stat_cols)
-    part_max = part_stats[:, :block_rows]
-    part_sum = part_stats[:, block_rows : 2 * block_rows]
+    part_out = arrived[:, :block_rows, :].astype(jnp.float32)
+    part_stats = arrived[:, block_rows:, :].reshape(n_blocks, stat_cols).astype(jnp.float32)
+    part_max = part_stats[:, :block_rows] + part_stats[:, block_rows : 2 * block_rows]
+    part_sum = part_stats[:, 2 * block_rows : 3 * block_rows] + part_stats[:, 3 * block_rows : 4 * block_rows]
     joint_max = jnp.max(part_max, axis=0)
     factor = jnp.exp(part_max - joint_max[None, :])
     joint_sum = jnp.sum(part_sum * factor, axis=0)

time: 145 us -> 131 us (0.903)
  blocking collectives: 63.7 us -> 50.8 us
  waiting for transfers between devices: 37.9 us -> 35.2 us
  local copies, waits for them, and re-layouts: 7.74 us -> 9.83 us
    all_to_all x1, blocking collectives: 49.1 us -> 36.1 us  [body(): arrived = lax.all_to_all(payload, ('page', 'yh'), 0, 0, tiled=True)]
    all_gather x1, waiting for transfers between devices: 18.9 us -> 16.2 us  [body(): values = lax.all_gather(value_pool, 'xc', tiled=True)]
    transpose x2 -> x5, local copies, waits for them, and re-layouts: 1.02 us -> 2.99 us  [the longest x4 2.46 us: to_blocks(): stat.astype(jnp.bfloat16).reshape(n_yh, rows, n_page, own_heads)]
  transfers between devices with their start and end apart: 2 -> 2, of which waited for: 2 -> 2; matrix products, arithmetic and copies ran while one was open for 12% -> 16% of each run, Pallas kernels for 0% -> 0%
where the time goes in v3:
time: 131 us; the launch traced here: 130 us
  blocking collectives  50.8 us (39%)
  waiting for transfers between devices  35.2 us (27%)
  between operations  13.6 us (10%)
  matrix products  11 us (8%)
  local copies, waits for them, and re-layouts  9.83 us (8%)
  other arithmetic  9.43 us (7%)
    all_to_all x1, blocking collectives, body(): arrived = lax.all_to_all(payload, ('page', 'yh'), 0, 0, tiled=True)  36.1 us
    all_gather x1, waiting for transfers between devices, body(): keys = lax.all_gather(key_pool, 'xc', tiled=True)  17.6 us
    all_gather x1, waiting for transfers between devices, body(): values = lax.all_gather(value_pool, 'xc', tiled=True)  16.2 us
    all_gather x1, blocking collectives, body(): all_packed = lax.all_gather(packed, 'yh', tiled=True)  14.7 us
    dot_general x1, matrix products, body(): jnp.einsum('rkgt,tkd->rkgd', weights, token_values, preferred_element_typ...  5.89 us
    reduce_sum x1, other arithmetic, body(): local_sum = jnp.sum(exp_terms, axis=3)  5.16 us
    dot_general x1, matrix products, body(): jnp.einsum('rkgd,tkd->rkgt', grouped, token_keys, preferred_element_type=...  5.13 us
    unnamed x5, local copies, waits for them, and re-layouts  4.59 us
  transfers between devices with their start and end apart: 2, of which 2 were waited for; matrix products, arithmetic and copies ran while one was open for 16% of the time, Pallas kernels for 0%

profile of v3, /device:TPU:6, one launch (start us, length us, event | category | flops | bytes accessed | tf_op | source)
XLA Modules:
  0.0 129.9 jit_solution(13986388797241195186)
XLA Ops:
  6.5 0.7 all-gather.3.cloned.1.call-update
  7.3 0.7 all-gather.5.cloned.1.call-update
  8.0 0.7 iota_compare_fusion
  8.8 1.1 and_reduce_fusion
  9.9 1.0 pad_maximum_fusion.1
  10.9 14.7 %all_gather.9 = bf16[32,8320]{1,0:T(8,128)(2,1)S(1)} all-gather(bf16[16,8320]{1,0:T(8,128)(2,1)S(1)} %pad_maximum_fusion.1), channel_id=1, replica_groups=mesh['page'=32,'yh'=2,'xc'=8] {'yh'}, dimensions={0}, use_global_device_ids=true | all-gather | bytes 798720 | tf_op jit(solution)/shard_map/all_gather | solution.py:44
  25.6 0.1 broadcast_in_dim.34
  25.8 0.1 copy.69
  25.9 17.6 %all-gather.3.cloned.1.call-done = bf16[8,128,1024]{2,1,0:T(8,128)(2,1)} async-done(((bf16[1,128,1024]{2,1,0:T(8,128)(2,1)}), bf16[8,128,1024]{2,1,0:T(8,128)(2,1)}) %all-gather.3.cloned.1.call-update) | async-done | bytes 2097168 | tf_op jit(solution)/shard_map/all_gather | solution.py:45
  43.5 2.2 %copy.70 = bf16[128,8,8,128]{3,2,1,0:T(8,128)(2,1)S(1)} copy(bf16[128,8,8,128]{3,1,2,0:T(8,128)(2,1)} %bitcast.80) | data formatting | bytes 4194304
  45.8 5.1 %bitcast_reduce_fusion = (f32[32,8,8]{2,0,1:T(8,128)S(1)}, f32[8,32,8,1024]{3,2,1,0:T(8,128)}) fusion(pred[32,1024]{1,0:T(8,128)(4,1)S(1)} %bitcast.85, bf16[1024,8,128,1]{2,1,0,3:T(8,128)(2,1)S(1)} %bitcast.76, bf16[32,8,8,128]{3,2,1,0:T(8,128)(2,1)S(1)} %bitcast.77), kind=kOutput, calls=%fused_computation.1 | convolution fusion | flops 543160320 | bytes 11051008 | tf_op jit(solution)/shard_map/rkgd,tkd->rkgt/dot_general | solution.py:58
  51.0 0.1 reduce_max.21
  51.2 5.2 %fusion.2 = f32[32,8,8]{2,0,1:T(8,128)S(1)} fusion(f32[8,32,8,1024]{3,2,1,0:T(8,128)} %get-tuple-element.12, f32[32,8,8]{2,0,1:T(8,128)S(1)} %copy.48, pred[32,1024]{1,0:T(8,128)(4,1)S(1)} %bitcast.86), kind=kLoop, calls=%fused_computation.5 | loop fusion | flops 10483712 | bytes 8437760 | tf_op jit(solution)/shard_map/reduce_sum | solution.py:65
  56.4 0.1 reduce_sum.32
  56.6 0.6 copy.56
  57.2 0.3 reshape.89
  57.6 0.6 copy.57
  58.2 0.3 reshape.90
  58.6 0.6 copy.53
  59.2 0.3 reshape.87
  59.5 0.6 copy.54
  60.2 0.3 reshape.88
  60.5 0.1 copy.59
  60.6 16.2 %all-gather.5.cloned.1.call-done = bf16[8,128,1024]{2,1,0:T(8,128)(2,1)} async-done(((bf16[1,128,1024]{2,1,0:T(8,128)(2,1)}), bf16[8,128,1024]{2,1,0:T(8,128)(2,1)}) %all-gather.5.cloned.1.call-update) | async-done | bytes 2097168 | tf_op jit(solution)/shard_map/all_gather | solution.py:46
  76.8 2.2 %copy.71 = bf16[128,8,8,128]{3,2,1,0:T(8,128)(2,1)S(1)} copy(bf16[128,8,8,128]{3,1,2,0:T(8,128)(2,1)} %bitcast.79) | data formatting | bytes 4194304
  79.0 5.9 %fusion.16 = bf16[32,8,8,128]{3,2,0,1:T(8,128)(2,1)S(1)} fusion(bf16[1024,8,128,1]{2,1,0,3:T(8,128)(2,1)S(1)} %bitcast.81, f32[8,32,8,1024]{3,2,1,0:T(8,128)} %get-tuple-element.12, f32[32,8,8]{2,0,1:T(8,128)S(1)} %copy.48, pred[32,1024]{1,0:T(8,128)(4,1)S(1)} %bitcast.87), kind=kOutput, calls=%fused_computation.14 | convolution fusion | flops 547618816 | bytes 11051008 | tf_op jit(solution)/shard_map/rkgt,tkd->rkgd/dot_general | solution.py:67
  85.0 0.5 copy.51
  85.6 36.1 %all_to_all.5 = bf16[64,33,128]{2,1,0:T(8,128)(2,1)S(1)} all-to-all(bf16[64,33,128]{2,1,0:T(8,128)(2,1)S(1)} %pad_maximum_fusion), channel_id=1, replica_groups=mesh['page'=32,'yh'=2,'xc'=8] {'page','yh'}, dimensions={0} | all-to-all | bytes 1081344 | tf_op jit(solution)/shard_map/all_to_all | solution.py:89
  121.7 0.1 fusion.34
  121.8 0.1 fusion.30
  121.9 0.3 multiply_reduce_fusion
  122.4 0.6 fusion.33
  (20 shorter events, 0.9 us)
Async XLA Ops:
  6.5 37.0 %all-gather.3.cloned.1.call-start = ((), (), s32[]{:S(2)}) async-start(), calls=%async_computation.1 | async-start | bytes 2359296 | tf_op jit(solution)/shard_map/all_gather | solution.py:45
  7.3 69.5 %all-gather.5.cloned.1.call-start = ((), (), s32[]{:S(2)}) async-start(), calls=%async_computation.2 | async-start | bytes 2359296 | tf_op jit(solution)/shard_map/all_gather | solution.py:46
Sparse Core Ops, SparseCore 0:
  9.5 34.0 all-gather.2
  45.7 31.0 all-gather.4

commit v4 on v3

--- a/solution.py
+++ b/solution.py
@@ -43,7 +43,15 @@
 
     all_packed = lax.all_gather(packed, "yh", tiled=True)
     keys = lax.all_gather(key_pool, "xc", tiled=True)
-    values = lax.all_gather(value_pool, "xc", tiled=True)
+    values = lax.all_to_all(
+        jnp.broadcast_to(value_pool[None], (n_xc,) + value_pool.shape).reshape(
+            (n_xc * pages_held,) + value_pool.shape[1:]
+        ),
+        "xc",
+        0,
+        0,
+        tiled=True,
+    )
 
     req_rows = all_packed.shape[0]
     all_q = all_packed[:, : H * HD]

time: 131 us -> 123 us (0.939)
  waiting for transfers between devices: 35.2 us -> 13.2 us
  starting transfers between devices: 0.04 us -> 9.36 us
  local copies, waits for them, and re-layouts: 9.83 us -> 12.1 us
    all_gather x1, waiting for transfers between devices: 17.6 us -> 0.01 us  [body(): keys = lax.all_gather(key_pool, 'xc', tiled=True)]
    all_gather x1 -> x0, waiting for transfers between devices: 16.2 us -> none  [body(): values = lax.all_gather(value_pool, 'xc', tiled=True)]
    all_to_all x0 -> x1, waiting for transfers between devices: none -> 12.5 us  [body(): lax.all_to_all(jnp.broadcast_to(value_pool[None], (n_xc,) + value_pool.sh...]
    all_to_all x0 -> x1, starting transfers between devices: none -> 9.36 us  [body(): lax.all_to_all(jnp.broadcast_to(value_pool[None], (n_xc,) + value_pool.sh...]
    all_gather x1, blocking collectives: 14.7 us -> 17.8 us  [body(): all_packed = lax.all_gather(packed, 'yh', tiled=True)]
    reshape x0 -> x1, local copies, waits for them, and re-layouts: none -> 2.51 us  [body(): jnp.broadcast_to(value_pool[None], (n_xc,) + value_pool.shape)]
    all_to_all x1, blocking collectives: 36.1 us -> 34.3 us  [body(): arrived = lax.all_to_all(payload, ('page', 'yh'), 0, 0, tiled=True)]
    unnamed x5 -> x7, local copies, waits for them, and re-layouts: 4.59 us -> 4.4 us
  transfers between devices with their start and end apart: 2 -> 2, of which waited for: 2 -> 1; matrix products, arithmetic and copies ran while one was open for 16% -> 6% of each run, Pallas kernels for 0% -> 0%
where the time goes in v4:
time: 123 us; the launch traced here: 121 us
  blocking collectives  52.1 us (42%)
  between operations  13.6 us (11%)
  waiting for transfers between devices  13.2 us (11%)
  local copies, waits for them, and re-layouts  12.1 us (10%)
  matrix products  11 us (9%)
  other arithmetic  9.6 us (8%)
  starting transfers between devices  9.36 us (8%)
    all_to_all x1, blocking collectives, body(): arrived = lax.all_to_all(payload, ('page', 'yh'), 0, 0, tiled=True)  34.3 us
    all_gather x1, blocking collectives, body(): all_packed = lax.all_gather(packed, 'yh', tiled=True)  17.8 us
    all_to_all x1, waiting for transfers between devices, body(): lax.all_to_all(jnp.broadcast_to(value_pool[None], (n_xc,) + value_pool.sh...  12.5 us
    all_to_all x1, starting transfers between devices, body(): lax.all_to_all(jnp.broadcast_to(value_pool[None], (n_xc,) + value_pool.sh...  9.36 us
    dot_general x1, matrix products, body(): jnp.einsum('rkgt,tkd->rkgd', weights, token_values, preferred_element_typ...  5.88 us
    reduce_sum x1, other arithmetic, body(): local_sum = jnp.sum(exp_terms, axis=3)  5.32 us
    dot_general x1, matrix products, body(): jnp.einsum('rkgd,tkd->rkgt', grouped, token_keys, preferred_element_type=...  5.13 us
    unnamed x7, local copies, waits for them, and re-layouts  4.4 us
  transfers between devices with their start and end apart: 2, of which 1 were waited for; matrix products, arithmetic and copies ran while one was open for 6% of the time, Pallas kernels for 0%

profile of v4, /device:TPU:6, one launch (start us, length us, event | category | flops | bytes accessed | tf_op | source)
XLA Modules:
  0.0 121.0 jit_solution(18207185544669441702)
XLA Ops:
  6.5 0.7 all-gather.2.cloned.1.call-update
  7.3 2.5 %reshape.90 = bf16[8,128,1024]{2,1,0:T(8,128)(2,1)} broadcast(bf16[128,1024]{1,0:T(8,128)(2,1)} %bitcast.89), dimensions={1,2} | broadcast | bytes 2359296 | tf_op jit(solution)/shard_map/reshape | solution.py:47
  9.8 9.4 %all-to-all-start = ((bf16[8,128,1024]{2,1,0:T(8,128)(2,1)}), bf16[8,128,1024]{2,1,0:T(8,128)(2,1)S(1)}, u32[]{:S(2)}, u32[]{:S(2)}) async-start(bf16[8,128,1024]{2,1,0:T(8,128)(2,1)} %reshape.90), calls=%async_computation | async-start | bytes 4194304 | tf_op jit(solution)/shard_map/all_to_all | solution.py:46
  19.1 0.7 iota_compare_fusion
  19.9 1.1 and_reduce_fusion
  21.0 1.0 pad_maximum_fusion.1
  22.0 17.8 %all_gather.6 = bf16[32,8320]{1,0:T(8,128)(2,1)S(1)} all-gather(bf16[16,8320]{1,0:T(8,128)(2,1)S(1)} %pad_maximum_fusion.1), channel_id=1, replica_groups=mesh['page'=32,'yh'=2,'xc'=8] {'yh'}, dimensions={0}, use_global_device_ids=true | all-gather | bytes 798720 | tf_op jit(solution)/shard_map/all_gather | solution.py:44
  39.8 0.1 broadcast_in_dim.40
  40.0 0.1 copy.69
  40.1 12.5 %all-to-all-done = bf16[8,128,1024]{2,1,0:T(8,128)(2,1)S(1)} async-done(((bf16[8,128,1024]{2,1,0:T(8,128)(2,1)}), bf16[8,128,1024]{2,1,0:T(8,128)(2,1)S(1)}, u32[]{:S(2)}, u32[]{:S(2)}) %all-to-all-start) | async-done | bytes 2097184 | tf_op jit(solution)/shard_map/all_to_all | solution.py:46
  52.6 2.0 %copy.71 = bf16[128,8,8,128]{3,2,1,0:T(8,128)(2,1)} copy(bf16[128,8,8,128]{3,1,2,0:T(8,128)(2,1)S(1)} %bitcast.78) | data formatting | bytes 4194304
  54.7 2.2 %copy.70 = bf16[128,8,8,128]{3,2,1,0:T(8,128)(2,1)S(1)} copy(bf16[128,8,8,128]{3,1,2,0:T(8,128)(2,1)} %bitcast.81) | data formatting | bytes 4194304
  56.9 5.1 %bitcast_reduce_fusion = (f32[32,8,8]{2,0,1:T(8,128)S(1)}, f32[8,32,8,1024]{3,2,1,0:T(8,128)}) fusion(pred[32,1024]{1,0:T(8,128)(4,1)S(1)} %bitcast.86, bf16[1024,8,128,1]{2,1,0,3:T(8,128)(2,1)S(1)} %bitcast.77, bf16[32,8,8,128]{3,2,1,0:T(8,128)(2,1)S(1)} %bitcast.79), kind=kOutput, calls=%fused_computation.1 | convolution fusion | flops 543160320 | bytes 11051008 | tf_op jit(solution)/shard_map/rkgd,tkd->rkgt/dot_general | solution.py:66
  62.1 0.1 reduce_max.21
  62.3 5.3 %fusion.2 = f32[32,8,8]{2,0,1:T(8,128)S(1)} fusion(f32[8,32,8,1024]{3,2,1,0:T(8,128)} %get-tuple-element.12, f32[32,8,8]{2,0,1:T(8,128)S(1)} %copy.48, pred[32,1024]{1,0:T(8,128)(4,1)S(1)} %bitcast.87), kind=kLoop, calls=%fused_computation.5 | loop fusion | flops 10483712 | bytes 8437760 | tf_op jit(solution)/shard_map/reduce_sum | solution.py:73
  67.7 0.1 reduce_sum.32
  67.9 0.6 copy.56
  68.5 0.3 reshape.96
  68.8 0.6 copy.57
  69.5 0.3 reshape.97
  69.9 0.6 copy.53
  70.5 0.3 reshape.94
  70.8 0.6 copy.54
  71.4 0.3 reshape.95
  71.8 0.1 copy.59
  71.9 5.9 %fusion.16 = bf16[32,8,8,128]{3,2,0,1:T(8,128)(2,1)S(1)} fusion(bf16[1024,8,128,1]{2,1,0,3:T(8,128)(2,1)S(1)} %bitcast.82, f32[8,32,8,1024]{3,2,1,0:T(8,128)} %get-tuple-element.12, f32[32,8,8]{2,0,1:T(8,128)S(1)} %copy.48, pred[32,1024]{1,0:T(8,128)(4,1)S(1)} %bitcast.88), kind=kOutput, calls=%fused_computation.14 | convolution fusion | flops 547618816 | bytes 11051008 | tf_op jit(solution)/shard_map/rkgt,tkd->rkgd/dot_general | solution.py:75
  77.9 0.5 copy.51
  78.5 34.3 %all_to_all.10 = bf16[64,33,128]{2,1,0:T(8,128)(2,1)S(1)} all-to-all(bf16[64,33,128]{2,1,0:T(8,128)(2,1)S(1)} %pad_maximum_fusion), channel_id=1, replica_groups=mesh['page'=32,'yh'=2,'xc'=8] {'page','yh'}, dimensions={0} | all-to-all | bytes 1081344 | tf_op jit(solution)/shard_map/all_to_all | solution.py:97
  112.8 0.1 fusion.34
  112.9 0.1 fusion.30
  113.0 0.3 multiply_reduce_fusion
  113.5 0.6 fusion.33
  (22 shorter events, 0.9 us)
Async XLA Ops:
  6.5 48.1 %all-gather.2.cloned.1.call-start = ((), (), s32[]{:S(2)}) async-start(), calls=%async_computation.2 | async-start | bytes 2359296 | tf_op jit(solution)/shard_map/all_gather | solution.py:45
  9.8 42.9 %all-to-all-start = ((bf16[8,128,1024]{2,1,0:T(8,128)(2,1)}), bf16[8,128,1024]{2,1,0:T(8,128)(2,1)S(1)}, u32[]{:S(2)}, u32[]{:S(2)}) async-start(bf16[8,128,1024]{2,1,0:T(8,128)(2,1)} %reshape.90), calls=%async_computation | async-start | bytes 4194304 | tf_op jit(solution)/shard_map/all_to_all | solution.py:46
  62.0 9.9 %copy-start = (bf16[128,8,8,128]{3,2,1,0:T(8,128)(2,1)S(1)}, bf16[128,8,8,128]{3,2,1,0:T(8,128)(2,1)}, u32[]{:S(2)}) copy-start(bf16[128,8,8,128]{3,2,1,0:T(8,128)(2,1)} %copy.71) | copy-start | bytes 6291460
Sparse Core Ops, SparseCore 0:
  9.5 40.3 all-gather.1

commit v5 on v4

--- a/solution.py
+++ b/solution.py
@@ -3,6 +3,8 @@
 import jax
 import jax.numpy as jnp
 from jax import lax
+from jax.experimental import pallas as pl
+from jax.experimental.pallas import tpu as pltpu
 from jax.sharding import Mesh
 from jax.sharding import PartitionSpec as P
 
@@ -16,6 +18,62 @@
     high = lax.reduce_precision(value, exponent_bits=8, mantissa_bits=7)
     low = lax.reduce_precision(value - high, exponent_bits=8, mantissa_bits=7)
     return high, low
+
+
+def attend_kernel(q_ref, k_ref, v_ref, hit_ref, out_ref, stat_ref):
+    pages, page_len, _ = k_ref.shape
+    q = q_ref[0]
+    keys = k_ref[...].reshape(pages * page_len, HD)
+    values = v_ref[...].reshape(pages * page_len, HD)
+    scores = lax.dot_general(
+        q, keys, (((1,), (1,)), ((), ())), preferred_element_type=jnp.float32
+    ) * (1.0 / math.sqrt(HD))
+    req_rows = hit_ref.shape[0]
+    groups = q.shape[0] // req_rows
+    hit = jnp.concatenate([hit_ref[...]] * groups, axis=0) > 0.5
+    scores = jnp.where(hit, scores, jnp.float32(-1e30))
+    top = jnp.max(scores, axis=1, keepdims=True)
+    high = top.astype(jnp.bfloat16).astype(jnp.float32)
+    low = (top - high).astype(jnp.bfloat16).astype(jnp.float32)
+    shift = high + low
+    terms = jnp.where(hit, jnp.exp(scores - shift), jnp.float32(0.0))
+    total = jnp.sum(terms, axis=1, keepdims=True)
+    out_ref[0] = jnp.dot(
+        terms.astype(jnp.bfloat16), values, preferred_element_type=jnp.float32
+    )
+    lane = lax.broadcasted_iota(jnp.int32, (q.shape[0], LANES), 1)
+    stat_ref[0] = jnp.where(
+        lane == 0, high, jnp.where(lane == 1, low, jnp.where(lane == 2, total, 0.0))
+    )
+
+
+def attend(grouped_q, keys, values, token_hit):
+    kv_heads, q_rows, _ = grouped_q.shape
+    pages, page_len, _ = keys.shape
+    tokens = pages * page_len
+    return pl.pallas_call(
+        attend_kernel,
+        grid=(kv_heads,),
+        in_specs=[
+            pl.BlockSpec((1, q_rows, HD), lambda k: (k, 0, 0)),
+            pl.BlockSpec((pages, page_len, HD), lambda k: (0, 0, k)),
+            pl.BlockSpec((pages, page_len, HD), lambda k: (0, 0, k)),
+            pl.BlockSpec(token_hit.shape, lambda k: (0, 0)),
+        ],
+        out_specs=[
+            pl.BlockSpec((1, q_rows, HD), lambda k: (k, 0, 0)),
+            pl.BlockSpec((1, q_rows, LANES), lambda k: (k, 0, 0)),
+        ],
+        out_shape=[
+            jax.ShapeDtypeStruct((kv_heads, q_rows, HD), jnp.float32),
+            jax.ShapeDtypeStruct((kv_heads, q_rows, LANES), jnp.float32),
+        ],
+        cost_estimate=pl.CostEstimate(
+            flops=4 * kv_heads * q_rows * tokens * HD,
+            transcendentals=kv_heads * q_rows * tokens,
+            bytes_accessed=2 * (grouped_q.size + keys.size + values.size) + 4 * 2 * kv_heads * q_rows * HD,
+        ),
+    )(grouped_q, keys, values, token_hit)
 
 
 def body(queries, key_pool, value_pool, page_table, page_count):
@@ -57,24 +115,16 @@
     all_q = all_packed[:, : H * HD]
     held = n_xc * pages_held
     page_hit = lax.dynamic_slice_in_dim(all_packed, H * HD + yh_index * held, held, 1) > 0.5
-    token_hit = jnp.repeat(page_hit, page_len, axis=1)[:, None, None, :]
+    token_hit = jnp.repeat(page_hit, page_len, axis=1).astype(jnp.float32)
 
-    grouped = all_q.reshape(req_rows, KVH, per_kv, HD)
-    token_keys = keys.reshape(-1, KVH, HD)
-    token_values = values.reshape(-1, KVH, HD)
-    scores = (
-        jnp.einsum("rkgd,tkd->rkgt", grouped, token_keys, preferred_element_type=jnp.float32)
-        * score_scale
-    )
-    scores = jnp.where(token_hit, scores, jnp.float32(-1e30))
-    max_hi, max_lo = split_pair(jnp.max(scores, axis=3))
-    local_max = max_hi + max_lo
-    exp_terms = jnp.where(token_hit, jnp.exp(scores - local_max[..., None]), jnp.float32(0.0))
-    local_sum = jnp.sum(exp_terms, axis=3)
-    weights = exp_terms.astype(jnp.bfloat16)
-    local_out = jnp.einsum(
-        "rkgt,tkd->rkgd", weights, token_values, preferred_element_type=jnp.float32
-    )
+    grouped = all_q.reshape(req_rows, KVH, per_kv, HD).transpose(1, 2, 0, 3)
+    grouped = grouped.reshape(KVH, per_kv * req_rows, HD)
+    out_k, stat_k = attend(grouped, keys, values, token_hit)
+    local_out = out_k.reshape(KVH, per_kv, req_rows, HD).transpose(2, 0, 1, 3)
+    stat_k = stat_k.reshape(KVH, per_kv, req_rows, LANES).transpose(2, 0, 1, 3)
+    max_hi = stat_k[..., 0]
+    max_lo = stat_k[..., 1]
+    local_sum = stat_k[..., 2]
 
     n_blocks = n_page * n_yh
     block_rows = rows * own_heads

time: 123 us -> 122 us (level)
  matrix products: 11 us -> 0 us
  Pallas kernels: 0 us -> 9.08 us
  local copies, waits for them, and re-layouts: 12.1 us -> 15.9 us
  other arithmetic: 9.6 us -> 6 us
    dot_general x2 -> x0, matrix products: 11 us -> none  [the longest x1 5.88 us: body(): jnp.einsum('rkgt,tkd->rkgd', weights, token_values, preferred_element_typ...]
    pallas_call x0 -> x1, Pallas kernels: none -> 9.08 us  [attend(): pl.pallas_call(attend_kernel, grid=(kv_heads,), in_specs=[pl.BlockSpec((1...]
    reshape x0 -> x2, local copies, waits for them, and re-layouts: none -> 5.57 us  [the longest x1 4.42 us: body(): stat_k = stat_k.reshape(KVH, per_kv, req_rows, LANES).transpose(2, 0, 1, 3)]
    reduce_sum x1 -> x0, other arithmetic: 5.32 us -> none  [body(): local_sum = jnp.sum(exp_terms, axis=3)]
    another operation x0 -> x1, other arithmetic: none -> 2.69 us
    unnamed x7 -> x13, local copies, waits for them, and re-layouts: 4.4 us -> 2.16 us
    convert_element_type x0 -> x2, other arithmetic: none -> 1.47 us  [the longest x1 1.39 us: body(): out_blocks = local_out.astype(jnp.bfloat16)]
  transfers between devices with their start and end apart: 2 -> 2, of which waited for: 1 -> 1; matrix products, arithmetic and copies ran while one was open for 6% -> 4% of each run, Pallas kernels for 0% -> 0%
where the time goes in v5:
time: 122 us; the launch traced here: 120 us
  blocking collectives  52.1 us (43%)
  local copies, waits for them, and re-layouts  15.9 us (13%)
  waiting for transfers between devices  13.7 us (11%)
  between operations  13.6 us (11%)
  starting transfers between devices  9.49 us (8%)
  Pallas kernels  9.08 us (7%)
  other arithmetic  6 us (5%)
    all_to_all x1, blocking collectives, body(): arrived = lax.all_to_all(payload, ('page', 'yh'), 0, 0, tiled=True)  34.3 us
    all_gather x1, blocking collectives, body(): all_packed = lax.all_gather(packed, 'yh', tiled=True)  17.8 us
    all_to_all x1, waiting for transfers between devices, body(): lax.all_to_all(jnp.broadcast_to(value_pool[None], (n_xc,) + value_pool.sh...  13 us
    all_to_all x1, starting transfers between devices, body(): lax.all_to_all(jnp.broadcast_to(value_pool[None], (n_xc,) + value_pool.sh...  9.49 us
    pallas_call x1, Pallas kernels, attend(): pl.pallas_call(attend_kernel, grid=(kv_heads,), in_specs=[pl.BlockSpec((1...  9.08 us
    reshape x1, local copies, waits for them, and re-layouts, body(): stat_k = stat_k.reshape(KVH, per_kv, req_rows, LANES).transpose(2, 0, 1, 3)  4.42 us
    another operation x1, other arithmetic  2.69 us
    reshape x1, local copies, waits for them, and re-layouts, body(): jnp.broadcast_to(value_pool[None], (n_xc,) + value_pool.shape)  2.52 us
  transfers between devices with their start and end apart: 2, of which 1 were waited for; matrix products, arithmetic and copies ran while one was open for 4% of the time, Pallas kernels for 0%

profile of v5, /device:TPU:6, one launch (start us, length us, event | category | flops | bytes accessed | tf_op | source)
XLA Modules:
  0.0 119.9 jit_solution(512915631045724069)
XLA Ops:
  6.5 0.7 all-gather.2.cloned.1.call-update
  7.3 2.5 %reshape.89 = bf16[8,128,1024]{2,1,0:T(8,128)(2,1)} broadcast(bf16[128,1024]{1,0:T(8,128)(2,1)} %bitcast.75), dimensions={1,2} | broadcast | bytes 2359296 | tf_op jit(solution)/shard_map/reshape | solution.py:105
  9.8 9.5 %all-to-all-start = ((bf16[8,128,1024]{2,1,0:T(8,128)(2,1)}), bf16[8,128,1024]{2,1,0:T(8,128)(2,1)S(1)}, u32[]{:S(2)}, u32[]{:S(2)}) async-start(bf16[8,128,1024]{2,1,0:T(8,128)(2,1)} %reshape.89), calls=%async_computation | async-start | bytes 4194304 | tf_op jit(solution)/shard_map/all_to_all | solution.py:104
  19.4 0.4 and_reduce_fusion
  19.8 17.8 %all_gather.6 = bf16[32,8320]{1,0:T(8,128)(2,1)S(1)} all-gather(bf16[16,8320]{1,0:T(8,128)(2,1)S(1)} %pad_maximum_fusion.1), channel_id=1, replica_groups=mesh['page'=32,'yh'=2,'xc'=8] {'yh'}, dimensions={0}, use_global_device_ids=true | all-gather | bytes 798720 | tf_op jit(solution)/shard_map/all_gather | solution.py:102
  37.7 0.1 copy.44
  37.8 1.1 copy.33
  39.0 0.1 broadcast_in_dim.5
  39.1 0.7 copy.49
  39.8 13.0 %all-to-all-done.v_ref = bf16[8,128,1024]{2,1,0:T(8,128)(2,1)S(1)} async-done(((bf16[8,128,1024]{2,1,0:T(8,128)(2,1)}), bf16[8,128,1024]{2,1,0:T(8,128)(2,1)S(1)}, u32[]{:S(2)}, u32[]{:S(2)}) %all-to-all-start) | async-done | bytes 2097184 | tf_op jit(solution)/shard_map/all_to_all | solution.py:104
  52.8 1.3 %copy-done = bf16[8,128,1024]{2,1,0:T(8,128)(2,1)} copy-done((bf16[8,128,1024]{2,1,0:T(8,128)(2,1)}, bf16[8,128,1024]{2,1,0:T(8,128)(2,1)S(1)}, u32[]{:S(2)}) %copy-start) | copy-done | bytes 2097176
  54.1 9.1 %shard_map.55 = (f32[8,256,128]{2,1,0:T(8,128)}, f32[8,256,128]{2,1,0:T(8,128)}) custom-call(bf16[8,256,128]{2,1,0:T(8,128)(2,1)} %bitcast.66, bf16[8,128,1024]{2,1,0:T(8,128)(2,1)} %all-gather.2.cloned.1.call-done.k_ref, bf16[8,128,1024]{2,1,0:T(8,128)(2,1)} %copy-done, f32[32,1024]{1,0:T(8,128)} %bitcast.73), custom_call_target="tpu_custom_call" | custom-call | flops 1073741824 | bytes 6815744 | tf_op jit(solution)/shard_map/pallas_call | solution.py:54
  63.2 1.4 %convert_element_type.49 = bf16[8,256,128]{2,1,0:T(8,128)(2,1)S(1)} convert(f32[8,256,128]{2,1,0:T(8,128)} %get-tuple-element.7) | non-fusion elementwise | flops 262144 | bytes 1572864 | tf_op jit(solution)/shard_map/convert_element_type | solution.py:131
  64.6 0.5 copy.34
  65.1 4.4 %copy.35 = f32[8,8,32,128]{2,1,0,3:T(8,128)} copy(f32[8,8,32,128]{3,2,1,0:T(8,128)S(1)} %bitcast.72) | data formatting | bytes 2097152 | tf_op jit(solution)/shard_map/reshape | solution.py:124
  69.5 2.7 %bitcast_convert_fusion = bf16[32,8,8,128]{0,2,1,3:T(8,128)(2,1)S(1)} fusion(f32[8,8,32,128]{2,1,0,3:T(8,128)} %copy.35), kind=kLoop, calls=%fused_computation.26 | loop fusion | flops 262144 | bytes 1572864 | tf_op jit(solution)/shard_map/convert.4
  72.2 0.8 slice.45
  73.0 0.1 squeeze.2
  73.2 0.6 copy.38
  73.8 0.3 reshape.95
  74.1 0.6 copy.39
  74.7 0.3 reshape.96
  75.2 0.6 copy.37
  75.9 0.3 reshape.94
  76.2 0.6 copy.36
  76.8 0.3 reshape.93
  77.2 0.1 copy.41
  77.3 34.3 %all_to_all.10 = bf16[64,33,128]{2,1,0:T(8,128)(2,1)S(1)} all-to-all(bf16[64,33,128]{2,1,0:T(8,128)(2,1)S(1)} %pad_maximum_fusion), channel_id=1, replica_groups=mesh['page'=32,'yh'=2,'xc'=8] {'page','yh'}, dimensions={0} | all-to-all | bytes 1081344 | tf_op jit(solution)/shard_map/all_to_all | solution.py:147
  111.6 0.1 fusion.7
  111.7 0.1 fusion.4
  111.9 0.3 multiply_reduce_fusion
  112.4 0.6 fusion.6
  (27 shorter events, 0.7 us)
Async XLA Ops:
  6.5 46.3 %all-gather.2.cloned.1.call-start = ((), (), s32[]{:S(2)}) async-start(), calls=%async_computation.2 | async-start | bytes 2359296 | tf_op jit(solution)/shard_map/all_gather | solution.py:103
  9.8 9.5 %copy-start.4 = (s32[16]{0:T(128)S(1)}, s32[16]{0:T(128)}, u32[]{:S(2)}) copy-start(s32[16]{0:T(128)} %param.9) | copy-start | bytes 196
  9.8 9.6 %copy-start.3 = (s32[16,32]{1,0:T(8,128)S(1)}, s32[16,32]{1,0:T(8,128)}, u32[]{:S(2)}) copy-start(s32[16,32]{1,0:T(8,128)} %param.8) | copy-start | bytes 6148
  9.8 10.0 %copy-start.2 = (bf16[16,8192]{1,0:T(8,128)(2,1)S(1)}, bf16[16,8192]{1,0:T(8,128)(2,1)}, u32[]{:S(2)}) copy-start(bf16[16,8192]{1,0:T(8,128)(2,1)} %param.5) | copy-start | bytes 786436
  9.8 43.0 %all-to-all-start = ((bf16[8,128,1024]{2,1,0:T(8,128)(2,1)}), bf16[8,128,1024]{2,1,0:T(8,128)(2,1)S(1)}, u32[]{:S(2)}, u32[]{:S(2)}) async-start(bf16[8,128,1024]{2,1,0:T(8,128)(2,1)} %reshape.89), calls=%async_computation | async-start | bytes 4194304 | tf_op jit(solution)/shard_map/all_to_all | solution.py:104
  52.8 1.3 %copy-start = (bf16[8,128,1024]{2,1,0:T(8,128)(2,1)}, bf16[8,128,1024]{2,1,0:T(8,128)(2,1)S(1)}, u32[]{:S(2)}) copy-start(bf16[8,128,1024]{2,1,0:T(8,128)(2,1)S(1)} %all-to-all-done.v_ref) | copy-start | bytes 6291460
  63.2 1.9 %copy-start.1 = (f32[8,256,128]{2,1,0:T(8,128)S(1)}, f32[8,256,128]{2,1,0:T(8,128)}, u32[]{:S(2)}) copy-start(f32[8,256,128]{2,1,0:T(8,128)} %get-tuple-element.8) | copy-start | bytes 3145732
Sparse Core Ops, SparseCore 0:
  9.5 40.3 all-gather.1

commit v6 on v5

--- a/solution.py
+++ b/solution.py
@@ -1,3 +1,4 @@
+import functools
 import math
 
 import jax
@@ -12,6 +13,7 @@
 KVH = 8
 HD = 128
 LANES = 128
+STAT_ROWS = 8
 
 
 def split_pair(value):
@@ -20,7 +22,7 @@
     return high, low
 
 
-def attend_kernel(q_ref, k_ref, v_ref, hit_ref, out_ref, stat_ref):
+def attend_kernel(rows, own_heads, q_ref, k_ref, v_ref, hit_ref, out_ref, stat_ref):
     pages, page_len, _ = k_ref.shape
     q = q_ref[0]
     keys = k_ref[...].reshape(pages * page_len, HD)
@@ -30,6 +32,7 @@
     ) * (1.0 / math.sqrt(HD))
     req_rows = hit_ref.shape[0]
     groups = q.shape[0] // req_rows
+    halves = req_rows // rows
     hit = jnp.concatenate([hit_ref[...]] * groups, axis=0) > 0.5
     scores = jnp.where(hit, scores, jnp.float32(-1e30))
     top = jnp.max(scores, axis=1, keepdims=True)
@@ -38,21 +41,32 @@
     shift = high + low
     terms = jnp.where(hit, jnp.exp(scores - shift), jnp.float32(0.0))
     total = jnp.sum(terms, axis=1, keepdims=True)
-    out_ref[0] = jnp.dot(
+    mixed = jnp.dot(
         terms.astype(jnp.bfloat16), values, preferred_element_type=jnp.float32
-    )
+    ).astype(jnp.bfloat16)
+    for g in range(groups):
+        for y in range(halves):
+            first = g * req_rows + y * rows
+            block = (g // own_heads) * halves + y
+            row = (g % own_heads) * rows
+            out_ref[block, row : row + rows, :] = mixed[first : first + rows, :]
     lane = lax.broadcasted_iota(jnp.int32, (q.shape[0], LANES), 1)
-    stat_ref[0] = jnp.where(
+    stat_tile = jnp.where(
         lane == 0, high, jnp.where(lane == 1, low, jnp.where(lane == 2, total, 0.0))
     )
+    stat_ref[0] = jnp.transpose(stat_tile)[: stat_ref.shape[1], :]
 
 
-def attend(grouped_q, keys, values, token_hit):
+def attend(grouped_q, keys, values, token_hit, rows, own_heads):
     kv_heads, q_rows, _ = grouped_q.shape
     pages, page_len, _ = keys.shape
     tokens = pages * page_len
+    req_rows = token_hit.shape[0]
+    groups = q_rows // req_rows
+    per_head_blocks = groups // own_heads * (req_rows // rows)
+    block_rows = own_heads * rows
     return pl.pallas_call(
-        attend_kernel,
+        functools.partial(attend_kernel, rows, own_heads),
         grid=(kv_heads,),
         in_specs=[
             pl.BlockSpec((1, q_rows, HD), lambda k: (k, 0, 0)),
@@ -61,20 +75,19 @@
             pl.BlockSpec(token_hit.shape, lambda k: (0, 0)),
         ],
         out_specs=[
-            pl.BlockSpec((1, q_rows, HD), lambda k: (k, 0, 0)),
-            pl.BlockSpec((1, q_rows, LANES), lambda k: (k, 0, 0)),
+            pl.BlockSpec((per_head_blocks, block_rows, HD), lambda k: (k, 0, 0)),
+            pl.BlockSpec((1, STAT_ROWS, q_rows), lambda k: (k, 0, 0)),
         ],
         out_shape=[
-            jax.ShapeDtypeStruct((kv_heads, q_rows, HD), jnp.float32),
-            jax.ShapeDtypeStruct((kv_heads, q_rows, LANES), jnp.float32),
+            jax.ShapeDtypeStruct((kv_heads * per_head_blocks, block_rows, HD), jnp.bfloat16),
+            jax.ShapeDtypeStruct((kv_heads, STAT_ROWS, q_rows), jnp.float32),
         ],
         cost_estimate=pl.CostEstimate(
             flops=4 * kv_heads * q_rows * tokens * HD,
             transcendentals=kv_heads * q_rows * tokens,
-            bytes_accessed=2 * (grouped_q.size + keys.size + values.size) + 4 * 2 * kv_heads * q_rows * HD,
+            bytes_accessed=2 * (grouped_q.size + keys.size + values.size) + 6 * kv_heads * q_rows * HD,
         ),
     )(grouped_q, keys, values, token_hit)
-
 
 def body(queries, key_pool, value_pool, page_table, page_count):
     n_page = lax.axis_size("page")
@@ -119,30 +132,20 @@
 
     grouped = all_q.reshape(req_rows, KVH, per_kv, HD).transpose(1, 2, 0, 3)
     grouped = grouped.reshape(KVH, per_kv * req_rows, HD)
-    out_k, stat_k = attend(grouped, keys, values, token_hit)
-    local_out = out_k.reshape(KVH, per_kv, req_rows, HD).transpose(2, 0, 1, 3)
-    stat_k = stat_k.reshape(KVH, per_kv, req_rows, LANES).transpose(2, 0, 1, 3)
-    max_hi = stat_k[..., 0]
-    max_lo = stat_k[..., 1]
-    local_sum = stat_k[..., 2]
-
     n_blocks = n_page * n_yh
     block_rows = rows * own_heads
-    out_blocks = local_out.astype(jnp.bfloat16)
-    out_blocks = out_blocks.reshape(n_yh, rows, n_page, own_heads, HD).transpose(2, 0, 1, 3, 4)
-    out_blocks = out_blocks.reshape(n_blocks, block_rows, HD)
-    sum_hi, sum_lo = split_pair(local_sum)
-
-    def to_blocks(stat):
-        stat = stat.astype(jnp.bfloat16).reshape(n_yh, rows, n_page, own_heads).transpose(2, 0, 1, 3)
-        return stat.reshape(n_blocks, block_rows)
-
+    out_blocks, stat_k = attend(grouped, keys, values, token_hit, rows, own_heads)
+    stat_k = stat_k[:, :3, :].reshape(KVH, 3, per_kv // own_heads, own_heads, n_yh, rows)
+    stat_k = stat_k.transpose(1, 0, 2, 4, 3, 5).reshape(3, n_blocks, block_rows)
+    max_hi = stat_k[0]
+    max_lo = stat_k[1]
+    sum_hi, sum_lo = split_pair(stat_k[2])
     stat_cols = -(-4 * block_rows // HD) * HD
     stats = jnp.concatenate(
-        [to_blocks(max_hi), to_blocks(max_lo), to_blocks(sum_hi), to_blocks(sum_lo)]
-        + [jnp.zeros((n_blocks, stat_cols - 4 * block_rows), jnp.bfloat16)],
+        [max_hi, max_lo, sum_hi, sum_lo]
+        + [jnp.zeros((n_blocks, stat_cols - 4 * block_rows), jnp.float32)],
         axis=1,
-    )
+    ).astype(jnp.bfloat16)
     payload = jnp.concatenate([out_blocks, stats.reshape(n_blocks, -1, HD)], axis=1)
     arrived = lax.all_to_all(payload, ("page", "yh"), 0, 0, tiled=True)
 
@@ -154,7 +157,7 @@
     factor = jnp.exp(part_max - joint_max[None, :])
     joint_sum = jnp.sum(part_sum * factor, axis=0)
     joint_out = jnp.sum(part_out * factor[..., None], axis=0)
-    result = joint_out / joint_sum[:, None]
+    result = (joint_out / joint_sum[:, None]).reshape(own_heads, rows, HD).transpose(1, 0, 2)
     return result.reshape(rows, own_heads * HD).astype(jnp.bfloat16)
 
 

time: 122 us -> 109 us (0.89)
  local copies, waits for them, and re-layouts: 15.9 us -> 7.88 us
  other arithmetic: 6 us -> 2.14 us
    reshape x6 -> x1, local copies, waits for them, and re-layouts: 5.84 us -> 0.3 us  [body(): stat_k[:, :3, :].reshape(KVH, 3, per_kv // own_heads, own_heads, n_yh, rows)]
    transpose x5 -> x0, local copies, waits for them, and re-layouts: 3 us -> none  [the longest x4 2.47 us: to_blocks(): stat.astype(jnp.bfloat16).reshape(n_yh, rows, n_page, own_heads)]
    another operation x1, other arithmetic: 2.69 us -> 0.07 us
    convert_element_type x1 -> x0, other arithmetic: 1.39 us -> none  [body(): out_blocks = local_out.astype(jnp.bfloat16)]
  transfers between devices with their start and end apart: 2 -> 2, of which waited for: 1 -> 1; matrix products, arithmetic and copies ran while one was open for 4% -> 5% of each run, Pallas kernels for 0% -> 0%
where the time goes in v6:
time: 109 us; the launch traced here: 108 us
  blocking collectives  52.1 us (48%)
  waiting for transfers between devices  13.7 us (13%)
  between operations  13.5 us (12%)
  starting transfers between devices  9.49 us (9%)
  Pallas kernels  9 us (8%)
  local copies, waits for them, and re-layouts  7.88 us (7%)
  other arithmetic  2.14 us (2%)
    all_to_all x1, blocking collectives, body(): arrived = lax.all_to_all(payload, ('page', 'yh'), 0, 0, tiled=True)  34.3 us
    all_gather x1, blocking collectives, body(): all_packed = lax.all_gather(packed, 'yh', tiled=True)  17.8 us
    all_to_all x1, waiting for transfers between devices, body(): lax.all_to_all(jnp.broadcast_to(value_pool[None], (n_xc,) + value_pool.sh...  13 us
    all_to_all x1, starting transfers between devices, body(): lax.all_to_all(jnp.broadcast_to(value_pool[None], (n_xc,) + value_pool.sh...  9.49 us
    pallas_call x1, Pallas kernels, attend(): pl.pallas_call(functools.partial(attend_kernel, rows, own_heads), grid=(k...  9 us
    reshape x1, local copies, waits for them, and re-layouts, body(): jnp.broadcast_to(value_pool[None], (n_xc,) + value_pool.shape)  2.52 us
  transfers between devices with their start and end apart: 2, of which 1 were waited for; matrix products, arithmetic and copies ran while one was open for 5% of the time, Pallas kernels for 0%

profile of v6, /device:TPU:6, one launch (start us, length us, event | category | flops | bytes accessed | tf_op | source)
XLA Modules:
  0.0 107.9 jit_solution(10401068387288173401)
XLA Ops:
  6.5 0.0 all-gather.2.cloned.1.call-start
  6.5 0.7 all-gather.2.cloned.1.call-update
  7.3 2.5 %reshape.129 = bf16[8,128,1024]{2,1,0:T(8,128)(2,1)} broadcast(bf16[128,1024]{1,0:T(8,128)(2,1)} %bitcast.35), dimensions={1,2} | broadcast | bytes 2359296 | tf_op jit(solution)/shard_map/reshape | solution.py:118
  9.8 9.5 %all-to-all-start = ((bf16[8,128,1024]{2,1,0:T(8,128)(2,1)}), bf16[8,128,1024]{2,1,0:T(8,128)(2,1)S(1)}, u32[]{:S(2)}, u32[]{:S(2)}) async-start(bf16[8,128,1024]{2,1,0:T(8,128)(2,1)} %reshape.129), calls=%async_computation | async-start | bytes 4194304 | tf_op jit(solution)/shard_map/all_to_all | solution.py:117
  19.3 0.0 copy-done.4
  19.3 0.1 iota_compare_fusion
  19.4 0.4 and_reduce_fusion
  19.8 17.8 %all_gather.6 = bf16[32,8320]{1,0:T(8,128)(2,1)S(1)} all-gather(bf16[16,8320]{1,0:T(8,128)(2,1)S(1)} %pad_maximum_fusion), channel_id=1, replica_groups=mesh['page'=32,'yh'=2,'xc'=8] {'yh'}, dimensions={0}, use_global_device_ids=true | all-gather | bytes 798720 | tf_op jit(solution)/shard_map/all_gather | solution.py:115
  37.6 0.1 compare_convert_fusion
  37.7 0.1 broadcast_in_dim.5
  37.8 0.7 copy.74
  38.5 0.1 copy.70
  38.6 1.1 %copy.57 = bf16[32,8,8,128]{3,0,2,1:T(8,128)(2,1)} copy(bf16[32,8,8,128]{3,2,1,0:T(8,128)(2,1)S(1)} %bitcast.29) | data formatting | bytes 1048576 | tf_op jit(solution)/shard_map/reshape | solution.py:133
  39.8 13.0 %all-to-all-done.v_ref = bf16[8,128,1024]{2,1,0:T(8,128)(2,1)S(1)} async-done(((bf16[8,128,1024]{2,1,0:T(8,128)(2,1)}), bf16[8,128,1024]{2,1,0:T(8,128)(2,1)S(1)}, u32[]{:S(2)}, u32[]{:S(2)}) %all-to-all-start) | async-done | bytes 2097184 | tf_op jit(solution)/shard_map/all_to_all | solution.py:117
  52.8 1.3 %copy-done = bf16[8,128,1024]{2,1,0:T(8,128)(2,1)} copy-done((bf16[8,128,1024]{2,1,0:T(8,128)(2,1)}, bf16[8,128,1024]{2,1,0:T(8,128)(2,1)S(1)}, u32[]{:S(2)}) %copy-start) | copy-done | bytes 2097176
  54.1 9.0 %shard_map.55 = (bf16[64,32,128]{2,1,0:T(8,128)(2,1)}, f32[8,8,256]{2,1,0:T(8,128)}) custom-call(bf16[8,256,128]{2,1,0:T(8,128)(2,1)} %bitcast.28, bf16[8,128,1024]{2,1,0:T(8,128)(2,1)} %all-gather.2.cloned.1.call-done.k_ref, bf16[8,128,1024]{2,1,0:T(8,128)(2,1)} %copy-done, f32[32,1024]{1,0:T(8,128)} %bitcast.33), custom_call_target="tpu_custom_call" | custom-call | flops 1073741824 | bytes 6291456 | tf_op jit(solution)/shard_map/pallas_call | solution.py:68
  63.1 0.9 slice.39
  64.0 0.3 reshape.130
  64.3 0.1 bitcast_convert_fusion
  64.5 0.1 concatenate.32
  64.6 0.1 concatenate.33
  64.8 0.1 squeeze.2
  64.9 0.1 copy.62
  64.9 0.1 copy.66
  65.0 0.1 copy.67
  65.2 0.2 maximum_maximum_fusion
  65.4 34.3 %all_to_all.10 = bf16[64,33,128]{2,1,0:T(8,128)(2,1)S(1)} all-to-all(bf16[64,33,128]{2,1,0:T(8,128)(2,1)S(1)} %maximum_maximum_fusion), channel_id=1, replica_groups=mesh['page'=32,'yh'=2,'xc'=8] {'page','yh'}, dimensions={0} | all-to-all | bytes 1081344 | tf_op jit(solution)/shard_map/all_to_all | solution.py:150
  99.7 0.1 fusion.4
  99.8 0.1 fusion.1
  99.9 0.1 div.11
  100.0 0.3 multiply_reduce_fusion
  100.3 0.7 copy_bitcast_fusion.1
  (21 shorter events, 0.2 us)
Async XLA Ops:
  6.5 46.3 %all-gather.2.cloned.1.call-start = ((), (), s32[]{:S(2)}) async-start(), calls=%async_computation.2 | async-start | bytes 2359296 | tf_op jit(solution)/shard_map/all_gather | solution.py:116
  9.8 9.5 %copy-start.4 = (s32[16]{0:T(128)S(1)}, s32[16]{0:T(128)}, u32[]{:S(2)}) copy-start(s32[16]{0:T(128)} %param.9) | copy-start | bytes 196
  9.8 9.6 %copy-start.3 = (s32[16,32]{1,0:T(8,128)S(1)}, s32[16,32]{1,0:T(8,128)}, u32[]{:S(2)}) copy-start(s32[16,32]{1,0:T(8,128)} %param.8) | copy-start | bytes 6148
  9.8 10.0 %copy-start.2 = (bf16[16,8192]{1,0:T(8,128)(2,1)S(1)}, bf16[16,8192]{1,0:T(8,128)(2,1)}, u32[]{:S(2)}) copy-start(bf16[16,8192]{1,0:T(8,128)(2,1)} %param.5) | copy-start | bytes 786436
  9.8 43.0 %all-to-all-start = ((bf16[8,128,1024]{2,1,0:T(8,128)(2,1)}), bf16[8,128,1024]{2,1,0:T(8,128)(2,1)S(1)}, u32[]{:S(2)}, u32[]{:S(2)}) async-start(bf16[8,128,1024]{2,1,0:T(8,128)(2,1)} %reshape.129), calls=%async_computation | async-start | bytes 4194304 | tf_op jit(solution)/shard_map/all_to_all | solution.py:117
  52.8 1.3 %copy-start = (bf16[8,128,1024]{2,1,0:T(8,128)(2,1)}, bf16[8,128,1024]{2,1,0:T(8,128)(2,1)S(1)}, u32[]{:S(2)}) copy-start(bf16[8,128,1024]{2,1,0:T(8,128)(2,1)S(1)} %all-to-all-done.v_ref) | copy-start | bytes 6291460
  63.1 2.1 %copy-start.1 = (bf16[64,32,128]{2,1,0:T(8,128)(2,1)S(1)}, bf16[64,32,128]{2,1,0:T(8,128)(2,1)}, u32[]{:S(2)}) copy-start(bf16[64,32,128]{2,1,0:T(8,128)(2,1)} %get-tuple-element.7) | copy-start | bytes 1572868
Sparse Core Ops, SparseCore 0:
  9.5 40.3 all-gather.1

commit v7 on v6

--- a/solution.py
+++ b/solution.py
@@ -146,11 +146,11 @@
         + [jnp.zeros((n_blocks, stat_cols - 4 * block_rows), jnp.float32)],
         axis=1,
     ).astype(jnp.bfloat16)
-    payload = jnp.concatenate([out_blocks, stats.reshape(n_blocks, -1, HD)], axis=1)
+    payload = jnp.concatenate([out_blocks.reshape(n_blocks, block_rows * HD), stats], axis=1)
     arrived = lax.all_to_all(payload, ("page", "yh"), 0, 0, tiled=True)
 
-    part_out = arrived[:, :block_rows, :].astype(jnp.float32)
-    part_stats = arrived[:, block_rows:, :].reshape(n_blocks, stat_cols).astype(jnp.float32)
+    part_out = arrived[:, : block_rows * HD].reshape(n_blocks, block_rows, HD).astype(jnp.float32)
+    part_stats = arrived[:, block_rows * HD :].astype(jnp.float32)
     part_max = part_stats[:, :block_rows] + part_stats[:, block_rows : 2 * block_rows]
     part_sum = part_stats[:, 2 * block_rows : 3 * block_rows] + part_stats[:, 3 * block_rows : 4 * block_rows]
     joint_max = jnp.max(part_max, axis=0)

time: 109 us -> 112 us (1.028)
  local copies, waits for them, and re-layouts: 7.88 us -> 10.9 us
  blocking collectives: 52.1 us -> 50 us
  other arithmetic: 2.14 us -> 3.34 us
    unnamed x13 -> x15, local copies, waits for them, and re-layouts: 2.15 us -> 4.41 us
    all_to_all x1, blocking collectives: 34.3 us -> 32.2 us  [body(): arrived = lax.all_to_all(payload, ('page', 'yh'), 0, 0, tiled=True)]
where the time goes in v7:
time: 112 us; the launch traced here: 110 us
  blocking collectives  50 us (45%)
  waiting for transfers between devices  13.7 us (12%)
  between operations  13.6 us (12%)
  local copies, waits for them, and re-layouts  10.9 us (10%)
  starting transfers between devices  9.49 us (8%)
  Pallas kernels  9 us (8%)
  other arithmetic  3.34 us (3%)
    all_to_all x1, blocking collectives, body(): arrived = lax.all_to_all(payload, ('page', 'yh'), 0, 0, tiled=True)  32.2 us
    all_gather x1, blocking collectives, body(): all_packed = lax.all_gather(packed, 'yh', tiled=True)  17.8 us
    all_to_all x1, waiting for transfers between devices, body(): lax.all_to_all(jnp.broadcast_to(value_pool[None], (n_xc,) + value_pool.sh...  13 us
    all_to_all x1, starting transfers between devices, body(): lax.all_to_all(jnp.broadcast_to(value_pool[None], (n_xc,) + value_pool.sh...  9.49 us
    pallas_call x1, Pallas kernels, attend(): pl.pallas_call(functools.partial(attend_kernel, rows, own_heads), grid=(k...  9 us
    unnamed x15, local copies, waits for them, and re-layouts  4.41 us
    reshape x1, local copies, waits for them, and re-layouts, body(): jnp.broadcast_to(value_pool[None], (n_xc,) + value_pool.shape)  2.51 us
  transfers between devices with their start and end apart: 2, of which 1 were waited for; matrix products, arithmetic and copies ran while one was open for 5% of the time, Pallas kernels for 0%

profile of v7, /device:TPU:6, one launch (start us, length us, event | category | flops | bytes accessed | tf_op | source)
XLA Modules:
  0.0 110.0 jit_solution(1904675083678089348)
XLA Ops:
  6.5 0.7 all-gather.2.cloned.1.call-update
  7.3 2.5 %reshape.73 = bf16[8,128,1024]{2,1,0:T(8,128)(2,1)} broadcast(bf16[128,1024]{1,0:T(8,128)(2,1)} %bitcast.47), dimensions={1,2} | broadcast | bytes 2359296 | tf_op jit(solution)/shard_map/reshape | solution.py:118
  9.8 9.5 %all-to-all-start = ((bf16[8,128,1024]{2,1,0:T(8,128)(2,1)}), bf16[8,128,1024]{2,1,0:T(8,128)(2,1)S(1)}, u32[]{:S(2)}, u32[]{:S(2)}) async-start(bf16[8,128,1024]{2,1,0:T(8,128)(2,1)} %reshape.73), calls=%async_computation | async-start | bytes 4194304 | tf_op jit(solution)/shard_map/all_to_all | solution.py:117
  19.3 0.1 iota_compare_fusion
  19.4 0.4 and_reduce_fusion
  19.8 17.8 %all_gather.6 = bf16[32,8320]{1,0:T(8,128)(2,1)S(1)} all-gather(bf16[16,8320]{1,0:T(8,128)(2,1)S(1)} %pad_maximum_fusion), channel_id=1, replica_groups=mesh['page'=32,'yh'=2,'xc'=8] {'yh'}, dimensions={0}, use_global_device_ids=true | all-gather | bytes 798720 | tf_op jit(solution)/shard_map/all_gather | solution.py:115
  37.6 0.1 compare_convert_fusion
  37.7 0.1 broadcast_in_dim.5
  37.8 0.7 copy.52
  38.5 0.1 copy.41
  38.6 1.1 %copy.32 = bf16[32,8,8,128]{3,0,2,1:T(8,128)(2,1)} copy(bf16[32,8,8,128]{3,2,1,0:T(8,128)(2,1)S(1)} %bitcast.42) | data formatting | bytes 1048576 | tf_op jit(solution)/shard_map/reshape | solution.py:133
  39.8 13.0 %all-to-all-done.v_ref = bf16[8,128,1024]{2,1,0:T(8,128)(2,1)S(1)} async-done(((bf16[8,128,1024]{2,1,0:T(8,128)(2,1)}), bf16[8,128,1024]{2,1,0:T(8,128)(2,1)S(1)}, u32[]{:S(2)}, u32[]{:S(2)}) %all-to-all-start) | async-done | bytes 2097184 | tf_op jit(solution)/shard_map/all_to_all | solution.py:117
  52.8 1.3 %copy-done = bf16[8,128,1024]{2,1,0:T(8,128)(2,1)} copy-done((bf16[8,128,1024]{2,1,0:T(8,128)(2,1)}, bf16[8,128,1024]{2,1,0:T(8,128)(2,1)S(1)}, u32[]{:S(2)}) %copy-start) | copy-done | bytes 2097176
  54.1 9.0 %shard_map.55 = (bf16[64,32,128]{2,1,0:T(8,128)(2,1)}, f32[8,8,256]{2,1,0:T(8,128)}) custom-call(bf16[8,256,128]{2,1,0:T(8,128)(2,1)} %bitcast.40, bf16[8,128,1024]{2,1,0:T(8,128)(2,1)} %all-gather.2.cloned.1.call-done.k_ref, bf16[8,128,1024]{2,1,0:T(8,128)(2,1)} %copy-done, f32[32,1024]{1,0:T(8,128)} %bitcast.44), custom_call_target="tpu_custom_call" | custom-call | flops 1073741824 | bytes 6291456 | tf_op jit(solution)/shard_map/pallas_call | solution.py:68
  63.1 0.8 slice.39
  63.9 0.3 reshape.75
  64.4 0.1 squeeze.11
  64.5 0.1 squeeze.12
  64.7 0.1 squeeze.13
  64.8 1.3 %copy.51 = bf16[8,8,32,128]{3,1,2,0:T(8,128)(2,1)S(1)} copy(bf16[8,8,32,128]{3,2,1,0:T(8,128)(2,1)} %bitcast.45) | data formatting | bytes 1048576
  66.0 0.3 concatenate.10
  66.3 0.5 broadcast.29
  66.8 1.0 reduce.1
  67.8 0.4 reshape.76
  68.2 32.2 %all_to_all.17 = bf16[64,2,2112]{2,1,0:T(2,128)(2,1)S(1)} all-to-all(bf16[64,2,2112]{2,1,0:T(2,128)(2,1)S(1)} %reshape.76), channel_id=1, replica_groups=mesh['page'=32,'yh'=2,'xc'=8] {'page','yh'}, dimensions={0} | all-to-all | bytes 1081344 | tf_op jit(solution)/shard_map/all_to_all | solution.py:150
  100.4 0.6 reshape.77
  101.1 0.1 fusion.5
  101.2 0.1 fusion.4
  101.3 0.3 mul.22
  101.6 0.8 fusion
  102.4 0.1 div.11
  102.5 0.7 copy_bitcast_fusion.3
  (23 shorter events, 0.4 us)
Async XLA Ops:
  6.5 46.2 %all-gather.2.cloned.1.call-start = ((), (), s32[]{:S(2)}) async-start(), calls=%async_computation.2 | async-start | bytes 2359296 | tf_op jit(solution)/shard_map/all_gather | solution.py:116
  9.8 9.5 %copy-start.3 = (s32[16]{0:T(128)S(1)}, s32[16]{0:T(128)}, u32[]{:S(2)}) copy-start(s32[16]{0:T(128)} %param.9) | copy-start | bytes 196
  9.8 9.6 %copy-start.2 = (s32[16,32]{1,0:T(8,128)S(1)}, s32[16,32]{1,0:T(8,128)}, u32[]{:S(2)}) copy-start(s32[16,32]{1,0:T(8,128)} %param.8) | copy-start | bytes 6148
  9.8 10.0 %copy-start.1 = (bf16[16,8192]{1,0:T(8,128)(2,1)S(1)}, bf16[16,8192]{1,0:T(8,128)(2,1)}, u32[]{:S(2)}) copy-start(bf16[16,8192]{1,0:T(8,128)(2,1)} %param.5) | copy-start | bytes 786436
  9.8 43.0 %all-to-all-start = ((bf16[8,128,1024]{2,1,0:T(8,128)(2,1)}), bf16[8,128,1024]{2,1,0:T(8,128)(2,1)S(1)}, u32[]{:S(2)}, u32[]{:S(2)}) async-start(bf16[8,128,1024]{2,1,0:T(8,128)(2,1)} %reshape.73), calls=%async_computation | async-start | bytes 4194304 | tf_op jit(solution)/shard_map/all_to_all | solution.py:117
  52.8 1.3 %copy-start = (bf16[8,128,1024]{2,1,0:T(8,128)(2,1)}, bf16[8,128,1024]{2,1,0:T(8,128)(2,1)S(1)}, u32[]{:S(2)}) copy-start(bf16[8,128,1024]{2,1,0:T(8,128)(2,1)S(1)} %all-to-all-done.v_ref) | copy-start | bytes 6291460
Sparse Core Ops, SparseCore 0:
  9.5 40.3 all-gather.1

commit v8 on v6

--- a/solution.py
+++ b/solution.py
@@ -33,13 +33,12 @@
     req_rows = hit_ref.shape[0]
     groups = q.shape[0] // req_rows
     halves = req_rows // rows
-    hit = jnp.concatenate([hit_ref[...]] * groups, axis=0) > 0.5
-    scores = jnp.where(hit, scores, jnp.float32(-1e30))
+    scores = (scores.reshape(groups, req_rows, -1) + hit_ref[...][None]).reshape(q.shape[0], -1)
     top = jnp.max(scores, axis=1, keepdims=True)
     high = top.astype(jnp.bfloat16).astype(jnp.float32)
     low = (top - high).astype(jnp.bfloat16).astype(jnp.float32)
     shift = high + low
-    terms = jnp.where(hit, jnp.exp(scores - shift), jnp.float32(0.0))
+    terms = jnp.exp(jnp.minimum(scores - shift, 1.0))
     total = jnp.sum(terms, axis=1, keepdims=True)
     mixed = jnp.dot(
         terms.astype(jnp.bfloat16), values, preferred_element_type=jnp.float32
@@ -128,7 +127,7 @@
     all_q = all_packed[:, : H * HD]
     held = n_xc * pages_held
     page_hit = lax.dynamic_slice_in_dim(all_packed, H * HD + yh_index * held, held, 1) > 0.5
-    token_hit = jnp.repeat(page_hit, page_len, axis=1).astype(jnp.float32)
+    token_hit = jnp.where(jnp.repeat(page_hit, page_len, axis=1), jnp.float32(0.0), jnp.float32(-1e30))
 
     grouped = all_q.reshape(req_rows, KVH, per_kv, HD).transpose(1, 2, 0, 3)
     grouped = grouped.reshape(KVH, per_kv * req_rows, HD)

time: 109 us -> 109 us (level)
  no operation moved by 1% of the time
where the time goes in v8:
time: 109 us; the launch traced here: 108 us
  blocking collectives  52.1 us (48%)
  waiting for transfers between devices  13.7 us (13%)
  between operations  13.5 us (12%)
  starting transfers between devices  9.49 us (9%)
  Pallas kernels  8.87 us (8%)
  local copies, waits for them, and re-layouts  7.88 us (7%)
  other arithmetic  2.14 us (2%)
    all_to_all x1, blocking collectives, body(): arrived = lax.all_to_all(payload, ('page', 'yh'), 0, 0, tiled=True)  34.3 us
    all_gather x1, blocking collectives, body(): all_packed = lax.all_gather(packed, 'yh', tiled=True)  17.8 us
    all_to_all x1, waiting for transfers between devices, body(): lax.all_to_all(jnp.broadcast_to(value_pool[None], (n_xc,) + value_pool.sh...  13 us
    all_to_all x1, starting transfers between devices, body(): lax.all_to_all(jnp.broadcast_to(value_pool[None], (n_xc,) + value_pool.sh...  9.49 us
    pallas_call x1, Pallas kernels, attend(): pl.pallas_call(functools.partial(attend_kernel, rows, own_heads), grid=(k...  8.87 us
    reshape x1, local copies, waits for them, and re-layouts, body(): jnp.broadcast_to(value_pool[None], (n_xc,) + value_pool.shape)  2.52 us
  transfers between devices with their start and end apart: 2, of which 1 were waited for; matrix products, arithmetic and copies ran while one was open for 5% of the time, Pallas kernels for 0%

profile of v8, /device:TPU:6, one launch (start us, length us, event | category | flops | bytes accessed | tf_op | source)
XLA Modules:
  0.0 107.7 jit_solution(16181591819784947751)
XLA Ops:
  6.5 0.0 all-gather.2.cloned.1.call-start
  6.5 0.7 all-gather.2.cloned.1.call-update
  7.3 2.5 %reshape.131 = bf16[8,128,1024]{2,1,0:T(8,128)(2,1)} broadcast(bf16[128,1024]{1,0:T(8,128)(2,1)} %bitcast.35), dimensions={1,2} | broadcast | bytes 2359296 | tf_op jit(solution)/shard_map/reshape | solution.py:117
  9.8 9.5 %all-to-all-start = ((bf16[8,128,1024]{2,1,0:T(8,128)(2,1)}), bf16[8,128,1024]{2,1,0:T(8,128)(2,1)S(1)}, u32[]{:S(2)}, u32[]{:S(2)}) async-start(bf16[8,128,1024]{2,1,0:T(8,128)(2,1)} %reshape.131), calls=%async_computation | async-start | bytes 4194304 | tf_op jit(solution)/shard_map/all_to_all | solution.py:116
  19.3 0.0 copy-done.4
  19.3 0.1 iota_compare_fusion
  19.4 0.4 and_reduce_fusion
  19.8 17.8 %all_gather.6 = bf16[32,8320]{1,0:T(8,128)(2,1)S(1)} all-gather(bf16[16,8320]{1,0:T(8,128)(2,1)S(1)} %pad_maximum_fusion), channel_id=1, replica_groups=mesh['page'=32,'yh'=2,'xc'=8] {'yh'}, dimensions={0}, use_global_device_ids=true | all-gather | bytes 798720 | tf_op jit(solution)/shard_map/all_gather | solution.py:114
  37.6 0.1 compare_select_fusion
  37.7 0.1 broadcast_in_dim.15
  37.8 0.7 copy.74
  38.5 0.1 copy.70
  38.6 1.1 %copy.57 = bf16[32,8,8,128]{3,0,2,1:T(8,128)(2,1)} copy(bf16[32,8,8,128]{3,2,1,0:T(8,128)(2,1)S(1)} %bitcast.29) | data formatting | bytes 1048576 | tf_op jit(solution)/shard_map/reshape | solution.py:132
  39.8 13.0 %all-to-all-done.v_ref = bf16[8,128,1024]{2,1,0:T(8,128)(2,1)S(1)} async-done(((bf16[8,128,1024]{2,1,0:T(8,128)(2,1)}), bf16[8,128,1024]{2,1,0:T(8,128)(2,1)S(1)}, u32[]{:S(2)}, u32[]{:S(2)}) %all-to-all-start) | async-done | bytes 2097184 | tf_op jit(solution)/shard_map/all_to_all | solution.py:116
  52.8 1.3 %copy-done = bf16[8,128,1024]{2,1,0:T(8,128)(2,1)} copy-done((bf16[8,128,1024]{2,1,0:T(8,128)(2,1)}, bf16[8,128,1024]{2,1,0:T(8,128)(2,1)S(1)}, u32[]{:S(2)}) %copy-start) | copy-done | bytes 2097176
  54.1 8.9 %shard_map.55 = (bf16[64,32,128]{2,1,0:T(8,128)(2,1)}, f32[8,8,256]{2,1,0:T(8,128)}) custom-call(bf16[8,256,128]{2,1,0:T(8,128)(2,1)} %bitcast.28, bf16[8,128,1024]{2,1,0:T(8,128)(2,1)} %all-gather.2.cloned.1.call-done.k_ref, bf16[8,128,1024]{2,1,0:T(8,128)(2,1)} %copy-done, f32[32,1024]{1,0:T(8,128)} %bitcast.33), custom_call_target="tpu_custom_call" | custom-call | flops 1073741824 | bytes 6291456 | tf_op jit(solution)/shard_map/pallas_call | solution.py:67
  63.0 0.9 slice.39
  63.9 0.3 reshape.132
  64.2 0.1 bitcast_convert_fusion
  64.4 0.1 concatenate.32
  64.5 0.1 concatenate.33
  64.6 0.1 squeeze.2
  64.7 0.1 copy.62
  64.8 0.1 copy.66
  64.9 0.1 copy.67
  65.0 0.2 maximum_maximum_fusion
  65.3 34.3 %all_to_all.10 = bf16[64,33,128]{2,1,0:T(8,128)(2,1)S(1)} all-to-all(bf16[64,33,128]{2,1,0:T(8,128)(2,1)S(1)} %maximum_maximum_fusion), channel_id=1, replica_groups=mesh['page'=32,'yh'=2,'xc'=8] {'page','yh'}, dimensions={0} | all-to-all | bytes 1081344 | tf_op jit(solution)/shard_map/all_to_all | solution.py:149
  99.6 0.1 fusion.4
  99.7 0.1 fusion.1
  99.8 0.1 div.11
  99.9 0.3 multiply_reduce_fusion
  100.2 0.7 copy_bitcast_fusion.1
  (21 shorter events, 0.2 us)
Async XLA Ops:
  6.5 46.3 %all-gather.2.cloned.1.call-start = ((), (), s32[]{:S(2)}) async-start(), calls=%async_computation.2 | async-start | bytes 2359296 | tf_op jit(solution)/shard_map/all_gather | solution.py:115
  9.8 9.5 %copy-start.4 = (s32[16]{0:T(128)S(1)}, s32[16]{0:T(128)}, u32[]{:S(2)}) copy-start(s32[16]{0:T(128)} %param.9) | copy-start | bytes 196
  9.8 9.6 %copy-start.3 = (s32[16,32]{1,0:T(8,128)S(1)}, s32[16,32]{1,0:T(8,128)}, u32[]{:S(2)}) copy-start(s32[16,32]{1,0:T(8,128)} %param.8) | copy-start | bytes 6148
  9.8 10.0 %copy-start.2 = (bf16[16,8192]{1,0:T(8,128)(2,1)S(1)}, bf16[16,8192]{1,0:T(8,128)(2,1)}, u32[]{:S(2)}) copy-start(bf16[16,8192]{1,0:T(8,128)(2,1)} %param.5) | copy-start | bytes 786436
  9.8 43.0 %all-to-all-start = ((bf16[8,128,1024]{2,1,0:T(8,128)(2,1)}), bf16[8,128,1024]{2,1,0:T(8,128)(2,1)S(1)}, u32[]{:S(2)}, u32[]{:S(2)}) async-start(bf16[8,128,1024]{2,1,0:T(8,128)(2,1)} %reshape.131), calls=%async_computation | async-start | bytes 4194304 | tf_op jit(solution)/shard_map/all_to_all | solution.py:116
  52.8 1.3 %copy-start = (bf16[8,128,1024]{2,1,0:T(8,128)(2,1)}, bf16[8,128,1024]{2,1,0:T(8,128)(2,1)S(1)}, u32[]{:S(2)}) copy-start(bf16[8,128,1024]{2,1,0:T(8,128)(2,1)S(1)} %all-to-all-done.v_ref) | copy-start | bytes 6291460
  63.0 2.1 %copy-start.1 = (bf16[64,32,128]{2,1,0:T(8,128)(2,1)S(1)}, bf16[64,32,128]{2,1,0:T(8,128)(2,1)}, u32[]{:S(2)}) copy-start(bf16[64,32,128]{2,1,0:T(8,128)(2,1)} %get-tuple-element.7) | copy-start | bytes 1572868
Sparse Core Ops, SparseCore 0:
  9.5 40.3 all-gather.1

commit v9 on v6

--- a/solution.py
+++ b/solution.py
@@ -22,17 +22,15 @@
     return high, low
 
 
-def attend_kernel(rows, own_heads, q_ref, k_ref, v_ref, hit_ref, out_ref, stat_ref):
+def score_kernel(q_ref, k_ref, hit_ref, w_ref, stat_ref):
     pages, page_len, _ = k_ref.shape
     q = q_ref[0]
     keys = k_ref[...].reshape(pages * page_len, HD)
-    values = v_ref[...].reshape(pages * page_len, HD)
     scores = lax.dot_general(
         q, keys, (((1,), (1,)), ((), ())), preferred_element_type=jnp.float32
     ) * (1.0 / math.sqrt(HD))
     req_rows = hit_ref.shape[0]
     groups = q.shape[0] // req_rows
-    halves = req_rows // rows
     hit = jnp.concatenate([hit_ref[...]] * groups, axis=0) > 0.5
     scores = jnp.where(hit, scores, jnp.float32(-1e30))
     top = jnp.max(scores, axis=1, keepdims=True)
@@ -41,20 +39,27 @@
     shift = high + low
     terms = jnp.where(hit, jnp.exp(scores - shift), jnp.float32(0.0))
     total = jnp.sum(terms, axis=1, keepdims=True)
-    mixed = jnp.dot(
-        terms.astype(jnp.bfloat16), values, preferred_element_type=jnp.float32
-    ).astype(jnp.bfloat16)
+    w_ref[0] = terms.astype(jnp.bfloat16)
+    lane = lax.broadcasted_iota(jnp.int32, (q.shape[0], LANES), 1)
+    stat_tile = jnp.where(
+        lane == 0, high, jnp.where(lane == 1, low, jnp.where(lane == 2, total, 0.0))
+    )
+    stat_ref[0] = jnp.transpose(stat_tile)[: stat_ref.shape[1], :]
+
+
+def mix_kernel(rows, own_heads, req_rows, w_ref, v_ref, out_ref):
+    pages, page_len, _ = v_ref.shape
+    values = v_ref[...].reshape(pages * page_len, HD)
+    weights = w_ref[0]
+    groups = weights.shape[0] // req_rows
+    halves = req_rows // rows
+    mixed = jnp.dot(weights, values, preferred_element_type=jnp.float32).astype(jnp.bfloat16)
     for g in range(groups):
         for y in range(halves):
             first = g * req_rows + y * rows
             block = (g // own_heads) * halves + y
             row = (g % own_heads) * rows
             out_ref[block, row : row + rows, :] = mixed[first : first + rows, :]
-    lane = lax.broadcasted_iota(jnp.int32, (q.shape[0], LANES), 1)
-    stat_tile = jnp.where(
-        lane == 0, high, jnp.where(lane == 1, low, jnp.where(lane == 2, total, 0.0))
-    )
-    stat_ref[0] = jnp.transpose(stat_tile)[: stat_ref.shape[1], :]
 
 
 def attend(grouped_q, keys, values, token_hit, rows, own_heads):
@@ -65,29 +70,40 @@
     groups = q_rows // req_rows
     per_head_blocks = groups // own_heads * (req_rows // rows)
     block_rows = own_heads * rows
-    return pl.pallas_call(
-        functools.partial(attend_kernel, rows, own_heads),
+    kv_spec = pl.BlockSpec((pages, page_len, HD), lambda k: (0, 0, k))
+    w_spec = pl.BlockSpec((1, q_rows, tokens), lambda k: (k, 0, 0))
+    weights, stats = pl.pallas_call(
+        score_kernel,
         grid=(kv_heads,),
         in_specs=[
             pl.BlockSpec((1, q_rows, HD), lambda k: (k, 0, 0)),
-            pl.BlockSpec((pages, page_len, HD), lambda k: (0, 0, k)),
-            pl.BlockSpec((pages, page_len, HD), lambda k: (0, 0, k)),
+            kv_spec,
             pl.BlockSpec(token_hit.shape, lambda k: (0, 0)),
         ],
-        out_specs=[
-            pl.BlockSpec((per_head_blocks, block_rows, HD), lambda k: (k, 0, 0)),
-            pl.BlockSpec((1, STAT_ROWS, q_rows), lambda k: (k, 0, 0)),
-        ],
+        out_specs=[w_spec, pl.BlockSpec((1, STAT_ROWS, q_rows), lambda k: (k, 0, 0))],
         out_shape=[
-            jax.ShapeDtypeStruct((kv_heads * per_head_blocks, block_rows, HD), jnp.bfloat16),
+            jax.ShapeDtypeStruct((kv_heads, q_rows, tokens), jnp.bfloat16),
             jax.ShapeDtypeStruct((kv_heads, STAT_ROWS, q_rows), jnp.float32),
         ],
         cost_estimate=pl.CostEstimate(
-            flops=4 * kv_heads * q_rows * tokens * HD,
+            flops=2 * kv_heads * q_rows * tokens * HD,
             transcendentals=kv_heads * q_rows * tokens,
-            bytes_accessed=2 * (grouped_q.size + keys.size + values.size) + 6 * kv_heads * q_rows * HD,
+            bytes_accessed=2 * (grouped_q.size + keys.size + kv_heads * q_rows * tokens),
         ),
-    )(grouped_q, keys, values, token_hit)
+    )(grouped_q, keys, token_hit)
+    out_blocks = pl.pallas_call(
+        functools.partial(mix_kernel, rows, own_heads, req_rows),
+        grid=(kv_heads,),
+        in_specs=[w_spec, kv_spec],
+        out_specs=pl.BlockSpec((per_head_blocks, block_rows, HD), lambda k: (k, 0, 0)),
+        out_shape=jax.ShapeDtypeStruct((kv_heads * per_head_blocks, block_rows, HD), jnp.bfloat16),
+        cost_estimate=pl.CostEstimate(
+            flops=2 * kv_heads * q_rows * tokens * HD,
+            transcendentals=0,
+            bytes_accessed=2 * (values.size + kv_heads * q_rows * tokens + kv_heads * q_rows * HD),
+        ),
+    )(weights, values)
+    return out_blocks, stats
 
 def body(queries, key_pool, value_pool, page_table, page_count):
     n_page = lax.axis_size("page")

time: 109 us -> 116 us (1.064)
  Pallas kernels: 9 us -> 15.4 us
  waiting for transfers between devices: 13.7 us -> 10.8 us
  blocking collectives: 52.1 us -> 53.9 us
    all_to_all x1, waiting for transfers between devices: 13 us -> 0.01 us  [body(): lax.all_to_all(jnp.broadcast_to(value_pool[None], (n_xc,) + value_pool.sh...]
    all_gather x1, waiting for transfers between devices: 0.01 us -> 10.1 us  [body(): keys = lax.all_gather(key_pool, 'xc', tiled=True)]
    pallas_call x1 -> x2, Pallas kernels: 9 us -> 15.4 us  [the longest x1 8.35 us: attend(): pl.pallas_call(score_kernel, grid=(kv_heads,), in_specs=[pl.BlockSpec((1,...]
    all_to_all x1, blocking collectives: 34.3 us -> 36.1 us  [body(): arrived = lax.all_to_all(payload, ('page', 'yh'), 0, 0, tiled=True)]
  transfers between devices with their start and end apart: 2 -> 2, of which waited for: 1 -> 1; matrix products, arithmetic and copies ran while one was open for 5% -> 6% of each run, Pallas kernels for 0% -> 7%
where the time goes in v9:
time: 116 us; the launch traced here: 114 us
  blocking collectives  53.9 us (46%)
  Pallas kernels  15.4 us (13%)
  between operations  13.5 us (12%)
  waiting for transfers between devices  10.8 us (9%)
  starting transfers between devices  9.49 us (8%)
  local copies, waits for them, and re-layouts  7.9 us (7%)
  other arithmetic  3.18 us (3%)
    all_to_all x1, blocking collectives, body(): arrived = lax.all_to_all(payload, ('page', 'yh'), 0, 0, tiled=True)  36.1 us
    all_gather x1, blocking collectives, body(): all_packed = lax.all_gather(packed, 'yh', tiled=True)  17.8 us
    all_gather x1, waiting for transfers between devices, body(): keys = lax.all_gather(key_pool, 'xc', tiled=True)  10.1 us
    all_to_all x1, starting transfers between devices, body(): lax.all_to_all(jnp.broadcast_to(value_pool[None], (n_xc,) + value_pool.sh...  9.49 us
    pallas_call x1, Pallas kernels, attend(): pl.pallas_call(score_kernel, grid=(kv_heads,), in_specs=[pl.BlockSpec((1,...  8.35 us
    pallas_call x1, Pallas kernels, attend(): pl.pallas_call(functools.partial(mix_kernel, rows, own_heads, req_rows),...  7.05 us
    reshape x1, local copies, waits for them, and re-layouts, body(): jnp.broadcast_to(value_pool[None], (n_xc,) + value_pool.shape)  2.53 us
  transfers between devices with their start and end apart: 2, of which 1 were waited for; matrix products, arithmetic and copies ran while one was open for 6% of the time, Pallas kernels for 7%

profile of v9, /device:TPU:6, one launch (start us, length us, event | category | flops | bytes accessed | tf_op | source)
XLA Modules:
  0.0 114.2 jit_solution(11240783434861488546)
XLA Ops:
  6.5 0.7 all-gather.2.cloned.1.call-update
  7.3 2.5 %reshape.129 = bf16[8,128,1024]{2,1,0:T(8,128)(2,1)} broadcast(bf16[128,1024]{1,0:T(8,128)(2,1)} %bitcast.34), dimensions={1,2} | broadcast | bytes 2359296 | tf_op jit(solution)/shard_map/reshape | solution.py:134
  9.8 9.5 %all-to-all-start = ((bf16[8,128,1024]{2,1,0:T(8,128)(2,1)}), bf16[8,128,1024]{2,1,0:T(8,128)(2,1)S(1)}, u32[]{:S(2)}, u32[]{:S(2)}) async-start(bf16[8,128,1024]{2,1,0:T(8,128)(2,1)} %reshape.129), calls=%async_computation | async-start | bytes 4194304 | tf_op jit(solution)/shard_map/all_to_all | solution.py:133
  19.3 0.1 iota_compare_fusion
  19.4 0.4 and_reduce_fusion
  19.8 17.8 %all_gather.6 = bf16[32,8320]{1,0:T(8,128)(2,1)S(1)} all-gather(bf16[16,8320]{1,0:T(8,128)(2,1)S(1)} %pad_maximum_fusion), channel_id=1, replica_groups=mesh['page'=32,'yh'=2,'xc'=8] {'yh'}, dimensions={0}, use_global_device_ids=true | all-gather | bytes 798720 | tf_op jit(solution)/shard_map/all_gather | solution.py:131
  37.7 0.1 copy.68
  37.8 1.2 %copy.55 = bf16[32,8,8,128]{3,0,2,1:T(8,128)(2,1)} copy(bf16[32,8,8,128]{3,2,1,0:T(8,128)(2,1)S(1)} %bitcast.28) | data formatting | bytes 1048576 | tf_op jit(solution)/shard_map/reshape | solution.py:149
  39.0 0.1 compare_convert_fusion
  39.1 0.1 broadcast_in_dim.4
  39.2 0.7 copy.72
  39.9 10.1 %all-gather.2.cloned.1.call-done.k_ref = bf16[8,128,1024]{2,1,0:T(8,128)(2,1)} async-done(((bf16[1,128,1024]{2,1,0:T(8,128)(2,1)}), bf16[8,128,1024]{2,1,0:T(8,128)(2,1)}) %all-gather.2.cloned.1.call-update) | async-done | bytes 2097168 | tf_op jit(solution)/shard_map/all_gather | solution.py:132
  49.9 8.4 %shard_map.55 = (bf16[8,256,1024]{2,1,0:T(8,128)(2,1)}, f32[8,8,256]{2,1,0:T(8,128)}) custom-call(bf16[8,256,128]{2,1,0:T(8,128)(2,1)} %bitcast.32, bf16[8,128,1024]{2,1,0:T(8,128)(2,1)} %all-gather.2.cloned.1.call-done.k_ref, f32[32,1024]{1,0:T(8,128)} %bitcast.35), custom_call_target="tpu_custom_call" | custom-call | flops 536870912 | bytes 6815744 | tf_op jit(solution)/shard_map/pallas_call | solution.py:75
  58.3 0.8 slice.39
  59.1 0.3 reshape.130
  59.5 0.1 squeeze.2
  59.6 0.1 copy.60
  59.7 0.1 copy.64
  59.8 0.1 copy.65
  59.9 0.1 bitcast_convert_fusion
  60.1 0.1 concatenate.32
  60.2 0.1 concatenate.33
  60.3 0.0 all-to-all-done.v_ref
  60.3 1.3 %copy-done = bf16[8,128,1024]{2,1,0:T(8,128)(2,1)} copy-done((bf16[8,128,1024]{2,1,0:T(8,128)(2,1)}, bf16[8,128,1024]{2,1,0:T(8,128)(2,1)S(1)}, u32[]{:S(2)}) %copy-start) | copy-done | bytes 2097176
  61.6 7.0 %shard_map.56 = bf16[64,32,128]{2,1,0:T(8,128)(2,1)} custom-call(bf16[8,256,1024]{2,1,0:T(8,128)(2,1)} %get-tuple-element.7.w_ref, bf16[8,128,1024]{2,1,0:T(8,128)(2,1)} %copy-done), custom_call_target="tpu_custom_call" | custom-call | flops 536870912 | bytes 6815744 | tf_op jit(solution)/shard_map/pallas_call | solution.py:94
  68.6 1.3 %maximum_maximum_fusion = bf16[64,33,128]{2,1,0:T(8,128)(2,1)S(1)} fusion(bf16[64,1,32]{2,1,0:T(2,128)(2,1)S(1)} %copy.65, bf16[64,1,32]{2,1,0:T(2,128)(2,1)S(1)} %copy.64, bf16[64,1,32]{2,1,0:T(2,128)(2,1)S(1)} %concatenate.33, bf16[64,1,32]{2,1,0:T(2,128)(2,1)S(1)} %concatenate.32, bf16[64,32,128]{2,1,0:T(8,128)(2,1)} %shard_map.56), kind=kLoop, calls=%fused_computation.1 | loop fusion | flops 2703360 | bytes 1081344 | tf_op jit(solution)/shard_map/concatenate | solution.py:165
  69.9 36.1 %all_to_all.10 = bf16[64,33,128]{2,1,0:T(8,128)(2,1)S(1)} all-to-all(bf16[64,33,128]{2,1,0:T(8,128)(2,1)S(1)} %maximum_maximum_fusion), channel_id=1, replica_groups=mesh['page'=32,'yh'=2,'xc'=8] {'page','yh'}, dimensions={0} | all-to-all | bytes 1081344 | tf_op jit(solution)/shard_map/all_to_all | solution.py:166
  106.0 0.1 fusion.4
  106.1 0.1 fusion.1
  106.2 0.1 div.11
  106.3 0.3 multiply_reduce_fusion
  106.6 0.7 copy_bitcast_fusion.1
  (20 shorter events, 0.2 us)
Async XLA Ops:
  6.5 43.4 %all-gather.2.cloned.1.call-start = ((), (), s32[]{:S(2)}) async-start(), calls=%async_computation.2 | async-start | bytes 2359296 | tf_op jit(solution)/shard_map/all_gather | solution.py:132
  9.8 9.5 %copy-start.3 = (s32[16]{0:T(128)S(1)}, s32[16]{0:T(128)}, u32[]{:S(2)}) copy-start(s32[16]{0:T(128)} %param.9) | copy-start | bytes 196
  9.8 9.6 %copy-start.2 = (s32[16,32]{1,0:T(8,128)S(1)}, s32[16,32]{1,0:T(8,128)}, u32[]{:S(2)}) copy-start(s32[16,32]{1,0:T(8,128)} %param.8) | copy-start | bytes 6148
  9.8 10.0 %copy-start.1 = (bf16[16,8192]{1,0:T(8,128)(2,1)S(1)}, bf16[16,8192]{1,0:T(8,128)(2,1)}, u32[]{:S(2)}) copy-start(bf16[16,8192]{1,0:T(8,128)(2,1)} %param.5) | copy-start | bytes 786436
  9.8 50.5 %all-to-all-start = ((bf16[8,128,1024]{2,1,0:T(8,128)(2,1)}), bf16[8,128,1024]{2,1,0:T(8,128)(2,1)S(1)}, u32[]{:S(2)}, u32[]{:S(2)}) async-start(bf16[8,128,1024]{2,1,0:T(8,128)(2,1)} %reshape.129), calls=%async_computation | async-start | bytes 4194304 | tf_op jit(solution)/shard_map/all_to_all | solution.py:133
  60.3 1.3 %copy-start = (bf16[8,128,1024]{2,1,0:T(8,128)(2,1)}, bf16[8,128,1024]{2,1,0:T(8,128)(2,1)S(1)}, u32[]{:S(2)}) copy-start(bf16[8,128,1024]{2,1,0:T(8,128)(2,1)S(1)} %all-to-all-done.v_ref) | copy-start | bytes 6291460
Sparse Core Ops, SparseCore 0:
  9.5 40.3 all-gather.1

commit v10 on v6

--- a/solution.py
+++ b/solution.py
@@ -14,6 +14,7 @@
 HD = 128
 LANES = 128
 STAT_ROWS = 8
+HEADS_PER_STEP = 2
 
 
 def split_pair(value):
@@ -23,10 +24,16 @@
 
 
 def attend_kernel(rows, own_heads, q_ref, k_ref, v_ref, hit_ref, out_ref, stat_ref):
+    for step in range(q_ref.shape[0]):
+        attend_head(rows, own_heads, step, q_ref, k_ref, v_ref, hit_ref, out_ref, stat_ref)
+
+
+def attend_head(rows, own_heads, step, q_ref, k_ref, v_ref, hit_ref, out_ref, stat_ref):
     pages, page_len, _ = k_ref.shape
-    q = q_ref[0]
-    keys = k_ref[...].reshape(pages * page_len, HD)
-    values = v_ref[...].reshape(pages * page_len, HD)
+    q = q_ref[step]
+    lanes = pl.ds(step * HD, HD)
+    keys = k_ref[:, :, lanes].reshape(pages * page_len, HD)
+    values = v_ref[:, :, lanes].reshape(pages * page_len, HD)
     scores = lax.dot_general(
         q, keys, (((1,), (1,)), ((), ())), preferred_element_type=jnp.float32
     ) * (1.0 / math.sqrt(HD))
@@ -44,17 +51,18 @@
     mixed = jnp.dot(
         terms.astype(jnp.bfloat16), values, preferred_element_type=jnp.float32
     ).astype(jnp.bfloat16)
+    base = step * (groups // own_heads) * halves
     for g in range(groups):
         for y in range(halves):
             first = g * req_rows + y * rows
-            block = (g // own_heads) * halves + y
+            block = base + (g // own_heads) * halves + y
             row = (g % own_heads) * rows
             out_ref[block, row : row + rows, :] = mixed[first : first + rows, :]
     lane = lax.broadcasted_iota(jnp.int32, (q.shape[0], LANES), 1)
     stat_tile = jnp.where(
         lane == 0, high, jnp.where(lane == 1, low, jnp.where(lane == 2, total, 0.0))
     )
-    stat_ref[0] = jnp.transpose(stat_tile)[: stat_ref.shape[1], :]
+    stat_ref[step] = jnp.transpose(stat_tile)[: stat_ref.shape[1], :]
 
 
 def attend(grouped_q, keys, values, token_hit, rows, own_heads):
@@ -67,16 +75,16 @@
     block_rows = own_heads * rows
     return pl.pallas_call(
         functools.partial(attend_kernel, rows, own_heads),
-        grid=(kv_heads,),
+        grid=(kv_heads // HEADS_PER_STEP,),
         in_specs=[
-            pl.BlockSpec((1, q_rows, HD), lambda k: (k, 0, 0)),
-            pl.BlockSpec((pages, page_len, HD), lambda k: (0, 0, k)),
-            pl.BlockSpec((pages, page_len, HD), lambda k: (0, 0, k)),
+            pl.BlockSpec((HEADS_PER_STEP, q_rows, HD), lambda k: (k, 0, 0)),
+            pl.BlockSpec((pages, page_len, HEADS_PER_STEP * HD), lambda k: (0, 0, k)),
+            pl.BlockSpec((pages, page_len, HEADS_PER_STEP * HD), lambda k: (0, 0, k)),
             pl.BlockSpec(token_hit.shape, lambda k: (0, 0)),
         ],
         out_specs=[
-            pl.BlockSpec((per_head_blocks, block_rows, HD), lambda k: (k, 0, 0)),
-            pl.BlockSpec((1, STAT_ROWS, q_rows), lambda k: (k, 0, 0)),
+            pl.BlockSpec((HEADS_PER_STEP * per_head_blocks, block_rows, HD), lambda k: (k, 0, 0)),
+            pl.BlockSpec((HEADS_PER_STEP, STAT_ROWS, q_rows), lambda k: (k, 0, 0)),
         ],
         out_shape=[
             jax.ShapeDtypeStruct((kv_heads * per_head_blocks, block_rows, HD), jnp.bfloat16),

time: 109 us -> 108 us (level)
  Pallas kernels: 9 us -> 7.35 us
    pallas_call x1, Pallas kernels: 9 us -> 7.35 us  [attend(): pl.pallas_call(functools.partial(attend_kernel, rows, own_heads), grid=(k...]
where the time goes in v10:
time: 108 us; the launch traced here: 106 us
  blocking collectives  52.1 us (48%)
  waiting for transfers between devices  13.7 us (13%)
  between operations  13.5 us (12%)
  starting transfers between devices  9.49 us (9%)
  local copies, waits for them, and re-layouts  7.88 us (7%)
  Pallas kernels  7.35 us (7%)
  other arithmetic  2.14 us (2%)
    all_to_all x1, blocking collectives, body(): arrived = lax.all_to_all(payload, ('page', 'yh'), 0, 0, tiled=True)  34.3 us
    all_gather x1, blocking collectives, body(): all_packed = lax.all_gather(packed, 'yh', tiled=True)  17.8 us
    all_to_all x1, waiting for transfers between devices, body(): lax.all_to_all(jnp.broadcast_to(value_pool[None], (n_xc,) + value_pool.sh...  13 us
    all_to_all x1, starting transfers between devices, body(): lax.all_to_all(jnp.broadcast_to(value_pool[None], (n_xc,) + value_pool.sh...  9.49 us
    pallas_call x1, Pallas kernels, attend(): pl.pallas_call(functools.partial(attend_kernel, rows, own_heads), grid=(k...  7.35 us
    reshape x1, local copies, waits for them, and re-layouts, body(): jnp.broadcast_to(value_pool[None], (n_xc,) + value_pool.shape)  2.52 us
  transfers between devices with their start and end apart: 2, of which 1 were waited for; matrix products, arithmetic and copies ran while one was open for 5% of the time, Pallas kernels for 0%

profile of v10, /device:TPU:6, one launch (start us, length us, event | category | flops | bytes accessed | tf_op | source)
XLA Modules:
  0.0 106.2 jit_solution(13763773297044228062)
XLA Ops:
  6.5 0.7 all-gather.2.cloned.1.call-update
  7.3 2.5 %reshape.129 = bf16[8,128,1024]{2,1,0:T(8,128)(2,1)} broadcast(bf16[128,1024]{1,0:T(8,128)(2,1)} %bitcast.35), dimensions={1,2} | broadcast | bytes 2359296 | tf_op jit(solution)/shard_map/reshape | solution.py:126
  9.8 9.5 %all-to-all-start = ((bf16[8,128,1024]{2,1,0:T(8,128)(2,1)}), bf16[8,128,1024]{2,1,0:T(8,128)(2,1)S(1)}, u32[]{:S(2)}, u32[]{:S(2)}) async-start(bf16[8,128,1024]{2,1,0:T(8,128)(2,1)} %reshape.129), calls=%async_computation | async-start | bytes 4194304 | tf_op jit(solution)/shard_map/all_to_all | solution.py:125
  19.3 0.0 copy-done.4
  19.3 0.1 iota_compare_fusion
  19.4 0.0 copy-done.3
  19.4 0.4 and_reduce_fusion
  19.8 17.8 %all_gather.6 = bf16[32,8320]{1,0:T(8,128)(2,1)S(1)} all-gather(bf16[16,8320]{1,0:T(8,128)(2,1)S(1)} %pad_maximum_fusion), channel_id=1, replica_groups=mesh['page'=32,'yh'=2,'xc'=8] {'yh'}, dimensions={0}, use_global_device_ids=true | all-gather | bytes 798720 | tf_op jit(solution)/shard_map/all_gather | solution.py:123
  37.6 0.1 compare_convert_fusion
  37.7 0.1 broadcast_in_dim.5
  37.8 0.7 copy.74
  38.5 0.1 copy.70
  38.6 1.1 %copy.57 = bf16[32,8,8,128]{3,0,2,1:T(8,128)(2,1)} copy(bf16[32,8,8,128]{3,2,1,0:T(8,128)(2,1)S(1)} %bitcast.29) | data formatting | bytes 1048576 | tf_op jit(solution)/shard_map/reshape | solution.py:141
  39.8 13.0 %all-to-all-done.v_ref = bf16[8,128,1024]{2,1,0:T(8,128)(2,1)S(1)} async-done(((bf16[8,128,1024]{2,1,0:T(8,128)(2,1)}), bf16[8,128,1024]{2,1,0:T(8,128)(2,1)S(1)}, u32[]{:S(2)}, u32[]{:S(2)}) %all-to-all-start) | async-done | bytes 2097184 | tf_op jit(solution)/shard_map/all_to_all | solution.py:125
  52.8 1.3 %copy-done = bf16[8,128,1024]{2,1,0:T(8,128)(2,1)} copy-done((bf16[8,128,1024]{2,1,0:T(8,128)(2,1)}, bf16[8,128,1024]{2,1,0:T(8,128)(2,1)S(1)}, u32[]{:S(2)}) %copy-start) | copy-done | bytes 2097176
  54.1 7.3 %shard_map.55 = (bf16[64,32,128]{2,1,0:T(8,128)(2,1)}, f32[8,8,256]{2,1,0:T(8,128)}) custom-call(bf16[8,256,128]{2,1,0:T(8,128)(2,1)} %bitcast.28, bf16[8,128,1024]{2,1,0:T(8,128)(2,1)} %all-gather.2.cloned.1.call-done.k_ref, bf16[8,128,1024]{2,1,0:T(8,128)(2,1)} %copy-done, f32[32,1024]{1,0:T(8,128)} %bitcast.33), custom_call_target="tpu_custom_call" | custom-call | flops 1073741824 | bytes 6291456 | tf_op jit(solution)/shard_map/pallas_call | solution.py:76
  61.4 0.9 slice.39
  62.4 0.3 reshape.130
  62.7 0.1 bitcast_convert_fusion
  62.8 0.1 concatenate.32
  63.0 0.1 concatenate.33
  63.1 0.1 squeeze.2
  63.2 0.1 copy.62
  63.3 0.1 copy.66
  63.4 0.1 copy.67
  63.5 0.2 maximum_maximum_fusion
  63.7 34.3 %all_to_all.10 = bf16[64,33,128]{2,1,0:T(8,128)(2,1)S(1)} all-to-all(bf16[64,33,128]{2,1,0:T(8,128)(2,1)S(1)} %maximum_maximum_fusion), channel_id=1, replica_groups=mesh['page'=32,'yh'=2,'xc'=8] {'page','yh'}, dimensions={0} | all-to-all | bytes 1081344 | tf_op jit(solution)/shard_map/all_to_all | solution.py:158
  98.0 0.1 fusion.4
  98.1 0.1 fusion.1
  98.2 0.1 div.11
  98.3 0.3 multiply_reduce_fusion
  98.7 0.7 copy_bitcast_fusion.1
  (21 shorter events, 0.2 us)
Async XLA Ops:
  6.5 46.3 %all-gather.2.cloned.1.call-start = ((), (), s32[]{:S(2)}) async-start(), calls=%async_computation.2 | async-start | bytes 2359296 | tf_op jit(solution)/shard_map/all_gather | solution.py:124
  9.8 9.5 %copy-start.4 = (s32[16]{0:T(128)S(1)}, s32[16]{0:T(128)}, u32[]{:S(2)}) copy-start(s32[16]{0:T(128)} %param.9) | copy-start | bytes 196
  9.8 9.6 %copy-start.3 = (s32[16,32]{1,0:T(8,128)S(1)}, s32[16,32]{1,0:T(8,128)}, u32[]{:S(2)}) copy-start(s32[16,32]{1,0:T(8,128)} %param.8) | copy-start | bytes 6148
  9.8 10.0 %copy-start.2 = (bf16[16,8192]{1,0:T(8,128)(2,1)S(1)}, bf16[16,8192]{1,0:T(8,128)(2,1)}, u32[]{:S(2)}) copy-start(bf16[16,8192]{1,0:T(8,128)(2,1)} %param.5) | copy-start | bytes 786436
  9.8 43.0 %all-to-all-start = ((bf16[8,128,1024]{2,1,0:T(8,128)(2,1)}), bf16[8,128,1024]{2,1,0:T(8,128)(2,1)S(1)}, u32[]{:S(2)}, u32[]{:S(2)}) async-start(bf16[8,128,1024]{2,1,0:T(8,128)(2,1)} %reshape.129), calls=%async_computation | async-start | bytes 4194304 | tf_op jit(solution)/shard_map/all_to_all | solution.py:125
  52.8 1.3 %copy-start = (bf16[8,128,1024]{2,1,0:T(8,128)(2,1)}, bf16[8,128,1024]{2,1,0:T(8,128)(2,1)S(1)}, u32[]{:S(2)}) copy-start(bf16[8,128,1024]{2,1,0:T(8,128)(2,1)S(1)} %all-to-all-done.v_ref) | copy-start | bytes 6291460
  61.4 2.1 %copy-start.1 = (bf16[64,32,128]{2,1,0:T(8,128)(2,1)S(1)}, bf16[64,32,128]{2,1,0:T(8,128)(2,1)}, u32[]{:S(2)}) copy-start(bf16[64,32,128]{2,1,0:T(8,128)(2,1)} %get-tuple-element.7) | copy-start | bytes 1572868
Sparse Core Ops, SparseCore 0:
  9.5 40.3 all-gather.1

commit v11 on v10

--- a/solution.py
+++ b/solution.py
@@ -14,7 +14,7 @@
 HD = 128
 LANES = 128
 STAT_ROWS = 8
-HEADS_PER_STEP = 2
+HEADS_PER_STEP = 4
 
 
 def split_pair(value):

time: 108 us -> 108 us (level)
  no operation moved by 1% of the time
where the time goes in v11:
time: 108 us; the launch traced here: 106 us
  blocking collectives  52.1 us (48%)
  waiting for transfers between devices  13.7 us (13%)
  between operations  13.5 us (12%)
  starting transfers between devices  9.49 us (9%)
  local copies, waits for them, and re-layouts  7.88 us (7%)
  Pallas kernels  7.41 us (7%)
  other arithmetic  2.14 us (2%)
    all_to_all x1, blocking collectives, body(): arrived = lax.all_to_all(payload, ('page', 'yh'), 0, 0, tiled=True)  34.3 us
    all_gather x1, blocking collectives, body(): all_packed = lax.all_gather(packed, 'yh', tiled=True)  17.8 us
    all_to_all x1, waiting for transfers between devices, body(): lax.all_to_all(jnp.broadcast_to(value_pool[None], (n_xc,) + value_pool.sh...  13 us
    all_to_all x1, starting transfers between devices, body(): lax.all_to_all(jnp.broadcast_to(value_pool[None], (n_xc,) + value_pool.sh...  9.49 us
    pallas_call x1, Pallas kernels, attend(): pl.pallas_call(functools.partial(attend_kernel, rows, own_heads), grid=(k...  7.41 us
    reshape x1, local copies, waits for them, and re-layouts, body(): jnp.broadcast_to(value_pool[None], (n_xc,) + value_pool.shape)  2.52 us
  transfers between devices with their start and end apart: 2, of which 1 were waited for; matrix products, arithmetic and copies ran while one was open for 5% of the time, Pallas kernels for 0%

profile of v11, /device:TPU:6, one launch (start us, length us, event | category | flops | bytes accessed | tf_op | source)
XLA Modules:
  0.0 106.3 jit_solution(16113134695891958713)
XLA Ops:
  6.5 0.0 all-gather.2.cloned.1.call-start
  6.5 0.7 all-gather.2.cloned.1.call-update
  7.3 2.5 %reshape.129 = bf16[8,128,1024]{2,1,0:T(8,128)(2,1)} broadcast(bf16[128,1024]{1,0:T(8,128)(2,1)} %bitcast.35), dimensions={1,2} | broadcast | bytes 2359296 | tf_op jit(solution)/shard_map/reshape | solution.py:126
  9.8 9.5 %all-to-all-start = ((bf16[8,128,1024]{2,1,0:T(8,128)(2,1)}), bf16[8,128,1024]{2,1,0:T(8,128)(2,1)S(1)}, u32[]{:S(2)}, u32[]{:S(2)}) async-start(bf16[8,128,1024]{2,1,0:T(8,128)(2,1)} %reshape.129), calls=%async_computation | async-start | bytes 4194304 | tf_op jit(solution)/shard_map/all_to_all | solution.py:125
  19.3 0.1 iota_compare_fusion
  19.4 0.4 and_reduce_fusion
  19.8 17.8 %all_gather.6 = bf16[32,8320]{1,0:T(8,128)(2,1)S(1)} all-gather(bf16[16,8320]{1,0:T(8,128)(2,1)S(1)} %pad_maximum_fusion), channel_id=1, replica_groups=mesh['page'=32,'yh'=2,'xc'=8] {'yh'}, dimensions={0}, use_global_device_ids=true | all-gather | bytes 798720 | tf_op jit(solution)/shard_map/all_gather | solution.py:123
  37.6 0.1 compare_convert_fusion
  37.7 0.1 broadcast_in_dim.5
  37.8 0.7 copy.74
  38.5 0.1 copy.70
  38.6 1.1 %copy.57 = bf16[32,8,8,128]{3,0,2,1:T(8,128)(2,1)} copy(bf16[32,8,8,128]{3,2,1,0:T(8,128)(2,1)S(1)} %bitcast.29) | data formatting | bytes 1048576 | tf_op jit(solution)/shard_map/reshape | solution.py:141
  39.8 13.0 %all-to-all-done.v_ref = bf16[8,128,1024]{2,1,0:T(8,128)(2,1)S(1)} async-done(((bf16[8,128,1024]{2,1,0:T(8,128)(2,1)}), bf16[8,128,1024]{2,1,0:T(8,128)(2,1)S(1)}, u32[]{:S(2)}, u32[]{:S(2)}) %all-to-all-start) | async-done | bytes 2097184 | tf_op jit(solution)/shard_map/all_to_all | solution.py:125
  52.8 1.3 %copy-done = bf16[8,128,1024]{2,1,0:T(8,128)(2,1)} copy-done((bf16[8,128,1024]{2,1,0:T(8,128)(2,1)}, bf16[8,128,1024]{2,1,0:T(8,128)(2,1)S(1)}, u32[]{:S(2)}) %copy-start) | copy-done | bytes 2097176
  54.1 7.4 %shard_map.55 = (bf16[64,32,128]{2,1,0:T(8,128)(2,1)}, f32[8,8,256]{2,1,0:T(8,128)}) custom-call(bf16[8,256,128]{2,1,0:T(8,128)(2,1)} %bitcast.28, bf16[8,128,1024]{2,1,0:T(8,128)(2,1)} %all-gather.2.cloned.1.call-done.k_ref, bf16[8,128,1024]{2,1,0:T(8,128)(2,1)} %copy-done, f32[32,1024]{1,0:T(8,128)} %bitcast.33), custom_call_target="tpu_custom_call" | custom-call | flops 1073741824 | bytes 6291456 | tf_op jit(solution)/shard_map/pallas_call | solution.py:76
  61.5 0.9 slice.39
  62.4 0.3 reshape.130
  62.7 0.1 bitcast_convert_fusion
  62.9 0.1 concatenate.32
  63.0 0.1 concatenate.33
  63.2 0.1 squeeze.2
  63.3 0.1 copy.62
  63.4 0.1 copy.66
  63.5 0.1 copy.67
  63.6 0.0 copy-done.1
  63.6 0.2 maximum_maximum_fusion
  63.8 34.3 %all_to_all.10 = bf16[64,33,128]{2,1,0:T(8,128)(2,1)S(1)} all-to-all(bf16[64,33,128]{2,1,0:T(8,128)(2,1)S(1)} %maximum_maximum_fusion), channel_id=1, replica_groups=mesh['page'=32,'yh'=2,'xc'=8] {'page','yh'}, dimensions={0} | all-to-all | bytes 1081344 | tf_op jit(solution)/shard_map/all_to_all | solution.py:158
  98.1 0.1 fusion.4
  98.2 0.1 fusion.1
  98.3 0.1 div.11
  98.4 0.3 multiply_reduce_fusion
  98.7 0.7 copy_bitcast_fusion.1
  (21 shorter events, 0.2 us)
Async XLA Ops:
  6.5 46.3 %all-gather.2.cloned.1.call-start = ((), (), s32[]{:S(2)}) async-start(), calls=%async_computation.2 | async-start | bytes 2359296 | tf_op jit(solution)/shard_map/all_gather | solution.py:124
  9.8 9.5 %copy-start.4 = (s32[16]{0:T(128)S(1)}, s32[16]{0:T(128)}, u32[]{:S(2)}) copy-start(s32[16]{0:T(128)} %param.9) | copy-start | bytes 196
  9.8 9.6 %copy-start.3 = (s32[16,32]{1,0:T(8,128)S(1)}, s32[16,32]{1,0:T(8,128)}, u32[]{:S(2)}) copy-start(s32[16,32]{1,0:T(8,128)} %param.8) | copy-start | bytes 6148
  9.8 10.0 %copy-start.2 = (bf16[16,8192]{1,0:T(8,128)(2,1)S(1)}, bf16[16,8192]{1,0:T(8,128)(2,1)}, u32[]{:S(2)}) copy-start(bf16[16,8192]{1,0:T(8,128)(2,1)} %param.5) | copy-start | bytes 786436
  9.8 43.0 %all-to-all-start = ((bf16[8,128,1024]{2,1,0:T(8,128)(2,1)}), bf16[8,128,1024]{2,1,0:T(8,128)(2,1)S(1)}, u32[]{:S(2)}, u32[]{:S(2)}) async-start(bf16[8,128,1024]{2,1,0:T(8,128)(2,1)} %reshape.129), calls=%async_computation | async-start | bytes 4194304 | tf_op jit(solution)/shard_map/all_to_all | solution.py:125
  52.8 1.3 %copy-start = (bf16[8,128,1024]{2,1,0:T(8,128)(2,1)}, bf16[8,128,1024]{2,1,0:T(8,128)(2,1)S(1)}, u32[]{:S(2)}) copy-start(bf16[8,128,1024]{2,1,0:T(8,128)(2,1)S(1)} %all-to-all-done.v_ref) | copy-start | bytes 6291460
  61.5 2.1 %copy-start.1 = (bf16[64,32,128]{2,1,0:T(8,128)(2,1)S(1)}, bf16[64,32,128]{2,1,0:T(8,128)(2,1)}, u32[]{:S(2)}) copy-start(bf16[64,32,128]{2,1,0:T(8,128)(2,1)} %get-tuple-element.7) | copy-start | bytes 1572868
Sparse Core Ops, SparseCore 0:
  9.5 40.3 all-gather.1

commit v12 on v10

--- a/solution.py
+++ b/solution.py
@@ -97,10 +97,18 @@
         ),
     )(grouped_q, keys, values, token_hit)
 
+def spread(block, axis):
+    count = lax.axis_size(axis)
+    copies = jnp.broadcast_to(block[None], (count,) + block.shape)
+    return lax.all_to_all(copies.reshape((count * block.shape[0],) + block.shape[1:]), axis, 0, 0, tiled=True)
+
+
 def body(queries, key_pool, value_pool, page_table, page_count):
     n_page = lax.axis_size("page")
     n_yh = lax.axis_size("yh")
-    n_xc = lax.axis_size("xc")
+    n_x = lax.axis_size("x")
+    n_core = lax.axis_size("core")
+    n_xc = n_x * n_core
     page_index = lax.axis_index("page")
     yh_index = lax.axis_index("yh")
     pages_held = key_pool.shape[0]
@@ -121,21 +129,15 @@
     packed = jnp.concatenate([queries, row_hit], axis=1)
 
     all_packed = lax.all_gather(packed, "yh", tiled=True)
-    keys = lax.all_gather(key_pool, "xc", tiled=True)
-    values = lax.all_to_all(
-        jnp.broadcast_to(value_pool[None], (n_xc,) + value_pool.shape).reshape(
-            (n_xc * pages_held,) + value_pool.shape[1:]
-        ),
-        "xc",
-        0,
-        0,
-        tiled=True,
-    )
+    keys = lax.all_gather(lax.all_gather(key_pool, "x", tiled=True), "core", tiled=True)
+    values = spread(spread(value_pool, "x"), "core")
 
     req_rows = all_packed.shape[0]
     all_q = all_packed[:, : H * HD]
     held = n_xc * pages_held
     page_hit = lax.dynamic_slice_in_dim(all_packed, H * HD + yh_index * held, held, 1) > 0.5
+    order = [(x * n_core + c) * pages_held + j for c in range(n_core) for x in range(n_x) for j in range(pages_held)]
+    page_hit = jnp.take(page_hit, jnp.asarray(order, dtype=jnp.int32), axis=1)
     token_hit = jnp.repeat(page_hit, page_len, axis=1).astype(jnp.float32)
 
     grouped = all_q.reshape(req_rows, KVH, per_kv, HD).transpose(1, 2, 0, 3)
@@ -171,9 +173,13 @@
 
 def solution(mesh):
     n_page, n_req = mesh.devices.shape
-    n_yh = 2 if n_req % 2 == 0 else 1
-    split = Mesh(mesh.devices.reshape(n_page, n_yh, n_req // n_yh), ("page", "yh", "xc"))
-    req = ("yh", "xc")
+    n_yh = 2 if n_req % 4 == 0 else 1
+    n_core = 2 if n_req % 2 == 0 else 1
+    split = Mesh(
+        mesh.devices.reshape(n_page, n_yh, n_req // (n_yh * n_core), n_core),
+        ("page", "yh", "x", "core"),
+    )
+    req = ("yh", "x", "core")
     return jax.shard_map(
         body,
         mesh=split,

time: 108 us -> 123 us (1.14)
  waiting for transfers between devices: 13.7 us -> 23.8 us
  blocking collectives: 52.1 us -> 58.9 us
    all_gather x1 -> x2, waiting for transfers between devices: 0.01 us -> 23 us  [the longest x1 23 us: body(): lax.all_gather(key_pool, 'x', tiled=True)]
    all_to_all x1, waiting for transfers between devices: 13 us -> 0.01 us  [spread(): lax.all_to_all(copies.reshape((count * block.shape[0],) + block.shape[1:]...]
    all_to_all x0 -> x1, blocking collectives: none -> 7.45 us  [spread(): lax.all_to_all(copies.reshape((count * block.shape[0],) + block.shape[1:]...]
    all_gather x1, blocking collectives: 17.8 us -> 13.1 us  [body(): all_packed = lax.all_gather(packed, 'yh', tiled=True)]
    all_to_all x1, blocking collectives: 34.3 us -> 38.4 us  [body(): arrived = lax.all_to_all(payload, ('page', 'yh'), 0, 0, tiled=True)]
  transfers between devices with their start and end apart: 2 -> 3, of which waited for: 1 -> 1; matrix products, arithmetic and copies ran while one was open for 5% -> 5% of each run, Pallas kernels for 0% -> 0%
where the time goes in v12:
time: 123 us; the launch traced here: 122 us
  blocking collectives  58.9 us (48%)
  waiting for transfers between devices  23.8 us (19%)
  between operations  13.6 us (11%)
  starting transfers between devices  9.45 us (8%)
  Pallas kernels  7.35 us (6%)
  local copies, waits for them, and re-layouts  7.2 us (6%)
  other arithmetic  2.08 us (2%)
    all_to_all x1, blocking collectives, body(): arrived = lax.all_to_all(payload, ('page', 'yh'), 0, 0, tiled=True)  38.4 us
    all_gather x1, waiting for transfers between devices, body(): lax.all_gather(key_pool, 'x', tiled=True)  23 us
    all_gather x1, blocking collectives, body(): all_packed = lax.all_gather(packed, 'yh', tiled=True)  13.1 us
    all_to_all x1, starting transfers between devices, spread(): lax.all_to_all(copies.reshape((count * block.shape[0],) + block.shape[1:]...  9.44 us
    all_to_all x1, blocking collectives, spread(): lax.all_to_all(copies.reshape((count * block.shape[0],) + block.shape[1:]...  7.45 us
    pallas_call x1, Pallas kernels, attend(): pl.pallas_call(functools.partial(attend_kernel, rows, own_heads), grid=(k...  7.35 us
  transfers between devices with their start and end apart: 3, of which 1 were waited for; matrix products, arithmetic and copies ran while one was open for 5% of the time, Pallas kernels for 0%

profile of v12, /device:TPU:6, one launch (start us, length us, event | category | flops | bytes accessed | tf_op | source)
XLA Modules:
  0.0 122.3 jit_solution(18060236216148997614)
XLA Ops:
  6.5 0.7 all-gather.3.cloned.1.call-update
  7.3 2.1 %reshape.138 = bf16[4,128,1024]{2,1,0:T(8,128)(2,1)} broadcast(bf16[128,1024]{1,0:T(8,128)(2,1)} %bitcast.39), dimensions={1,2} | broadcast | bytes 1310720 | tf_op jit(solution)/shard_map/reshape | solution.py:103
  9.3 9.4 %all-to-all-start = ((bf16[4,128,1024]{2,1,0:T(8,128)(2,1)}), bf16[4,128,1024]{2,1,0:T(8,128)(2,1)S(1)}, u32[]{:S(2)}, u32[]{:S(2)}) async-start(bf16[4,128,1024]{2,1,0:T(8,128)(2,1)} %reshape.138), calls=%async_computation | async-start | bytes 2097152 | tf_op jit(solution)/shard_map/all_to_all | solution.py:103
  18.8 0.1 iota_compare_fusion
  18.9 0.4 and_reduce_fusion
  19.3 23.0 %all-gather.3.cloned.1.call-done = bf16[4,128,1024]{2,1,0:T(8,128)(2,1)} async-done(((bf16[1,128,1024]{2,1,0:T(8,128)(2,1)}), bf16[4,128,1024]{2,1,0:T(8,128)(2,1)}) %all-gather.3.cloned.1.call-update) | async-done | bytes 1048592 | tf_op jit(solution)/shard_map/all_gather | solution.py:132
  42.4 13.1 %all_gather.9 = bf16[32,8320]{1,0:T(8,128)(2,1)S(1)} all-gather(bf16[16,8320]{1,0:T(8,128)(2,1)S(1)} %pad_maximum_fusion), channel_id=1, replica_groups=mesh['page'=32,'yh'=2,'x'=4,'core'=2] {'yh'}, dimensions={0}, use_global_device_ids=true | all-gather | bytes 798720 | tf_op jit(solution)/shard_map/all_gather | solution.py:131
  55.5 0.1 constant_dynamic-slice_fusion
  55.6 0.1 copy.82
  55.7 0.6 gather_fusion
  56.3 0.1 copy.70
  56.3 0.1 broadcast_in_dim.40
  56.4 0.7 copy.88
  57.2 0.1 copy.84
  57.3 1.2 copy.68
  58.4 0.2 broadcast_in_dim.19
  58.7 7.4 %all_to_all.15.v_ref = bf16[8,128,1024]{2,1,0:T(8,128)(2,1)} all-to-all(bf16[8,128,1024]{2,1,0:T(8,128)(2,1)S(1)} %bitcast.31), channel_id=1, replica_groups=mesh['page'=32,'yh'=2,'x'=4,'core'=2] {'core'}, dimensions={0} | all-to-all | bytes 4194304 | tf_op jit(solution)/shard_map/all_to_all | solution.py:103
  66.1 7.4 %shard_map.64 = (bf16[64,32,128]{2,1,0:T(8,128)(2,1)}, f32[8,8,256]{2,1,0:T(8,128)}) custom-call(bf16[8,256,128]{2,1,0:T(8,128)(2,1)} %bitcast.32, bf16[8,128,1024]{2,1,0:T(8,128)(2,1)} %all-gather.5.cloned.1.call-done.k_ref, bf16[8,128,1024]{2,1,0:T(8,128)(2,1)} %all_to_all.15.v_ref, f32[32,1024]{1,0:T(8,128)} %bitcast.37), custom_call_target="tpu_custom_call" | custom-call | flops 1073741824 | bytes 6291456 | tf_op jit(solution)/shard_map/pallas_call | solution.py:76
  73.5 0.9 slice.39
  74.4 0.3 reshape.140
  74.9 0.1 concatenate.32
  75.0 0.1 concatenate.33
  75.2 0.1 squeeze.2
  75.3 0.1 copy.79
  75.4 0.1 copy.80
  75.6 0.2 maximum_maximum_fusion
  75.8 38.4 %all_to_all.16 = bf16[64,33,128]{2,1,0:T(8,128)(2,1)S(1)} all-to-all(bf16[64,33,128]{2,1,0:T(8,128)(2,1)S(1)} %maximum_maximum_fusion), channel_id=1, replica_groups=mesh['page'=32,'yh'=2,'x'=4,'core'=2] {'page','yh'}, dimensions={0} | all-to-all | bytes 1081344 | tf_op jit(solution)/shard_map/all_to_all | solution.py:160
  114.2 0.1 fusion.4
  114.3 0.1 fusion.1
  114.4 0.1 div.11
  114.5 0.3 multiply_reduce_fusion
  114.8 0.7 copy_bitcast_fusion.1
  (32 shorter events, 0.4 us)
Async XLA Ops:
  6.5 35.8 %all-gather.3.cloned.1.call-start = ((), (), s32[]{:S(2)}) async-start(), calls=%async_computation.3 | async-start | bytes 1310720 | tf_op jit(solution)/shard_map/all_gather | solution.py:132
  9.3 9.5 %copy-start.3 = (s32[16]{0:T(128)S(1)}, s32[16]{0:T(128)}, u32[]{:S(2)}) copy-start(s32[16]{0:T(128)} %param.10) | copy-start | bytes 196
  9.3 9.5 %copy-start.2 = (s32[16,32]{1,0:T(8,128)S(1)}, s32[16,32]{1,0:T(8,128)}, u32[]{:S(2)}) copy-start(s32[16,32]{1,0:T(8,128)} %param.9) | copy-start | bytes 6148
  9.3 33.0 %copy-start.1 = (bf16[16,8192]{1,0:T(8,128)(2,1)S(1)}, bf16[16,8192]{1,0:T(8,128)(2,1)}, u32[]{:S(2)}) copy-start(bf16[16,8192]{1,0:T(8,128)(2,1)} %param.6) | copy-start | bytes 786436
  9.3 49.1 %all-to-all-start = ((bf16[4,128,1024]{2,1,0:T(8,128)(2,1)}), bf16[4,128,1024]{2,1,0:T(8,128)(2,1)S(1)}, u32[]{:S(2)}, u32[]{:S(2)}) async-start(bf16[4,128,1024]{2,1,0:T(8,128)(2,1)} %reshape.138), calls=%async_computation | async-start | bytes 2097152 | tf_op jit(solution)/shard_map/all_to_all | solution.py:103
  18.8 36.9 %copy-start.4 = (s32[8]{0:T(128)S(1)}, s32[8]{0:T(128)}, u32[]{:S(2)}) copy-start(s32[8]{0:T(128)} %constant.62) | copy-start | bytes 100
  18.8 47.4 %all-gather.5.cloned.1.call-start = ((), (), s32[]{:S(2)}) async-start(), calls=%async_computation.4 | async-start | bytes 3145728 | tf_op jit(solution)/shard_map/all_gather | solution.py:132
  73.5 2.1 %copy-start = (bf16[64,32,128]{2,1,0:T(8,128)(2,1)S(1)}, bf16[64,32,128]{2,1,0:T(8,128)(2,1)}, u32[]{:S(2)}) copy-start(bf16[64,32,128]{2,1,0:T(8,128)(2,1)} %get-tuple-element.7) | copy-start | bytes 1572868
Sparse Core Ops, SparseCore 0:
  9.4 32.8 all-gather.2
  44.4 21.5 all-gather.4

commit v13 on v10

--- a/solution.py
+++ b/solution.py
@@ -58,6 +58,9 @@
             block = base + (g // own_heads) * halves + y
             row = (g % own_heads) * rows
             out_ref[block, row : row + rows, :] = mixed[first : first + rows, :]
+    stat_rows = out_ref.shape[1] - own_heads * rows
+    for block in range(base, base + (groups // own_heads) * halves):
+        out_ref[block, own_heads * rows :, :] = jnp.zeros((stat_rows, HD), out_ref.dtype)
     lane = lax.broadcasted_iota(jnp.int32, (q.shape[0], LANES), 1)
     stat_tile = jnp.where(
         lane == 0, high, jnp.where(lane == 1, low, jnp.where(lane == 2, total, 0.0))
@@ -73,6 +76,7 @@
     groups = q_rows // req_rows
     per_head_blocks = groups // own_heads * (req_rows // rows)
     block_rows = own_heads * rows
+    stat_rows = -(-4 * block_rows // HD)
     return pl.pallas_call(
         functools.partial(attend_kernel, rows, own_heads),
         grid=(kv_heads // HEADS_PER_STEP,),
@@ -83,11 +87,11 @@
             pl.BlockSpec(token_hit.shape, lambda k: (0, 0)),
         ],
         out_specs=[
-            pl.BlockSpec((HEADS_PER_STEP * per_head_blocks, block_rows, HD), lambda k: (k, 0, 0)),
+            pl.BlockSpec((HEADS_PER_STEP * per_head_blocks, block_rows + stat_rows, HD), lambda k: (k, 0, 0)),
             pl.BlockSpec((HEADS_PER_STEP, STAT_ROWS, q_rows), lambda k: (k, 0, 0)),
         ],
         out_shape=[
-            jax.ShapeDtypeStruct((kv_heads * per_head_blocks, block_rows, HD), jnp.bfloat16),
+            jax.ShapeDtypeStruct((kv_heads * per_head_blocks, block_rows + stat_rows, HD), jnp.bfloat16),
             jax.ShapeDtypeStruct((kv_heads, STAT_ROWS, q_rows), jnp.float32),
         ],
         cost_estimate=pl.CostEstimate(
@@ -154,7 +158,7 @@
         + [jnp.zeros((n_blocks, stat_cols - 4 * block_rows), jnp.float32)],
         axis=1,
     ).astype(jnp.bfloat16)
-    payload = jnp.concatenate([out_blocks, stats.reshape(n_blocks, -1, HD)], axis=1)
+    payload = lax.dynamic_update_slice_in_dim(out_blocks, stats.reshape(n_blocks, -1, HD), block_rows, 1)
     arrived = lax.all_to_all(payload, ("page", "yh"), 0, 0, tiled=True)
 
     part_out = arrived[:, :block_rows, :].astype(jnp.float32)

time: 108 us -> 108 us (level)
  no operation moved by 1% of the time
where the time goes in v13:
time: 108 us; the launch traced here: 107 us
  blocking collectives  52.3 us (48%)
  waiting for transfers between devices  13.7 us (13%)
  between operations  13.5 us (12%)
  starting transfers between devices  9.49 us (9%)
  local copies, waits for them, and re-layouts  7.82 us (7%)
  Pallas kernels  7.36 us (7%)
  other arithmetic  2.76 us (3%)
    all_to_all x1, blocking collectives, body(): arrived = lax.all_to_all(payload, ('page', 'yh'), 0, 0, tiled=True)  34.5 us
    all_gather x1, blocking collectives, body(): all_packed = lax.all_gather(packed, 'yh', tiled=True)  17.8 us
    all_to_all x1, waiting for transfers between devices, body(): lax.all_to_all(jnp.broadcast_to(value_pool[None], (n_xc,) + value_pool.sh...  13 us
    all_to_all x1, starting transfers between devices, body(): lax.all_to_all(jnp.broadcast_to(value_pool[None], (n_xc,) + value_pool.sh...  9.49 us
    pallas_call x1, Pallas kernels, attend(): pl.pallas_call(functools.partial(attend_kernel, rows, own_heads), grid=(k...  7.36 us
    reshape x1, local copies, waits for them, and re-layouts, body(): jnp.broadcast_to(value_pool[None], (n_xc,) + value_pool.shape)  2.52 us
  transfers between devices with their start and end apart: 2, of which 1 were waited for; matrix products, arithmetic and copies ran while one was open for 5% of the time, Pallas kernels for 0%

profile of v13, /device:TPU:6, one launch (start us, length us, event | category | flops | bytes accessed | tf_op | source)
XLA Modules:
  0.0 106.9 jit_solution(13332333337383189955)
XLA Ops:
  6.5 0.0 all-gather.2.cloned.1.call-start
  6.5 0.7 all-gather.2.cloned.1.call-update
  7.3 2.5 %reshape.129 = bf16[8,128,1024]{2,1,0:T(8,128)(2,1)} broadcast(bf16[128,1024]{1,0:T(8,128)(2,1)} %bitcast.35), dimensions={1,2} | broadcast | bytes 2359296 | tf_op jit(solution)/shard_map/reshape | solution.py:130
  9.8 9.5 %all-to-all-start = ((bf16[8,128,1024]{2,1,0:T(8,128)(2,1)}), bf16[8,128,1024]{2,1,0:T(8,128)(2,1)S(1)}, u32[]{:S(2)}, u32[]{:S(2)}) async-start(bf16[8,128,1024]{2,1,0:T(8,128)(2,1)} %reshape.129), calls=%async_computation | async-start | bytes 4194304 | tf_op jit(solution)/shard_map/all_to_all | solution.py:129
  19.3 0.1 iota_compare_fusion
  19.4 0.4 and_reduce_fusion
  19.8 0.0 copy-done.1
  19.8 17.8 %all_gather.6 = bf16[32,8320]{1,0:T(8,128)(2,1)S(1)} all-gather(bf16[16,8320]{1,0:T(8,128)(2,1)S(1)} %pad_maximum_fusion), channel_id=1, replica_groups=mesh['page'=32,'yh'=2,'xc'=8] {'yh'}, dimensions={0}, use_global_device_ids=true | all-gather | bytes 798720 | tf_op jit(solution)/shard_map/all_gather | solution.py:127
  37.6 0.1 compare_convert_fusion
  37.7 0.1 broadcast_in_dim.5
  37.8 0.7 copy.74
  38.5 0.1 copy.70
  38.6 1.1 %copy.57 = bf16[32,8,8,128]{3,0,2,1:T(8,128)(2,1)} copy(bf16[32,8,8,128]{3,2,1,0:T(8,128)(2,1)S(1)} %bitcast.29) | data formatting | bytes 1048576 | tf_op jit(solution)/shard_map/reshape | solution.py:145
  39.8 13.0 %all-to-all-done.v_ref = bf16[8,128,1024]{2,1,0:T(8,128)(2,1)S(1)} async-done(((bf16[8,128,1024]{2,1,0:T(8,128)(2,1)}), bf16[8,128,1024]{2,1,0:T(8,128)(2,1)S(1)}, u32[]{:S(2)}, u32[]{:S(2)}) %all-to-all-start) | async-done | bytes 2097184 | tf_op jit(solution)/shard_map/all_to_all | solution.py:129
  52.8 1.3 %copy-done = bf16[8,128,1024]{2,1,0:T(8,128)(2,1)} copy-done((bf16[8,128,1024]{2,1,0:T(8,128)(2,1)}, bf16[8,128,1024]{2,1,0:T(8,128)(2,1)S(1)}, u32[]{:S(2)}) %copy-start) | copy-done | bytes 2097176
  54.1 7.4 %shard_map.55 = (bf16[64,33,128]{2,1,0:T(8,128)(2,1)}, f32[8,8,256]{2,1,0:T(8,128)}) custom-call(bf16[8,256,128]{2,1,0:T(8,128)(2,1)} %bitcast.28, bf16[8,128,1024]{2,1,0:T(8,128)(2,1)} %all-gather.2.cloned.1.call-done.k_ref, bf16[8,128,1024]{2,1,0:T(8,128)(2,1)} %copy-done, f32[32,1024]{1,0:T(8,128)} %bitcast.33), custom_call_target="tpu_custom_call" | custom-call | flops 1073741824 | bytes 6291456 | tf_op jit(solution)/shard_map/pallas_call | solution.py:80
  61.4 0.8 slice.39
  62.3 0.3 reshape.130
  62.6 0.1 bitcast_convert_fusion
  62.8 0.1 concatenate.28
  62.9 0.1 concatenate.29
  63.0 0.1 squeeze.2
  63.1 0.1 copy.62
  63.2 0.1 copy.66
  63.3 0.1 copy.67
  63.4 0.8 maximum_dynamic-update-slice_fusion
  64.3 34.5 %all_to_all.10 = bf16[64,33,128]{2,1,0:T(8,128)(2,1)S(1)} all-to-all(bf16[64,33,128]{2,1,0:T(8,128)(2,1)} %maximum_dynamic-update-slice_fusion), channel_id=1, replica_groups=mesh['page'=32,'yh'=2,'xc'=8] {'page','yh'}, dimensions={0} | all-to-all | bytes 1081344 | tf_op jit(solution)/shard_map/all_to_all | solution.py:162
  98.8 0.1 fusion.4
  98.9 0.1 fusion.1
  99.0 0.1 div.11
  99.1 0.3 multiply_reduce_fusion
  99.4 0.7 copy_bitcast_fusion.1
  (19 shorter events, 0.2 us)
Async XLA Ops:
  6.5 46.2 %all-gather.2.cloned.1.call-start = ((), (), s32[]{:S(2)}) async-start(), calls=%async_computation.2 | async-start | bytes 2359296 | tf_op jit(solution)/shard_map/all_gather | solution.py:128
  9.8 9.5 %copy-start.3 = (s32[16]{0:T(128)S(1)}, s32[16]{0:T(128)}, u32[]{:S(2)}) copy-start(s32[16]{0:T(128)} %param.9) | copy-start | bytes 196
  9.8 9.6 %copy-start.2 = (s32[16,32]{1,0:T(8,128)S(1)}, s32[16,32]{1,0:T(8,128)}, u32[]{:S(2)}) copy-start(s32[16,32]{1,0:T(8,128)} %param.8) | copy-start | bytes 6148
  9.8 10.0 %copy-start.1 = (bf16[16,8192]{1,0:T(8,128)(2,1)S(1)}, bf16[16,8192]{1,0:T(8,128)(2,1)}, u32[]{:S(2)}) copy-start(bf16[16,8192]{1,0:T(8,128)(2,1)} %param.5) | copy-start | bytes 786436
  9.8 43.0 %all-to-all-start = ((bf16[8,128,1024]{2,1,0:T(8,128)(2,1)}), bf16[8,128,1024]{2,1,0:T(8,128)(2,1)S(1)}, u32[]{:S(2)}, u32[]{:S(2)}) async-start(bf16[8,128,1024]{2,1,0:T(8,128)(2,1)} %reshape.129), calls=%async_computation | async-start | bytes 4194304 | tf_op jit(solution)/shard_map/all_to_all | solution.py:129
  52.8 1.3 %copy-start = (bf16[8,128,1024]{2,1,0:T(8,128)(2,1)}, bf16[8,128,1024]{2,1,0:T(8,128)(2,1)S(1)}, u32[]{:S(2)}) copy-start(bf16[8,128,1024]{2,1,0:T(8,128)(2,1)S(1)} %all-to-all-done.v_ref) | copy-start | bytes 6291460
Sparse Core Ops, SparseCore 0:
  9.5 40.3 all-gather.1
